TPU v7x, 128 devices: a whole 4x4x4 slice. The times are simulated.
128 devices in a mesh: src: 4 (over z), vol: 32 (over y, x, core).
Axes of the slice: x: 4, y: 4, z: 4, core: 2. Of those that a mesh axis runs over, the one named last changes fastest.
Arguments:
- forward: bfloat16 [16384, 36, 512], P(('src', 'vol')), may hold values from -6 to 6
- item_tx: int32 [16384], P(('src', 'vol')), may hold values from 0 to 15, as said below
- item_brick: int32 [16384], P(('src', 'vol')), may hold values from 0 to 1023
- tx_place: int32 [16], replicated, may hold values from 0 to 15, as said below
- brick_place: int32 [1024], replicated, may hold values from 0 to 1023, as said below
- adjoint: bfloat16 [16, 1024, 36, 512], P('src', 'vol'), may hold values from -6 to 6
Outputs:
- gradient: float32 [2, 256, 16, 128], P(None, 'vol')
Inputs may be any that keep to these rules, and one draw needn't show every extreme that they name: Stored brick i goes to owner (tx_place[item_tx[i]] // 4, brick_place[item_brick[i]] // 32) as (src index, vol index). Among the stored bricks of one device at most 2 share an owner; in every draw one owner receives exactly 2 from every device. `tx_place`: A permutation. `brick_place`: A permutation.
All inputs are finite; a program needn't handle non-finite values.
Results may differ from a plain program's by a relative error of at most 0.0003.
Values may be sent and summed in bfloat16 or wider, within the bound.
No kernel may reach another device: no remote copies, remote signals or barrier semaphores. Data moves between devices by JAX's collectives and lax.ppermute only.
A program may use at most 128 MiB of HBM per device.

v0:
```python
import math

import jax
import jax.numpy as jnp
from jax import lax
from jax.sharding import PartitionSpec as P

E = 8
NFREQ = 6
NBY = 2
NBZ = 16


def with_halo(cells, sides, width):
    for axis, dim in sides:
        count = lax.axis_size(axis)
        ends = count - 1
        head = lax.slice_in_dim(cells, 0, width, axis=dim)
        tail = lax.slice_in_dim(cells, cells.shape[dim] - width, cells.shape[dim], axis=dim)
        cells = jnp.concatenate(
            [
                lax.ppermute(tail, axis, [(i, (i + 1) % count) for i in range(ends)]),
                cells,
                lax.ppermute(head, axis, [((i + 1) % count, i) for i in range(ends)]),
            ],
            axis=dim,
        )
    return cells


def tap_weights():
    raw_taps = [math.exp(-(offset - 4) * (offset - 4) / 4.5) for offset in range(9)]
    tap_total = sum(raw_taps)
    return [tap_value / tap_total for tap_value in raw_taps]


def correlate(fwd_field, adj_field):
    lead_shape = fwd_field.shape[:-2]
    fwd_split = fwd_field.reshape(lead_shape + (NFREQ, 3, 2, fwd_field.shape[-1]))
    adj_split = adj_field.reshape(lead_shape + (NFREQ, 3, 2, adj_field.shape[-1]))
    products = (
        fwd_split[..., 0, :] * adj_split[..., 0, :] - fwd_split[..., 1, :] * adj_split[..., 1, :]
    )
    horizontal = jnp.sum(products[..., 0:2, :], axis=(-3, -2))
    vertical = jnp.sum(products[..., 2, :], axis=-2)
    return jnp.stack([horizontal, vertical], axis=-2)


def smooth_axis(padded, axis):
    weights = tap_weights()
    length = padded.shape[axis] - 8
    summed = jnp.zeros(padded.shape[:axis] + (length,) + padded.shape[axis + 1 :], jnp.float32)
    for offset in range(9):
        summed = summed + weights[offset] * lax.slice_in_dim(
            padded, offset, offset + length, axis=axis
        )
    return summed


def pad_axis(field, axis):
    widths = [(0, 0)] * field.ndim
    widths[axis] = (4, 4)
    return jnp.pad(field, widths)


def lookup(indices, table):
    hits = indices[:, None] == jnp.arange(table.shape[0], dtype=jnp.int32)[None, :]
    return jnp.sum(jnp.where(hits, table[None, :], 0), axis=1)


def local(forward, item_tx, item_brick, tx_place, brick_place, adjoint):
    stored = forward.shape[0]
    channels = forward.shape[1]
    cells = forward.shape[2]
    src_count = lax.axis_size("src")
    vol_count = lax.axis_size("vol")
    devices = src_count * vol_count
    local_tx = adjoint.shape[0]
    local_bricks = adjoint.shape[1]
    capacity = max(2, 2 * stored // devices)
    slot_total = devices * capacity
    tx_at = lookup(item_tx, tx_place)
    brick_at = lookup(item_brick, brick_place)
    destination = tx_at // local_tx * vol_count + brick_at // local_bricks
    pair_index = tx_at % local_tx * local_bricks + brick_at % local_bricks
    positions = jnp.arange(stored, dtype=jnp.int32)
    same_owner = destination[:, None] == destination[None, :]
    earlier = positions[:, None] > positions[None, :]
    order_rank = jnp.sum((same_owner & earlier).astype(jnp.int32), axis=1)
    slot_index = destination * capacity + order_rank
    outgoing = jnp.zeros((slot_total, channels, cells), forward.dtype).at[slot_index].set(forward)
    slot_pairs = jnp.full((slot_total,), -1, jnp.int32).at[slot_index].set(pair_index)
    arrived, arrived_pairs = (
        lax.all_to_all(outgoing, ("src", "vol"), split_axis=0, concat_axis=0, tiled=True),
        lax.all_to_all(slot_pairs, ("src", "vol"), split_axis=0, concat_axis=0, tiled=True),
    )
    filled = arrived_pairs >= 0
    flat_adjoint = adjoint.reshape(local_tx * local_bricks, channels, cells)
    picked = flat_adjoint[jnp.maximum(arrived_pairs, 0)]
    product = correlate(arrived.astype(jnp.float32), picked.astype(jnp.float32))
    owner_brick = arrived_pairs % local_bricks
    owner_table = (
        (owner_brick[None, :] == jnp.arange(local_bricks, dtype=jnp.int32)[:, None])
        & filled[None, :]
    ).astype(jnp.float32)
    gradient = jnp.dot(
        owner_table, product.reshape(slot_total, 2 * cells), precision=lax.Precision.HIGHEST
    )
    gradient = gradient.reshape(local_bricks, 2, cells)
    slab = (
        gradient.reshape(NBY, NBZ, 2, E, E, E)
        .transpose(2, 3, 0, 4, 1, 5)
        .reshape(2, E, NBY * E, NBZ * E)
    )
    summed = lax.psum(slab, "src")
    padded = with_halo(summed, (("vol", 1),), 4)
    field = smooth_axis(padded, 1)
    for axis in (2, 3):
        field = smooth_axis(pad_axis(field, axis), axis)
    return field


def solution(mesh):
    in_specs = (
        P(("src", "vol"), None, None),
        P(("src", "vol")),
        P(("src", "vol")),
        P(),
        P(),
        P("src", "vol", None, None),
    )
    out_specs = P(None, "vol", None, None)
    return jax.shard_map(local, mesh=mesh, in_specs=in_specs, out_specs=out_specs, check_vma=False)
```

profile of v0, /device:TPU:57, one launch (start us, length us, event | category | flops | bytes accessed | tf_op | source)
XLA Modules:
  0.0 294.8 jit_solution(5812231663383494735)
XLA Ops:
  6.5 0.8 select_reduce_fusion.1
  7.3 0.9 select_reduce_fusion
  8.4 1.0 scatter_custom_fusion
  9.4 0.8 all_to_all.11
  10.2 10.4 %all-to-all-start = ((s32[128,2,1]{1,2,0:T(1,128)}), s32[128,2,1]{1,2,0:T(1,128)S(1)}, u32[]{:S(2)}, u32[]{:S(2)}) async-start(s32[128,2,1]{1,2,0:T(1,128)} %bitcast.4), calls=%async_computation | async-start | bytes 131072 | tf_op jit(solution)/shard_map/all_to_all | solution.py:95
  20.6 7.3 %copy.49 = bf16[128,36,512]{2,1,0:T(8,128)(2,1)} copy(bf16[128,36,512]{2,0,1:T(8,128)(2,1)} %param.6) | data formatting | bytes 9437184 | tf_op args[0]
  27.9 4.6 %broadcast_in_dim.33 = bf16[256,36,512]{2,1,0:T(8,128)(2,1)} broadcast(bf16[]{:T(256)} %constant.76.clone.1), dimensions={} | broadcast | bytes 9437186 | tf_op jit(solution)/shard_map/broadcast_in_dim | solution.py:91
  32.5 20.5 %scatter_fusion = bf16[256,36,512]{2,1,0:T(8,128)(2,1)} fusion(bf16[256,36,512]{2,1,0:T(8,128)(2,1)} %broadcast_in_dim.33, s32[128]{0:T(128)S(1)} %fusion.52, bf16[128,36,512]{2,1,0:T(8,128)(2,1)} %copy.49), kind=kCustom, calls=%fused_computation.2 | custom fusion | bytes 14156288 | tf_op jit(solution)/shard_map/scatter | solution.py:91
  52.9 10.2 %all-to-all-start.1 = ((bf16[256,36,512]{2,1,0:T(8,128)(2,1)}), bf16[256,36,512]{2,1,0:T(8,128)(2,1)}, u32[]{:S(2)}, u32[]{:S(2)}) async-start(bf16[256,36,512]{2,1,0:T(8,128)(2,1)} %scatter_fusion), calls=%async_computation.1 | async-start | bytes 20971520 | tf_op jit(solution)/shard_map/all_to_all | solution.py:94
  63.4 2.7 copy.51
  66.1 5.1 %copy.52 = bf16[128,36,512]{2,1,0:T(8,128)(2,1)} copy(bf16[128,36,512]{2,0,1:T(8,128)(2,1)S(1)} %bitcast.58) | data formatting | bytes 9437184 | tf_op jit(solution)/shard_map/reshape | solution.py:98
  71.1 0.5 broadcast.393
  71.6 1.0 fusion.55
  72.9 12.1 %gather_fusion = bf16[256,36,512]{2,1,0:T(8,128)(2,1)} fusion(bf16[128,36,512]{2,1,0:T(8,128)(2,1)} %copy.52, s32[1024]{0:T(1024)S(1)} %pad_clamp_fusion), kind=kCustom, calls=%fused_computation | custom fusion | bytes 18875392 | tf_op jit(solution)/shard_map/gather | solution.py:99
  85.1 10.9 %copy.53 = bf16[256,36,512]{2,0,1:T(8,128)(2,1)} copy(bf16[256,36,512]{2,1,0:T(8,128)(2,1)} %gather_fusion) | data formatting | bytes 18874368 | tf_op jit(solution)/shard_map/gather | solution.py:99
  95.9 12.7 %convert.3 = f32[256,6,3,2,512]{4,0,3,2,1:T(8,128)} convert(bf16[256,6,3,2,512]{4,0,3,2,1:T(8,128)(2,1)} %bitcast.56) | non-fusion elementwise | flops 4718592 | bytes 28311552 | tf_op jit(solution)/shard_map/convert_element_type | solution.py:100
  108.7 78.3 %all-to-all-done.1 = bf16[256,36,512]{2,1,0:T(8,128)(2,1)} async-done(((bf16[256,36,512]{2,1,0:T(8,128)(2,1)}), bf16[256,36,512]{2,1,0:T(8,128)(2,1)}, u32[]{:S(2)}, u32[]{:S(2)}) %all-to-all-start.1) | async-done | bytes 9437216 | tf_op jit(solution)/shard_map/all_to_all | solution.py:94
  187.0 10.9 %copy.50 = bf16[256,36,512]{2,0,1:T(8,128)(2,1)} copy(bf16[256,36,512]{2,1,0:T(8,128)(2,1)} %all-to-all-done.1) | data formatting | bytes 18874368 | tf_op jit(solution)/shard_map/all_to_all | solution.py:94
  197.9 12.7 %convert.2 = f32[256,6,3,2,512]{4,0,3,2,1:T(8,128)} convert(bf16[256,6,3,2,512]{4,0,3,2,1:T(8,128)(2,1)} %bitcast.57) | non-fusion elementwise | flops 4718592 | bytes 28311552 | tf_op jit(solution)/shard_map/reshape | solution.py:39
  210.6 14.0 %fusion.1 = f32[256,6,3,512]{3,0,2,1:T(8,128)S(1)} fusion(f32[256,6,3,2,512]{4,0,3,2,1:T(8,128)} %convert.3, f32[256,6,3,2,512]{4,0,3,2,1:T(8,128)} %convert.2), kind=kLoop, calls=%fused_computation.5 | loop fusion | flops 7077888 | bytes 47185920 | tf_op jit(solution)/shard_map/sub | solution.py:42
  225.0 0.7 slice_reduce_fusion
  226.1 0.7 convolution_bitcast_fusion
  226.8 0.6 copy.55
  227.5 1.6 reshape.258
  229.1 44.7 %all-reduce.4.cloned.1.call-done = f32[2,8,16,128]{3,2,1,0:T(8,128)} async-done(((f32[2,8,16,128]{3,2,1,0:T(8,128)}), f32[2,8,16,128]{3,2,1,0:T(8,128)}) %all-reduce.4.cloned.1.call-update) | async-done | bytes 131088 | tf_op jit(solution)/shard_map/psum | solution.py:115
  273.8 0.9 fusion.56
  274.7 5.4 %collective-permute-start = (f32[2,4,16,128]{3,2,1,0:T(8,128)S(1)}, f32[2,4,16,128]{3,2,1,0:T(8,128)S(1)}, u32[]{:S(2)}, u32[]{:S(2)}) collective-permute-start(f32[2,4,16,128]{3,2,1,0:T(8,128)S(1)} %get-tuple-element.9), channel_id=1, source_target_pairs={{0,1},{1,2},{2,3},{3,4},{4,5},{5,6},{6,7},{7,8},{8,9},{9,10},{10,1... | collective-permute-start | bytes 196616 | tf_op jit(solution)/shard_map/ppermute | solution.py:22
  280.2 1.9 collective-permute-start.1
  282.1 0.9 constant_dynamic-update-slice_fusion
  283.1 2.7 collective-permute-done.1
  285.8 1.0 fusion.34
  286.9 1.0 fusion.26
  (19 shorter events, 1.7 us)
Async XLA Ops:
  10.2 42.8 %all-to-all-start = ((s32[128,2,1]{1,2,0:T(1,128)}), s32[128,2,1]{1,2,0:T(1,128)S(1)}, u32[]{:S(2)}, u32[]{:S(2)}) async-start(s32[128,2,1]{1,2,0:T(1,128)} %bitcast.4), calls=%async_computation | async-start | bytes 131072 | tf_op jit(solution)/shard_map/all_to_all | solution.py:95
  52.9 134.0 %all-to-all-start.1 = ((bf16[256,36,512]{2,1,0:T(8,128)(2,1)}), bf16[256,36,512]{2,1,0:T(8,128)(2,1)}, u32[]{:S(2)}, u32[]{:S(2)}) async-start(bf16[256,36,512]{2,1,0:T(8,128)(2,1)} %scatter_fusion), calls=%async_computation.1 | async-start | bytes 20971520 | tf_op jit(solution)/shard_map/all_to_all | solution.py:94
  63.1 210.7 %all-reduce.4.cloned.1.call-start = ((), (), s32[]{:S(2)}) async-start(), calls=%async_computation.2 | async-start | bytes 262144 | tf_op jit(solution)/shard_map/psum | solution.py:115
  274.7 7.4 %collective-permute-start = (f32[2,4,16,128]{3,2,1,0:T(8,128)S(1)}, f32[2,4,16,128]{3,2,1,0:T(8,128)S(1)}, u32[]{:S(2)}, u32[]{:S(2)}) collective-permute-start(f32[2,4,16,128]{3,2,1,0:T(8,128)S(1)} %get-tuple-element.9), channel_id=1, source_target_pairs={{0,1},{1,2},{2,3},{3,4},{4,5},{5,6},{6,7},{7,8},{8,9},{9,10},{10,1... | collective-permute-start | bytes 196616 | tf_op jit(solution)/shard_map/ppermute | solution.py:22
  280.2 5.6 %collective-permute-start.1 = (f32[2,4,16,128]{3,2,1,0:T(8,128)S(1)}, f32[2,4,16,128]{3,2,1,0:T(8,128)S(1)}, u32[]{:S(2)}, u32[]{:S(2)}) collective-permute-start(f32[2,4,16,128]{3,2,1,0:T(8,128)S(1)} %get-tuple-element.10), channel_id=1, source_target_pairs={{1,0},{2,1},{3,2},{4,3},{5,4},{6,5},{7,6},{8,7},{9,8},{10,9},{11,1... | collective-permute-start | bytes 196616 | tf_op jit(solution)/shard_map/ppermute | solution.py:24
Sparse Core Ops, SparseCore 0:
  229.2 44.5 all-reduce.3
where the time goes:
time: 300 us; the launch traced here: 295 us
  waiting for transfers between devices  126 us (42%)
  local copies, waits for them, and re-layouts  81 us (27%)
  other arithmetic  45.6 us (15%)
  starting transfers between devices  28.2 us (9%)
  between operations  13.6 us (5%)
    all_to_all x1, waiting for transfers between devices, local(): lax.all_to_all(outgoing, ('src', 'vol'), split_axis=0, concat_axis=0, til...  78.3 us
    psum x1, waiting for transfers between devices, local(): summed = lax.psum(slab, 'src')  44.7 us
    gather x2, local copies, waits for them, and re-layouts, local(): picked = flat_adjoint[jnp.maximum(arrived_pairs, 0)]  23 us
    scatter x1, local copies, waits for them, and re-layouts, local(): jnp.zeros((slot_total, channels, cells), forward.dtype).at[slot_index]  20.5 us
    sub x1, other arithmetic, correlate(): fwd_split[..., 0, :] * adj_split[..., 0, :]  14 us
    convert_element_type x1, other arithmetic, local(): product = correlate(arrived.astype(jnp.float32), picked.astype(jnp.float32))  12.7 us
    reshape x1, other arithmetic, correlate(): fwd_field.reshape(lead_shape + (NFREQ, 3, 2, fwd_field.shape[-1]))  12.7 us
    all_to_all x1, local copies, waits for them, and re-layouts, local(): lax.all_to_all(outgoing, ('src', 'vol'), split_axis=0, concat_axis=0, til...  10.9 us
  transfers between devices with their start and end apart: 5, of which 3 were waited for; matrix products, arithmetic and copies ran while one was open for 27% of the time, Pallas kernels for 0%

commit v1 on v0

v1 whole, which is shorter than its diff:
```python
import math

import jax
import jax.numpy as jnp
from jax import lax
from jax.experimental import pallas as pl
from jax.experimental.pallas import tpu as pltpu
from jax.sharding import PartitionSpec as P

E = 8
NFREQ = 6
NBY = 2
NBZ = 16
LANES = 128
META = 16


def with_halo(cells, sides, width):
    for axis, dim in sides:
        count = lax.axis_size(axis)
        ends = count - 1
        head = lax.slice_in_dim(cells, 0, width, axis=dim)
        tail = lax.slice_in_dim(cells, cells.shape[dim] - width, cells.shape[dim], axis=dim)
        cells = jnp.concatenate(
            [
                lax.ppermute(tail, axis, [(i, (i + 1) % count) for i in range(ends)]),
                cells,
                lax.ppermute(head, axis, [((i + 1) % count, i) for i in range(ends)]),
            ],
            axis=dim,
        )
    return cells


def tap_weights():
    raw_taps = [math.exp(-(offset - 4) * (offset - 4) / 4.5) for offset in range(9)]
    tap_total = sum(raw_taps)
    return [tap_value / tap_total for tap_value in raw_taps]


def smooth_axis(padded, axis):
    weights = tap_weights()
    length = padded.shape[axis] - 8
    summed = jnp.zeros(padded.shape[:axis] + (length,) + padded.shape[axis + 1 :], jnp.float32)
    for offset in range(9):
        summed = summed + weights[offset] * lax.slice_in_dim(
            padded, offset, offset + length, axis=axis
        )
    return summed


def pad_axis(field, axis):
    widths = [(0, 0)] * field.ndim
    widths[axis] = (4, 4)
    return jnp.pad(field, widths)


def lookup(indices, table):
    hits = indices[:, None] == jnp.arange(table.shape[0], dtype=jnp.int32)[None, :]
    return jnp.sum(jnp.where(hits, table[None, :], 0), axis=1)


def pack_kernel(src_ref, pair_ref, fwd_ref, out_ref):
    dests = out_ref.shape[0]
    rows = fwd_ref.shape[1]
    base = pl.program_id(0) * dests * 2

    def one_dest(d, carry):
        slot = base + 2 * d
        first = src_ref[slot]
        second = src_ref[slot + 1]
        out_ref[d, 0:rows, :] = fwd_ref[jnp.maximum(first, 0)]
        out_ref[d, rows : 2 * rows, :] = fwd_ref[jnp.maximum(second, 0)]
        row_at = lax.broadcasted_iota(jnp.int32, (META, LANES), 0)
        tags = jnp.where(row_at < META // 2, pair_ref[slot], pair_ref[slot + 1])
        out_ref[d, 2 * rows : 2 * rows + META, :] = tags.astype(jnp.float32).astype(out_ref.dtype)
        return carry

    lax.fori_loop(0, dests, one_dest, 0)


def correlate_kernel(pair_ref, arrived_ref, adj_ref, acc_ref):
    dests = arrived_ref.shape[0]
    rows = adj_ref.shape[2]
    bricks = adj_ref.shape[1]
    groups = rows // 8
    step = pl.program_id(0)

    @pl.when(step == 0)
    def _():
        acc_ref[...] = jnp.zeros(acc_ref.shape, acc_ref.dtype)

    base = step * dests * 2

    def one_slot(d, s):
        pair = pair_ref[base + 2 * d + s]

        @pl.when(pair >= 0)
        def _():
            tx = pair // bricks
            brick = pair % bricks
            fwd = arrived_ref[d, s * rows : (s + 1) * rows, :].astype(jnp.float32)
            adj = adj_ref[tx, brick].astype(jnp.float32)
            prod = (fwd * adj).reshape(groups, 8, LANES)
            horizontal = None
            vertical = None
            for g in range(groups):
                if g % 3 == 2:
                    vertical = prod[g] if vertical is None else vertical + prod[g]
                else:
                    horizontal = prod[g] if horizontal is None else horizontal + prod[g]
            acc_ref[brick, 0] += horizontal
            acc_ref[brick, 1] += vertical

    def one_dest(d, carry):
        one_slot(d, 0)
        one_slot(d, 1)
        return carry

    lax.fori_loop(0, dests, one_dest, 0)


def src_sum(part):
    count = lax.axis_size("src")
    me = lax.axis_index("src")
    parts = [part] + [
        lax.ppermute(part, "src", [(i, (i + k) % count) for i in range(count)])
        for k in range(1, count)
    ]
    stacked = jnp.stack(parts)
    total = lax.dynamic_index_in_dim(stacked, me % count, keepdims=False)
    for j in range(1, count):
        total = total + lax.dynamic_index_in_dim(stacked, (me - j) % count, keepdims=False)
    return total


def local(forward, item_tx, item_brick, tx_place, brick_place, adjoint):
    stored = forward.shape[0]
    channels = forward.shape[1]
    cells = forward.shape[2]
    rows = channels * cells // LANES
    src_count = lax.axis_size("src")
    vol_count = lax.axis_size("vol")
    devices = src_count * vol_count
    local_tx = adjoint.shape[0]
    local_bricks = adjoint.shape[1]
    capacity = 2
    slot_total = devices * capacity
    tx_at = lookup(item_tx, tx_place)
    brick_at = lookup(item_brick, brick_place)
    destination = tx_at // local_tx * vol_count + brick_at // local_bricks
    pair_index = tx_at % local_tx * local_bricks + brick_at % local_bricks
    positions = jnp.arange(stored, dtype=jnp.int32)
    same_owner = destination[:, None] == destination[None, :]
    earlier = positions[:, None] > positions[None, :]
    order_rank = jnp.sum((same_owner & earlier).astype(jnp.int32), axis=1)
    slot_index = destination * capacity + order_rank
    slot_hits = slot_index[None, :] == jnp.arange(slot_total, dtype=jnp.int32)[:, None]
    filled = jnp.any(slot_hits, axis=1)
    src_of_slot = jnp.where(
        filled, jnp.sum(jnp.where(slot_hits, positions[None, :], 0), axis=1), -1
    ).astype(jnp.int32)
    pair_of_slot = jnp.where(
        filled, jnp.sum(jnp.where(slot_hits, pair_index[None, :], 0), axis=1), -1
    ).astype(jnp.int32)

    fwd_rows = forward.reshape(stored, rows, LANES)
    chunk = 2 * rows + META
    pack_steps = 8
    dests_per_step = devices // pack_steps
    payload = pl.pallas_call(
        pack_kernel,
        out_shape=jax.ShapeDtypeStruct((devices, chunk, LANES), forward.dtype),
        grid_spec=pltpu.PrefetchScalarGridSpec(
            num_scalar_prefetch=2,
            grid=(pack_steps,),
            in_specs=[pl.BlockSpec((stored, rows, LANES), lambda g, s, p: (0, 0, 0))],
            out_specs=pl.BlockSpec((dests_per_step, chunk, LANES), lambda g, s, p: (g, 0, 0)),
        ),
        compiler_params=pltpu.CompilerParams(vmem_limit_bytes=48 * 1024 * 1024),
    )(src_of_slot, pair_of_slot, fwd_rows)

    arrived = lax.all_to_all(payload, ("src", "vol"), split_axis=0, concat_axis=0, tiled=True)
    tags = jnp.stack(
        [arrived[:, 2 * rows, 0], arrived[:, 2 * rows + META // 2, 0]], axis=1
    ).reshape(slot_total)
    arrived_pairs = tags.astype(jnp.float32).astype(jnp.int32)

    adj_rows = adjoint.reshape(local_tx, local_bricks, rows, LANES)
    acc = pl.pallas_call(
        correlate_kernel,
        out_shape=jax.ShapeDtypeStruct((local_bricks, 2, 8, LANES), jnp.float32),
        grid_spec=pltpu.PrefetchScalarGridSpec(
            num_scalar_prefetch=1,
            grid=(pack_steps,),
            in_specs=[
                pl.BlockSpec((dests_per_step, chunk, LANES), lambda g, p: (g, 0, 0)),
                pl.BlockSpec((local_tx, local_bricks, rows, LANES), lambda g, p: (0, 0, 0, 0)),
            ],
            out_specs=pl.BlockSpec((local_bricks, 2, 8, LANES), lambda g, p: (0, 0, 0, 0)),
        ),
        compiler_params=pltpu.CompilerParams(vmem_limit_bytes=48 * 1024 * 1024),
    )(arrived_pairs, arrived, adj_rows)

    gradient = (acc[:, :, 0:4, :] - acc[:, :, 4:8, :]).reshape(local_bricks, 2, cells)
    slab = (
        gradient.reshape(NBY, NBZ, 2, E, E, E)
        .transpose(2, 3, 0, 4, 1, 5)
        .reshape(2, E, NBY * E, NBZ * E)
    )
    summed = src_sum(slab)
    padded = with_halo(summed, (("vol", 1),), 4)
    field = smooth_axis(padded, 1)
    for axis in (2, 3):
        field = smooth_axis(pad_axis(field, axis), axis)
    return field


def solution(mesh):
    in_specs = (
        P(("src", "vol"), None, None),
        P(("src", "vol")),
        P(("src", "vol")),
        P(),
        P(),
        P("src", "vol", None, None),
    )
    out_specs = P(None, "vol", None, None)
    return jax.shard_map(local, mesh=mesh, in_specs=in_specs, out_specs=out_specs, check_vma=False)
```

time: 300 us -> 197 us (0.66); the launches traced: 295 us -> 196 us
  other arithmetic: 45.6 us -> 3.46 us
  local copies, waits for them, and re-layouts: 81 us -> 40.4 us
  waiting for transfers between devices: 126 us -> 106 us
  Pallas kernels: 0 us -> 15.4 us
  between operations: 13.6 us -> 0.15 us
    psum x1 -> x0, waiting for transfers between devices: 44.7 us -> none  [local(): summed = lax.psum(slab, 'src')]
    gather x2 -> x0, local copies, waits for them, and re-layouts: 23 us -> none  [local(): picked = flat_adjoint[jnp.maximum(arrived_pairs, 0)]]
    scatter x2 -> x0, local copies, waits for them, and re-layouts: 21.5 us -> none  [the longest x1 20.5 us: local(): jnp.zeros((slot_total, channels, cells), forward.dtype).at[slot_index]]
    all_to_all x2 -> x1, waiting for transfers between devices: 78.3 us -> 99 us  [local(): lax.all_to_all(payload, ('src', 'vol'), split_axis=0, concat_axis=0, tile...]
    pallas_call x0 -> x2, Pallas kernels: none -> 15.4 us  [the longest x1 9.23 us: local(): pl.pallas_call(correlate_kernel, out_shape=jax.ShapeDtypeStruct((local_br...]
    sub x1, other arithmetic: 14 us -> 0.03 us  [local(): acc[:, :, 0:4, :] - acc[:, :, 4:8, :]]
    convert_element_type x1, other arithmetic: 12.7 us -> 0.01 us  [local(): arrived_pairs = tags.astype(jnp.float32).astype(jnp.int32)]
    reshape x1 -> x0, other arithmetic: 12.7 us -> none  [correlate(): fwd_field.reshape(lead_shape + (NFREQ, 3, 2, fwd_field.shape[-1]))]
  transfers between devices with their start and end apart: 5 -> 6, of which waited for: 3 -> 3; matrix products, arithmetic and copies ran while one was open for 27% -> 9% of each run, Pallas kernels for 0% -> 0%
where the time goes in v1:
time: 197 us; the launch traced here: 196 us
  waiting for transfers between devices  106 us (54%)
  local copies, waits for them, and re-layouts  40.4 us (21%)
  starting transfers between devices  30.7 us (16%)
  Pallas kernels  15.4 us (8%)
  other arithmetic  3.46 us (2%)
    all_to_all x1, waiting for transfers between devices, local(): lax.all_to_all(payload, ('src', 'vol'), split_axis=0, concat_axis=0, tile...  99 us
    unnamed x6, local copies, waits for them, and re-layouts  18.6 us
    all_to_all x1, starting transfers between devices, local(): lax.all_to_all(payload, ('src', 'vol'), split_axis=0, concat_axis=0, tile...  10.8 us
    ppermute x1, starting transfers between devices, with_halo(): lax.ppermute(tail, axis, [(i, (i + 1) % count) for i in range(ends)])  10.2 us
    pallas_call x1, Pallas kernels, local(): pl.pallas_call(correlate_kernel, out_shape=jax.ShapeDtypeStruct((local_br...  9.23 us
    reshape x1, local copies, waits for them, and re-layouts, local(): adj_rows = adjoint.reshape(local_tx, local_bricks, rows, LANES)  8.7 us
    ppermute x3, starting transfers between devices, src_sum(): lax.ppermute(part, 'src', [(i, (i + k) % count) for i in range(count)])  7.78 us
    reshape x1, local copies, waits for them, and re-layouts, local(): fwd_rows = forward.reshape(stored, rows, LANES)  6.97 us
  transfers between devices with their start and end apart: 6, of which 3 were waited for; matrix products, arithmetic and copies ran while one was open for 9% of the time, Pallas kernels for 0%

profile of v1, /device:TPU:57, one launch (start us, length us, event | category | flops | bytes accessed | tf_op | source)
XLA Modules:
  0.0 195.6 jit_solution(11082018173707909555)
XLA Ops:
  0.0 0.9 select_reduce_fusion
  0.9 0.8 select_reduce_fusion.3
  1.7 0.2 convert_reduce_fusion
  1.9 0.1 fusion.54
  2.0 0.2 select_reduce_fusion.1
  2.1 6.6 %copy.18 = bf16[128,36,512]{0,2,1:T(8,128)(2,1)} copy(bf16[128,36,512]{2,0,1:T(8,128)(2,1)} %param.6) | data formatting | bytes 9437184 | tf_op args[0]
  8.8 7.0 %copy.19.fwd_ref = bf16[128,144,128]{2,1,0:T(8,128)(2,1)} copy(bf16[128,144,128]{0,2,1:T(8,128)(2,1)} %bitcast.17) | data formatting | bytes 9437184 | tf_op jit(solution)/shard_map/reshape | solution.py:167
  15.7 2.3 %copy-done.1 = bf16[128,144,128]{2,1,0:T(8,128)(2,1)S(1)} copy-done((bf16[128,144,128]{2,1,0:T(8,128)(2,1)S(1)}, bf16[128,144,128]{2,1,0:T(8,128)(2,1)}, u32[]{:S(2)}) %copy-start.1) | copy-done | bytes 4718616
  18.1 6.1 %shard_map.64 = bf16[128,304,128]{2,1,0:T(8,128)(2,1)} custom-call(s32[256]{0:T(256)S(1)} %get-tuple-element.14.src_ref, s32[256]{0:T(256)S(1)} %get-tuple-element.13.pair_ref, bf16[128,144,128]{2,1,0:T(8,128)(2,1)S(1)} %copy-done.1), custom_call_target="tpu_custom_call" | custom-call | tf_op jit(solution)/shard_map/pallas_call | solution.py:171
  24.2 10.8 %all-to-all-start = ((bf16[128,304,128]{2,1,0:T(8,128)(2,1)}), bf16[128,304,128]{2,1,0:T(8,128)(2,1)}, u32[]{:S(2)}, u32[]{:S(2)}) async-start(bf16[128,304,128]{2,1,0:T(8,128)(2,1)} %shard_map.64), calls=%async_computation | async-start | bytes 19922944 | tf_op jit(solution)/shard_map/all_to_all | solution.py:183
  35.0 7.4 %copy.21 = bf16[4,32,36,512]{3,2,1,0:T(8,128)(2,1)} copy(bf16[4,32,36,512]{3,1,2,0:T(8,128)(2,1)} %param.11) | data formatting | bytes 9437184 | tf_op args[5]
  42.4 8.7 %reshape.128.adj_ref = bf16[4,32,144,128]{3,2,1,0:T(8,128)(2,1)} reshape(bf16[4,32,36,512]{3,2,1,0:T(8,128)(2,1)} %copy.21) | data formatting | bytes 9437184 | tf_op jit(solution)/shard_map/reshape | solution.py:189
  51.1 99.0 %all-to-all-done.arrived_ref = bf16[128,304,128]{2,1,0:T(8,128)(2,1)} async-done(((bf16[128,304,128]{2,1,0:T(8,128)(2,1)}), bf16[128,304,128]{2,1,0:T(8,128)(2,1)}, u32[]{:S(2)}, u32[]{:S(2)}) %all-to-all-start) | async-done | bytes 9961504 | tf_op jit(solution)/shard_map/all_to_all | solution.py:183
  150.0 2.1 %slice_reduce_fusion.1 = (bf16[128]{0:T(256)(128)(2,1)S(1)}, bf16[128]{0:T(256)(128)(2,1)S(1)}) fusion(bf16[128,304,128]{2,1,0:T(8,128)(2,1)} %all-to-all-done.arrived_ref), kind=kLoop, calls=%fused_computation.94 | loop fusion | bytes 1024 | tf_op jit(solution)/shard_map/slice | solution.py:185
  152.1 0.1 copy.20
  152.2 0.1 convert_element_type.19.pair_ref
  152.4 2.3 %copy-done = bf16[4,32,144,128]{3,2,1,0:T(8,128)(2,1)S(1)} copy-done((bf16[4,32,144,128]{3,2,1,0:T(8,128)(2,1)S(1)}, bf16[4,32,144,128]{3,2,1,0:T(8,128)(2,1)}, u32[]{:S(2)}) %copy-start) | copy-done | bytes 4718616
  154.7 9.2 %shard_map.65 = f32[32,2,8,128]{3,2,1,0:T(8,128)S(1)} custom-call(s32[256]{0:T(256)S(1)} %convert_element_type.19.pair_ref, bf16[128,304,128]{2,1,0:T(8,128)(2,1)} %all-to-all-done.arrived_ref, bf16[4,32,144,128]{3,2,1,0:T(8,128)(2,1)S(1)} %copy-done), custom_call_target="tpu_custom_call" | custom-call | tf_op jit(solution)/shard_map/pallas_call | solution.py:190
  164.0 0.2 copy.22
  164.2 0.6 reshape_reshape.3
  164.8 0.9 copy.23
  165.7 1.0 reshape.129
  166.7 0.4 collective-permute-start
  167.1 5.4 %collective-permute-start.1 = (f32[2,8,16,128]{3,2,1,0:T(8,128)S(1)}, f32[2,8,16,128]{3,2,1,0:T(8,128)S(1)}, u32[]{:S(2)}, u32[]{:S(2)}) collective-permute-start(f32[2,8,16,128]{3,2,1,0:T(8,128)S(1)} %reshape.129), channel_id=1, source_target_pairs={{0,64},{32,96},{64,0},{96,32},{1,65},{33,97},{65,1},{97,33},{2,66}... | collective-permute-start | bytes 393224 | tf_op jit(solution)/shard_map/ppermute | solution.py:127
  172.5 2.0 %collective-permute-start.2 = (f32[2,8,16,128]{3,2,1,0:T(8,128)S(1)}, f32[2,8,16,128]{3,2,1,0:T(8,128)S(1)}, u32[]{:S(2)}, u32[]{:S(2)}) collective-permute-start(f32[2,8,16,128]{3,2,1,0:T(8,128)S(1)} %reshape.129), channel_id=1, source_target_pairs={{0,96},{32,0},{64,32},{96,64},{1,97},{33,1},{65,33},{97,65},{2,98}... | collective-permute-start | bytes 393224 | tf_op jit(solution)/shard_map/ppermute | solution.py:127
  174.5 1.0 stack_reshape.3
  175.6 2.9 %collective-permute-done.2 = f32[2,8,16,128]{3,2,1,0:T(8,128)S(1)} collective-permute-done((f32[2,8,16,128]{3,2,1,0:T(8,128)S(1)}, f32[2,8,16,128]{3,2,1,0:T(8,128)S(1)}, u32[]{:S(2)}, u32[]{:S(2)}) %collective-permute-start.2) | collective-permute-done | bytes 131104 | tf_op jit(solution)/shard_map/ppermute | solution.py:127
  178.6 10.2 %collective-permute-start.3 = (f32[2,4,16,128]{3,2,1,0:T(8,128)S(1)}, f32[2,4,16,128]{3,2,1,0:T(8,128)S(1)}, u32[]{:S(2)}, u32[]{:S(2)}) collective-permute-start(f32[2,4,16,128]{3,2,1,0:T(8,128)S(1)} %get-tuple-element.9), channel_id=1, source_target_pairs={{0,1},{1,2},{2,3},{3,4},{4,5},{5,6},{6,7},{7,8},{8,9},{9,10},{10,1... | collective-permute-start | bytes 196616 | tf_op jit(solution)/shard_map/ppermute | solution.py:26
  188.8 1.9 collective-permute-start.4
  190.8 3.6 %collective-permute-done.4 = f32[2,4,16,128]{3,2,1,0:T(8,128)S(1)} collective-permute-done((f32[2,4,16,128]{3,2,1,0:T(8,128)S(1)}, f32[2,4,16,128]{3,2,1,0:T(8,128)S(1)}, u32[]{:S(2)}, u32[]{:S(2)}) %collective-permute-start.4) | collective-permute-done | bytes 65568 | tf_op jit(solution)/shard_map/ppermute | solution.py:28
  194.5 0.1 fusion.28
  194.6 1.0 fusion.44
  (14 shorter events, 0.2 us)
Async XLA Ops:
  15.7 2.3 %copy-start.1 = (bf16[128,144,128]{2,1,0:T(8,128)(2,1)S(1)}, bf16[128,144,128]{2,1,0:T(8,128)(2,1)}, u32[]{:S(2)}) copy-start(bf16[128,144,128]{2,1,0:T(8,128)(2,1)} %copy.19.fwd_ref) | copy-start | bytes 14155780
  24.2 125.8 %all-to-all-start = ((bf16[128,304,128]{2,1,0:T(8,128)(2,1)}), bf16[128,304,128]{2,1,0:T(8,128)(2,1)}, u32[]{:S(2)}, u32[]{:S(2)}) async-start(bf16[128,304,128]{2,1,0:T(8,128)(2,1)} %shard_map.64), calls=%async_computation | async-start | bytes 19922944 | tf_op jit(solution)/shard_map/all_to_all | solution.py:183
  152.4 2.3 %copy-start = (bf16[4,32,144,128]{3,2,1,0:T(8,128)(2,1)S(1)}, bf16[4,32,144,128]{3,2,1,0:T(8,128)(2,1)}, u32[]{:S(2)}) copy-start(bf16[4,32,144,128]{3,2,1,0:T(8,128)(2,1)} %reshape.128.adj_ref) | copy-start | bytes 14155780
  166.7 8.8 %collective-permute-start = (f32[2,8,16,128]{3,2,1,0:T(8,128)S(1)}, f32[2,8,16,128]{3,2,1,0:T(8,128)S(1)}, u32[]{:S(2)}, u32[]{:S(2)}) collective-permute-start(f32[2,8,16,128]{3,2,1,0:T(8,128)S(1)} %reshape.129), channel_id=1, source_target_pairs={{0,32},{32,64},{64,96},{96,0},{1,33},{33,65},{65,97},{97,1},{2,34}... | collective-permute-start | bytes 393224 | tf_op jit(solution)/shard_map/ppermute | solution.py:127
  167.1 8.4 %collective-permute-start.1 = (f32[2,8,16,128]{3,2,1,0:T(8,128)S(1)}, f32[2,8,16,128]{3,2,1,0:T(8,128)S(1)}, u32[]{:S(2)}, u32[]{:S(2)}) collective-permute-start(f32[2,8,16,128]{3,2,1,0:T(8,128)S(1)} %reshape.129), channel_id=1, source_target_pairs={{0,64},{32,96},{64,0},{96,32},{1,65},{33,97},{65,1},{97,33},{2,66}... | collective-permute-start | bytes 393224 | tf_op jit(solution)/shard_map/ppermute | solution.py:127
  172.5 6.0 %collective-permute-start.2 = (f32[2,8,16,128]{3,2,1,0:T(8,128)S(1)}, f32[2,8,16,128]{3,2,1,0:T(8,128)S(1)}, u32[]{:S(2)}, u32[]{:S(2)}) collective-permute-start(f32[2,8,16,128]{3,2,1,0:T(8,128)S(1)} %reshape.129), channel_id=1, source_target_pairs={{0,96},{32,0},{64,32},{96,64},{1,97},{33,1},{65,33},{97,65},{2,98}... | collective-permute-start | bytes 393224 | tf_op jit(solution)/shard_map/ppermute | solution.py:127
  178.6 12.2 %collective-permute-start.3 = (f32[2,4,16,128]{3,2,1,0:T(8,128)S(1)}, f32[2,4,16,128]{3,2,1,0:T(8,128)S(1)}, u32[]{:S(2)}, u32[]{:S(2)}) collective-permute-start(f32[2,4,16,128]{3,2,1,0:T(8,128)S(1)} %get-tuple-element.9), channel_id=1, source_target_pairs={{0,1},{1,2},{2,3},{3,4},{4,5},{5,6},{6,7},{7,8},{8,9},{9,10},{10,1... | collective-permute-start | bytes 196616 | tf_op jit(solution)/shard_map/ppermute | solution.py:26
  188.8 5.6 %collective-permute-start.4 = (f32[2,4,16,128]{3,2,1,0:T(8,128)S(1)}, f32[2,4,16,128]{3,2,1,0:T(8,128)S(1)}, u32[]{:S(2)}, u32[]{:S(2)}) collective-permute-start(f32[2,4,16,128]{3,2,1,0:T(8,128)S(1)} %get-tuple-element.10), channel_id=1, source_target_pairs={{1,0},{2,1},{3,2},{4,3},{5,4},{6,5},{7,6},{8,7},{9,8},{10,9},{11,1... | collective-permute-start | bytes 196616 | tf_op jit(solution)/shard_map/ppermute | solution.py:28

commit v2 on v1

--- a/solution.py
+++ b/solution.py
@@ -13,23 +13,6 @@
 NBZ = 16
 LANES = 128
 META = 16
-
-
-def with_halo(cells, sides, width):
-    for axis, dim in sides:
-        count = lax.axis_size(axis)
-        ends = count - 1
-        head = lax.slice_in_dim(cells, 0, width, axis=dim)
-        tail = lax.slice_in_dim(cells, cells.shape[dim] - width, cells.shape[dim], axis=dim)
-        cells = jnp.concatenate(
-            [
-                lax.ppermute(tail, axis, [(i, (i + 1) % count) for i in range(ends)]),
-                cells,
-                lax.ppermute(head, axis, [((i + 1) % count, i) for i in range(ends)]),
-            ],
-            axis=dim,
-        )
-    return cells
 
 
 def tap_weights():
@@ -117,21 +100,66 @@
         one_slot(d, 1)
         return carry
 
-    lax.fori_loop(0, dests, one_dest, 0)
-
-
-def src_sum(part):
-    count = lax.axis_size("src")
-    me = lax.axis_index("src")
-    parts = [part] + [
-        lax.ppermute(part, "src", [(i, (i + k) % count) for i in range(count)])
-        for k in range(1, count)
-    ]
-    stacked = jnp.stack(parts)
+    lax.fori_loop(0, dests, one_dest, 0, unroll=4)
+
+
+def canonical_sum(received, me, count):
+    stacked = jnp.stack(received)
     total = lax.dynamic_index_in_dim(stacked, me % count, keepdims=False)
     for j in range(1, count):
         total = total + lax.dynamic_index_in_dim(stacked, (me - j) % count, keepdims=False)
     return total
+
+
+def summed_with_halo(part, width):
+    src_count = lax.axis_size("src")
+    vol_count = lax.axis_size("vol")
+    me = lax.axis_index("src")
+    axes = ("src", "vol")
+
+    def flat(s, v):
+        return s * vol_count + v
+
+    head = part[:, :width]
+    tail = part[:, part.shape[1] - width :]
+    centre = [part]
+    from_left = []
+    from_right = []
+    for k in range(src_count):
+        if k:
+            centre.append(
+                lax.ppermute(
+                    part,
+                    axes,
+                    [(flat(s, v), flat((s + k) % src_count, v)) for s in range(src_count) for v in range(vol_count)],
+                )
+            )
+        from_left.append(
+            lax.ppermute(
+                tail,
+                axes,
+                [
+                    (flat(s, v), flat((s + k) % src_count, v + 1))
+                    for s in range(src_count)
+                    for v in range(vol_count - 1)
+                ],
+            )
+        )
+        from_right.append(
+            lax.ppermute(
+                head,
+                axes,
+                [
+                    (flat(s, v + 1), flat((s + k) % src_count, v))
+                    for s in range(src_count)
+                    for v in range(vol_count - 1)
+                ],
+            )
+        )
+    summed = canonical_sum(centre, me, src_count)
+    left = canonical_sum(from_left, me, src_count)
+    right = canonical_sum(from_right, me, src_count)
+    return jnp.concatenate([left, summed, right], axis=1)
 
 
 def local(forward, item_tx, item_brick, tx_place, brick_place, adjoint):
@@ -208,8 +236,7 @@
         .transpose(2, 3, 0, 4, 1, 5)
         .reshape(2, E, NBY * E, NBZ * E)
     )
-    summed = src_sum(slab)
-    padded = with_halo(summed, (("vol", 1),), 4)
+    padded = summed_with_halo(slab, 4)
     field = smooth_axis(padded, 1)
     for axis in (2, 3):
         field = smooth_axis(pad_axis(field, axis), axis)

time: 197 us -> 218 us (1.11)
  starting transfers between devices: 30.7 us -> 50.7 us
    ppermute x5 -> x11, starting transfers between devices: 19.9 us -> 39.9 us  [the longest x4 20.6 us: summed_with_halo(): lax.ppermute(tail, axes, [(flat(s, v), flat((s + k) % src_count, v + 1))...]
    ppermute x5 -> x11, waiting for transfers between devices: 6.59 us -> 7 us  [the longest x3 5.78 us: summed_with_halo(): lax.ppermute(part, axes, [(flat(s, v), flat((s + k) % src_count, v)) for...]
  transfers between devices with their start and end apart: 6 -> 12, of which waited for: 3 -> 5; matrix products, arithmetic and copies ran while one was open for 9% -> 8% of each run, Pallas kernels for 0% -> 0%
where the time goes in v2:
time: 218 us; the launch traced here: 216 us
  waiting for transfers between devices  106 us (49%)
  starting transfers between devices  50.7 us (23%)
  local copies, waits for them, and re-layouts  40.4 us (19%)
  Pallas kernels  15.1 us (7%)
  other arithmetic  3.54 us (2%)
    all_to_all x1, waiting for transfers between devices, local(): lax.all_to_all(payload, ('src', 'vol'), split_axis=0, concat_axis=0, tile...  99 us
    ppermute x4, starting transfers between devices, summed_with_halo(): lax.ppermute(tail, axes, [(flat(s, v), flat((s + k) % src_count, v + 1))...  20.6 us
    unnamed x6, local copies, waits for them, and re-layouts  18.6 us
    ppermute x4, starting transfers between devices, summed_with_halo(): lax.ppermute(head, axes, [(flat(s, v + 1), flat((s + k) % src_count, v))...  16 us
    all_to_all x1, starting transfers between devices, local(): lax.all_to_all(payload, ('src', 'vol'), split_axis=0, concat_axis=0, tile...  10.8 us
    pallas_call x1, Pallas kernels, local(): pl.pallas_call(correlate_kernel, out_shape=jax.ShapeDtypeStruct((local_br...  8.94 us
    reshape x1, local copies, waits for them, and re-layouts, local(): adj_rows = adjoint.reshape(local_tx, local_bricks, rows, LANES)  8.7 us
    reshape x1, local copies, waits for them, and re-layouts, local(): fwd_rows = forward.reshape(stored, rows, LANES)  6.97 us
  transfers between devices with their start and end apart: 12, of which 5 were waited for; matrix products, arithmetic and copies ran while one was open for 8% of the time, Pallas kernels for 0%

profile of v2, /device:TPU:57, one launch (start us, length us, event | category | flops | bytes accessed | tf_op | source)
XLA Modules:
  0.0 216.0 jit_solution(13350250990674885709)
XLA Ops:
  0.0 0.9 select_reduce_fusion
  0.9 0.8 select_reduce_fusion.3
  2.1 6.6 %copy.18 = bf16[128,36,512]{0,2,1:T(8,128)(2,1)} copy(bf16[128,36,512]{2,0,1:T(8,128)(2,1)} %param.6) | data formatting | bytes 9437184 | tf_op args[0]
  8.8 7.0 %copy.19.fwd_ref = bf16[128,144,128]{2,1,0:T(8,128)(2,1)} copy(bf16[128,144,128]{0,2,1:T(8,128)(2,1)} %bitcast.29) | data formatting | bytes 9437184 | tf_op jit(solution)/shard_map/reshape | solution.py:195
  15.7 2.3 %copy-done.1 = bf16[128,144,128]{2,1,0:T(8,128)(2,1)S(1)} copy-done((bf16[128,144,128]{2,1,0:T(8,128)(2,1)S(1)}, bf16[128,144,128]{2,1,0:T(8,128)(2,1)}, u32[]{:S(2)}) %copy-start.1) | copy-done | bytes 4718616
  18.1 6.1 %shard_map.64 = bf16[128,304,128]{2,1,0:T(8,128)(2,1)} custom-call(s32[256]{0:T(256)S(1)} %get-tuple-element.14.src_ref, s32[256]{0:T(256)S(1)} %get-tuple-element.13.pair_ref, bf16[128,144,128]{2,1,0:T(8,128)(2,1)S(1)} %copy-done.1), custom_call_target="tpu_custom_call" | custom-call | tf_op jit(solution)/shard_map/pallas_call | solution.py:199
  24.2 10.8 %all-to-all-start = ((bf16[128,304,128]{2,1,0:T(8,128)(2,1)}), bf16[128,304,128]{2,1,0:T(8,128)(2,1)}, u32[]{:S(2)}, u32[]{:S(2)}) async-start(bf16[128,304,128]{2,1,0:T(8,128)(2,1)} %shard_map.64), calls=%async_computation | async-start | bytes 19922944 | tf_op jit(solution)/shard_map/all_to_all | solution.py:211
  35.0 7.4 %copy.21 = bf16[4,32,36,512]{3,2,1,0:T(8,128)(2,1)} copy(bf16[4,32,36,512]{3,1,2,0:T(8,128)(2,1)} %param.11) | data formatting | bytes 9437184 | tf_op args[5]
  42.4 8.7 %reshape.134.adj_ref = bf16[4,32,144,128]{3,2,1,0:T(8,128)(2,1)} reshape(bf16[4,32,36,512]{3,2,1,0:T(8,128)(2,1)} %copy.21) | data formatting | bytes 9437184 | tf_op jit(solution)/shard_map/reshape | solution.py:217
  51.1 99.0 %all-to-all-done.arrived_ref = bf16[128,304,128]{2,1,0:T(8,128)(2,1)} async-done(((bf16[128,304,128]{2,1,0:T(8,128)(2,1)}), bf16[128,304,128]{2,1,0:T(8,128)(2,1)}, u32[]{:S(2)}, u32[]{:S(2)}) %all-to-all-start) | async-done | bytes 9961504 | tf_op jit(solution)/shard_map/all_to_all | solution.py:211
  150.0 2.1 slice_reduce_fusion.1
  152.4 2.3 %copy-done = bf16[4,32,144,128]{3,2,1,0:T(8,128)(2,1)S(1)} copy-done((bf16[4,32,144,128]{3,2,1,0:T(8,128)(2,1)S(1)}, bf16[4,32,144,128]{3,2,1,0:T(8,128)(2,1)}, u32[]{:S(2)}) %copy-start) | copy-done | bytes 4718616
  154.7 8.9 %shard_map.65 = f32[32,2,8,128]{3,2,1,0:T(8,128)S(1)} custom-call(s32[256]{0:T(256)S(1)} %convert_element_type.19.pair_ref, bf16[128,304,128]{2,1,0:T(8,128)(2,1)} %all-to-all-done.arrived_ref, bf16[4,32,144,128]{3,2,1,0:T(8,128)(2,1)S(1)} %copy-done), custom_call_target="tpu_custom_call" | custom-call | tf_op jit(solution)/shard_map/pallas_call | solution.py:218
  163.9 0.6 reshape_reshape.3
  164.5 0.9 copy.23
  165.4 1.0 reshape.135
  166.4 9.4 %collective-permute-start = (f32[2,4,16,128]{3,2,1,0:T(8,128)S(1)}, f32[2,4,16,128]{3,2,1,0:T(8,128)S(1)}, u32[]{:S(2)}, u32[]{:S(2)}) collective-permute-start(f32[2,4,16,128]{3,2,1,0:T(8,128)S(1)} %get-tuple-element.9), channel_id=1, source_target_pairs={{0,1},{1,2},{2,3},{3,4},{4,5},{5,6},{6,7},{7,8},{8,9},{9,10},{10,1... | collective-permute-start | bytes 196616 | tf_op jit(solution)/shard_map/ppermute | solution.py:138
  175.8 5.9 %collective-permute-start.1 = (f32[2,4,16,128]{3,2,1,0:T(8,128)S(1)}, f32[2,4,16,128]{3,2,1,0:T(8,128)S(1)}, u32[]{:S(2)}, u32[]{:S(2)}) collective-permute-start(f32[2,4,16,128]{3,2,1,0:T(8,128)S(1)} %get-tuple-element.9), channel_id=1, source_target_pairs={{0,33},{1,34},{2,35},{3,36},{4,37},{5,38},{6,39},{7,40},{8,41},{9,... | collective-permute-start | bytes 196616 | tf_op jit(solution)/shard_map/ppermute | solution.py:138
  181.7 1.9 collective-permute-start.2
  183.6 3.5 %collective-permute-start.3 = (f32[2,4,16,128]{3,2,1,0:T(8,128)S(1)}, f32[2,4,16,128]{3,2,1,0:T(8,128)S(1)}, u32[]{:S(2)}, u32[]{:S(2)}) collective-permute-start(f32[2,4,16,128]{3,2,1,0:T(8,128)S(1)} %get-tuple-element.9), channel_id=1, source_target_pairs={{0,97},{1,98},{2,99},{3,100},{4,101},{5,102},{6,103},{7,104},{8,10... | collective-permute-start | bytes 196616 | tf_op jit(solution)/shard_map/ppermute | solution.py:138
  187.2 1.0 stack_reshape.3
  188.2 2.5 %collective-permute-start.7 = (f32[2,4,16,128]{3,2,1,0:T(8,128)S(1)}, f32[2,4,16,128]{3,2,1,0:T(8,128)S(1)}, u32[]{:S(2)}, u32[]{:S(2)}) collective-permute-start(f32[2,4,16,128]{3,2,1,0:T(8,128)S(1)} %get-tuple-element.10), channel_id=1, source_target_pairs={{1,0},{2,1},{3,2},{4,3},{5,4},{6,5},{7,6},{8,7},{9,8},{10,9},{11,1... | collective-permute-start | bytes 196616 | tf_op jit(solution)/shard_map/ppermute | solution.py:149
  190.8 5.3 %collective-permute-start.8 = (f32[2,4,16,128]{3,2,1,0:T(8,128)S(1)}, f32[2,4,16,128]{3,2,1,0:T(8,128)S(1)}, u32[]{:S(2)}, u32[]{:S(2)}) collective-permute-start(f32[2,4,16,128]{3,2,1,0:T(8,128)S(1)} %get-tuple-element.10), channel_id=1, source_target_pairs={{1,32},{2,33},{3,34},{4,35},{5,36},{6,37},{7,38},{8,39},{9,40},{10... | collective-permute-start | bytes 196616 | tf_op jit(solution)/shard_map/ppermute | solution.py:149
  196.1 6.2 %collective-permute-start.9 = (f32[2,4,16,128]{3,2,1,0:T(8,128)S(1)}, f32[2,4,16,128]{3,2,1,0:T(8,128)S(1)}, u32[]{:S(2)}, u32[]{:S(2)}) collective-permute-start(f32[2,4,16,128]{3,2,1,0:T(8,128)S(1)} %get-tuple-element.10), channel_id=1, source_target_pairs={{1,64},{2,65},{3,66},{4,67},{5,68},{6,69},{7,70},{8,71},{9,72},{10... | collective-permute-start | bytes 196616 | tf_op jit(solution)/shard_map/ppermute | solution.py:149
  202.3 1.9 collective-permute-start.10
  204.2 1.4 collective-permute-start.4
  205.7 1.4 collective-permute-start.5
  207.6 1.2 collective-permute-done.10
  208.9 0.6 collective-permute-done.4
  209.4 3.0 %collective-permute-done.5 = f32[2,8,16,128]{3,2,1,0:T(8,128)S(1)} collective-permute-done((f32[2,8,16,128]{3,2,1,0:T(8,128)S(1)}, f32[2,8,16,128]{3,2,1,0:T(8,128)S(1)}, u32[]{:S(2)}, u32[]{:S(2)}) %collective-permute-start.5) | collective-permute-done | bytes 131104 | tf_op jit(solution)/shard_map/ppermute | solution.py:131
  212.5 2.2 %collective-permute-done.6 = f32[2,8,16,128]{3,2,1,0:T(8,128)S(1)} collective-permute-done((f32[2,8,16,128]{3,2,1,0:T(8,128)S(1)}, f32[2,8,16,128]{3,2,1,0:T(8,128)S(1)}, u32[]{:S(2)}, u32[]{:S(2)}) %collective-permute-start.6) | collective-permute-done | bytes 131104 | tf_op jit(solution)/shard_map/ppermute | solution.py:131
  215.0 1.0 fusion.44
  (29 shorter events, 1.9 us)
Async XLA Ops:
  15.7 2.3 %copy-start.1 = (bf16[128,144,128]{2,1,0:T(8,128)(2,1)S(1)}, bf16[128,144,128]{2,1,0:T(8,128)(2,1)}, u32[]{:S(2)}) copy-start(bf16[128,144,128]{2,1,0:T(8,128)(2,1)} %copy.19.fwd_ref) | copy-start | bytes 14155780
  24.2 125.8 %all-to-all-start = ((bf16[128,304,128]{2,1,0:T(8,128)(2,1)}), bf16[128,304,128]{2,1,0:T(8,128)(2,1)}, u32[]{:S(2)}, u32[]{:S(2)}) async-start(bf16[128,304,128]{2,1,0:T(8,128)(2,1)} %shard_map.64), calls=%async_computation | async-start | bytes 19922944 | tf_op jit(solution)/shard_map/all_to_all | solution.py:211
  152.4 2.3 %copy-start = (bf16[4,32,144,128]{3,2,1,0:T(8,128)(2,1)S(1)}, bf16[4,32,144,128]{3,2,1,0:T(8,128)(2,1)}, u32[]{:S(2)}) copy-start(bf16[4,32,144,128]{3,2,1,0:T(8,128)(2,1)} %reshape.134.adj_ref) | copy-start | bytes 14155780
  166.4 24.3 %collective-permute-start = (f32[2,4,16,128]{3,2,1,0:T(8,128)S(1)}, f32[2,4,16,128]{3,2,1,0:T(8,128)S(1)}, u32[]{:S(2)}, u32[]{:S(2)}) collective-permute-start(f32[2,4,16,128]{3,2,1,0:T(8,128)S(1)} %get-tuple-element.9), channel_id=1, source_target_pairs={{0,1},{1,2},{2,3},{3,4},{4,5},{5,6},{6,7},{7,8},{8,9},{9,10},{10,1... | collective-permute-start | bytes 196616 | tf_op jit(solution)/shard_map/ppermute | solution.py:138
  175.8 20.3 %collective-permute-start.1 = (f32[2,4,16,128]{3,2,1,0:T(8,128)S(1)}, f32[2,4,16,128]{3,2,1,0:T(8,128)S(1)}, u32[]{:S(2)}, u32[]{:S(2)}) collective-permute-start(f32[2,4,16,128]{3,2,1,0:T(8,128)S(1)} %get-tuple-element.9), channel_id=1, source_target_pairs={{0,33},{1,34},{2,35},{3,36},{4,37},{5,38},{6,39},{7,40},{8,41},{9,... | collective-permute-start | bytes 196616 | tf_op jit(solution)/shard_map/ppermute | solution.py:138
  181.7 20.6 %collective-permute-start.2 = (f32[2,4,16,128]{3,2,1,0:T(8,128)S(1)}, f32[2,4,16,128]{3,2,1,0:T(8,128)S(1)}, u32[]{:S(2)}, u32[]{:S(2)}) collective-permute-start(f32[2,4,16,128]{3,2,1,0:T(8,128)S(1)} %get-tuple-element.9), channel_id=1, source_target_pairs={{0,65},{1,66},{2,67},{3,68},{4,69},{5,70},{6,71},{7,72},{8,73},{9,... | collective-permute-start | bytes 196616 | tf_op jit(solution)/shard_map/ppermute | solution.py:138
  183.6 20.6 %collective-permute-start.3 = (f32[2,4,16,128]{3,2,1,0:T(8,128)S(1)}, f32[2,4,16,128]{3,2,1,0:T(8,128)S(1)}, u32[]{:S(2)}, u32[]{:S(2)}) collective-permute-start(f32[2,4,16,128]{3,2,1,0:T(8,128)S(1)} %get-tuple-element.9), channel_id=1, source_target_pairs={{0,97},{1,98},{2,99},{3,100},{4,101},{5,102},{6,103},{7,104},{8,10... | collective-permute-start | bytes 196616 | tf_op jit(solution)/shard_map/ppermute | solution.py:138
  188.2 17.5 %collective-permute-start.7 = (f32[2,4,16,128]{3,2,1,0:T(8,128)S(1)}, f32[2,4,16,128]{3,2,1,0:T(8,128)S(1)}, u32[]{:S(2)}, u32[]{:S(2)}) collective-permute-start(f32[2,4,16,128]{3,2,1,0:T(8,128)S(1)} %get-tuple-element.10), channel_id=1, source_target_pairs={{1,0},{2,1},{3,2},{4,3},{5,4},{6,5},{7,6},{8,7},{9,8},{10,9},{11,1... | collective-permute-start | bytes 196616 | tf_op jit(solution)/shard_map/ppermute | solution.py:149
  190.8 16.3 %collective-permute-start.8 = (f32[2,4,16,128]{3,2,1,0:T(8,128)S(1)}, f32[2,4,16,128]{3,2,1,0:T(8,128)S(1)}, u32[]{:S(2)}, u32[]{:S(2)}) collective-permute-start(f32[2,4,16,128]{3,2,1,0:T(8,128)S(1)} %get-tuple-element.10), channel_id=1, source_target_pairs={{1,32},{2,33},{3,34},{4,35},{5,36},{6,37},{7,38},{8,39},{9,40},{10... | collective-permute-start | bytes 196616 | tf_op jit(solution)/shard_map/ppermute | solution.py:149
  196.1 11.5 %collective-permute-start.9 = (f32[2,4,16,128]{3,2,1,0:T(8,128)S(1)}, f32[2,4,16,128]{3,2,1,0:T(8,128)S(1)}, u32[]{:S(2)}, u32[]{:S(2)}) collective-permute-start(f32[2,4,16,128]{3,2,1,0:T(8,128)S(1)} %get-tuple-element.10), channel_id=1, source_target_pairs={{1,64},{2,65},{3,66},{4,67},{5,68},{6,69},{7,70},{8,71},{9,72},{10... | collective-permute-start | bytes 196616 | tf_op jit(solution)/shard_map/ppermute | solution.py:149
  202.3 6.5 %collective-permute-start.10 = (f32[2,4,16,128]{3,2,1,0:T(8,128)S(1)}, f32[2,4,16,128]{3,2,1,0:T(8,128)S(1)}, u32[]{:S(2)}, u32[]{:S(2)}) collective-permute-start(f32[2,4,16,128]{3,2,1,0:T(8,128)S(1)} %get-tuple-element.10), channel_id=1, source_target_pairs={{1,96},{2,97},{3,98},{4,99},{5,100},{6,101},{7,102},{8,103},{9,104... | collective-permute-start | bytes 196616 | tf_op jit(solution)/shard_map/ppermute | solution.py:149
  204.2 5.2 %collective-permute-start.4 = (f32[2,8,16,128]{3,2,1,0:T(8,128)S(1)}, f32[2,8,16,128]{3,2,1,0:T(8,128)S(1)}, u32[]{:S(2)}, u32[]{:S(2)}) collective-permute-start(f32[2,8,16,128]{3,2,1,0:T(8,128)S(1)} %reshape.135), channel_id=1, source_target_pairs={{0,32},{1,33},{2,34},{3,35},{4,36},{5,37},{6,38},{7,39},{8,40},{9,... | collective-permute-start | bytes 393224 | tf_op jit(solution)/shard_map/ppermute | solution.py:131
  205.7 6.8 %collective-permute-start.5 = (f32[2,8,16,128]{3,2,1,0:T(8,128)S(1)}, f32[2,8,16,128]{3,2,1,0:T(8,128)S(1)}, u32[]{:S(2)}, u32[]{:S(2)}) collective-permute-start(f32[2,8,16,128]{3,2,1,0:T(8,128)S(1)} %reshape.135), channel_id=1, source_target_pairs={{0,64},{1,65},{2,66},{3,67},{4,68},{5,69},{6,70},{7,71},{8,72},{9,... | collective-permute-start | bytes 393224 | tf_op jit(solution)/shard_map/ppermute | solution.py:131
  207.1 7.5 %collective-permute-start.6 = (f32[2,8,16,128]{3,2,1,0:T(8,128)S(1)}, f32[2,8,16,128]{3,2,1,0:T(8,128)S(1)}, u32[]{:S(2)}, u32[]{:S(2)}) collective-permute-start(f32[2,8,16,128]{3,2,1,0:T(8,128)S(1)} %reshape.135), channel_id=1, source_target_pairs={{0,96},{1,97},{2,98},{3,99},{4,100},{5,101},{6,102},{7,103},{8,104... | collective-permute-start | bytes 393224 | tf_op jit(solution)/shard_map/ppermute | solution.py:131

commit v3 on v1

--- a/solution.py
+++ b/solution.py
@@ -164,7 +164,9 @@
         filled, jnp.sum(jnp.where(slot_hits, pair_index[None, :], 0), axis=1), -1
     ).astype(jnp.int32)
 
-    fwd_rows = forward.reshape(stored, rows, LANES)
+    fwd_rows = jnp.transpose(
+        jnp.transpose(forward, (1, 0, 2)).reshape(channels, stored, cells // LANES, LANES), (1, 0, 2, 3)
+    ).reshape(stored, rows, LANES)
     chunk = 2 * rows + META
     pack_steps = 8
     dests_per_step = devices // pack_steps
@@ -186,7 +188,10 @@
     ).reshape(slot_total)
     arrived_pairs = tags.astype(jnp.float32).astype(jnp.int32)
 
-    adj_rows = adjoint.reshape(local_tx, local_bricks, rows, LANES)
+    adj_rows = jnp.transpose(
+        jnp.transpose(adjoint, (0, 2, 1, 3)).reshape(local_tx, channels, local_bricks, cells // LANES, LANES),
+        (0, 2, 1, 3, 4),
+    ).reshape(local_tx, local_bricks, rows, LANES)
     acc = pl.pallas_call(
         correlate_kernel,
         out_shape=jax.ShapeDtypeStruct((local_bricks, 2, 8, LANES), jnp.float32),

time: 197 us -> 193 us (0.980)
  local copies, waits for them, and re-layouts: 40.4 us -> 33.9 us
  waiting for transfers between devices: 106 us -> 108 us
    unnamed x6 -> x2, local copies, waits for them, and re-layouts: 18.6 us -> 2.33 us
    reshape x2 -> x4, local copies, waits for them, and re-layouts: 15.7 us -> 25.5 us  [the longest x2 13.8 us: local(): jnp.transpose(adjoint, (0, 2, 1, 3))]
    all_to_all x1, waiting for transfers between devices: 99 us -> 101 us  [local(): lax.all_to_all(payload, ('src', 'vol'), split_axis=0, concat_axis=0, tile...]
  transfers between devices with their start and end apart: 6 -> 6, of which waited for: 3 -> 4; matrix products, arithmetic and copies ran while one was open for 9% -> 8% of each run, Pallas kernels for 0% -> 0%
where the time goes in v3:
time: 193 us; the launch traced here: 191 us
  waiting for transfers between devices  108 us (56%)
  local copies, waits for them, and re-layouts  33.9 us (18%)
  starting transfers between devices  29.9 us (15%)
  Pallas kernels  15.3 us (8%)
  other arithmetic  3.46 us (2%)
    all_to_all x1, waiting for transfers between devices, local(): lax.all_to_all(payload, ('src', 'vol'), split_axis=0, concat_axis=0, tile...  101 us
    reshape x2, local copies, waits for them, and re-layouts, local(): jnp.transpose(adjoint, (0, 2, 1, 3))  13.8 us
    reshape x2, local copies, waits for them, and re-layouts, local(): jnp.transpose(forward, (1, 0, 2))  11.7 us
    all_to_all x1, starting transfers between devices, local(): lax.all_to_all(payload, ('src', 'vol'), split_axis=0, concat_axis=0, tile...  10.8 us
    pallas_call x1, Pallas kernels, local(): pl.pallas_call(correlate_kernel, out_shape=jax.ShapeDtypeStruct((local_br...  9.2 us
    ppermute x1, starting transfers between devices, with_halo(): lax.ppermute(tail, axis, [(i, (i + 1) % count) for i in range(ends)])  9.1 us
    ppermute x3, starting transfers between devices, src_sum(): lax.ppermute(part, 'src', [(i, (i + k) % count) for i in range(count)])  8.04 us
    pallas_call x1, Pallas kernels, local(): pl.pallas_call(pack_kernel, out_shape=jax.ShapeDtypeStruct((devices, chun...  6.13 us
  transfers between devices with their start and end apart: 6, of which 4 were waited for; matrix products, arithmetic and copies ran while one was open for 8% of the time, Pallas kernels for 0%

profile of v3, /device:TPU:57, one launch (start us, length us, event | category | flops | bytes accessed | tf_op | source)
XLA Modules:
  0.0 191.1 jit_solution(15096935243181665280)
XLA Ops:
  0.0 0.9 select_reduce_fusion
  0.9 0.8 select_reduce_fusion.3
  1.7 0.2 convert_reduce_fusion
  1.9 0.1 fusion.54
  2.0 0.2 select_reduce_fusion.1
  2.1 7.7 %reshape.133 = bf16[36,128,4,128]{3,2,1,0:T(4,128)(2,1)} reshape(bf16[36,128,512]{2,1,0:T(8,128)(2,1)} %bitcast.28) | data formatting | bytes 9437184 | tf_op jit(solution)/shard_map/reshape | solution.py:168
  9.8 4.0 %copy.17 = bf16[36,128,4,128]{3,2,0,1:T(4,128)(2,1)S(1)} copy(bf16[36,128,4,128]{3,2,1,0:T(4,128)(2,1)} %reshape.133) | data formatting | bytes 9437184 | tf_op jit(solution)/shard_map/reshape | solution.py:168
  13.8 6.1 %shard_map.64 = bf16[128,304,128]{2,1,0:T(8,128)(2,1)} custom-call(s32[256]{0:T(256)S(1)} %get-tuple-element.14.src_ref, s32[256]{0:T(256)S(1)} %get-tuple-element.13.pair_ref, bf16[128,144,128]{2,1,0:T(8,128)(2,1)S(1)} %bitcast.27), custom_call_target="tpu_custom_call" | custom-call | tf_op jit(solution)/shard_map/pallas_call | solution.py:173
  19.9 10.8 %all-to-all-start = ((bf16[128,304,128]{2,1,0:T(8,128)(2,1)}), bf16[128,304,128]{2,1,0:T(8,128)(2,1)}, u32[]{:S(2)}, u32[]{:S(2)}) async-start(bf16[128,304,128]{2,1,0:T(8,128)(2,1)} %shard_map.64), calls=%async_computation | async-start | bytes 19922944 | tf_op jit(solution)/shard_map/all_to_all | solution.py:185
  30.8 7.7 %reshape.135 = bf16[4,36,32,4,128]{4,3,2,1,0:T(4,128)(2,1)} reshape(bf16[4,36,32,512]{3,2,1,0:T(8,128)(2,1)} %bitcast.29) | data formatting | bytes 9437184 | tf_op jit(solution)/shard_map/reshape | solution.py:192
  38.5 6.1 %copy.19 = bf16[4,36,32,4,128]{4,3,1,2,0:T(4,128)(2,1)} copy(bf16[4,36,32,4,128]{4,3,2,1,0:T(4,128)(2,1)} %reshape.135) | data formatting | bytes 9437184 | tf_op jit(solution)/shard_map/reshape | solution.py:192
  44.6 101.2 %all-to-all-done.arrived_ref = bf16[128,304,128]{2,1,0:T(8,128)(2,1)} async-done(((bf16[128,304,128]{2,1,0:T(8,128)(2,1)}), bf16[128,304,128]{2,1,0:T(8,128)(2,1)}, u32[]{:S(2)}, u32[]{:S(2)}) %all-to-all-start) | async-done | bytes 9961504 | tf_op jit(solution)/shard_map/all_to_all | solution.py:185
  145.8 2.1 %slice_reduce_fusion.1 = (bf16[128]{0:T(256)(128)(2,1)S(1)}, bf16[128]{0:T(256)(128)(2,1)S(1)}) fusion(bf16[128,304,128]{2,1,0:T(8,128)(2,1)} %all-to-all-done.arrived_ref), kind=kLoop, calls=%fused_computation.94 | loop fusion | bytes 1024 | tf_op jit(solution)/shard_map/slice | solution.py:187
  147.9 0.1 copy.18
  148.0 0.1 convert_element_type.19.pair_ref
  148.1 2.3 %copy-done = bf16[4,36,32,4,128]{4,3,1,2,0:T(4,128)(2,1)S(1)} copy-done((bf16[4,36,32,4,128]{4,3,1,2,0:T(4,128)(2,1)S(1)}, bf16[4,36,32,4,128]{4,3,1,2,0:T(4,128)(2,1)}, u32[]{:S(2)}) %copy-start) | copy-done | bytes 4718616
  150.5 9.2 %shard_map.65 = f32[32,2,8,128]{3,2,1,0:T(8,128)S(1)} custom-call(s32[256]{0:T(256)S(1)} %convert_element_type.19.pair_ref, bf16[128,304,128]{2,1,0:T(8,128)(2,1)} %all-to-all-done.arrived_ref, bf16[4,32,144,128]{3,2,1,0:T(8,128)(2,1)S(1)} %bitcast.26), custom_call_target="tpu_custom_call" | custom-call | tf_op jit(solution)/shard_map/pallas_call | solution.py:195
  159.7 0.2 copy.20
  159.9 0.6 reshape_reshape.3
  160.5 0.9 copy.21
  161.4 1.0 reshape.137
  162.4 0.3 collective-permute-start
  162.8 5.7 %collective-permute-start.1 = (f32[2,8,16,128]{3,2,1,0:T(8,128)S(1)}, f32[2,8,16,128]{3,2,1,0:T(8,128)S(1)}, u32[]{:S(2)}, u32[]{:S(2)}) collective-permute-start(f32[2,8,16,128]{3,2,1,0:T(8,128)S(1)} %reshape.137), channel_id=1, source_target_pairs={{0,64},{32,96},{64,0},{96,32},{1,65},{33,97},{65,1},{97,33},{2,66}... | collective-permute-start | bytes 393224 | tf_op jit(solution)/shard_map/ppermute | solution.py:127
  168.5 2.0 %collective-permute-start.2 = (f32[2,8,16,128]{3,2,1,0:T(8,128)S(1)}, f32[2,8,16,128]{3,2,1,0:T(8,128)S(1)}, u32[]{:S(2)}, u32[]{:S(2)}) collective-permute-start(f32[2,8,16,128]{3,2,1,0:T(8,128)S(1)} %reshape.137), channel_id=1, source_target_pairs={{0,96},{32,0},{64,32},{96,64},{1,97},{33,1},{65,33},{97,65},{2,98}... | collective-permute-start | bytes 393224 | tf_op jit(solution)/shard_map/ppermute | solution.py:127
  170.5 1.0 stack_reshape.3
  171.5 0.4 collective-permute-done.1
  171.9 3.2 %collective-permute-done.2 = f32[2,8,16,128]{3,2,1,0:T(8,128)S(1)} collective-permute-done((f32[2,8,16,128]{3,2,1,0:T(8,128)S(1)}, f32[2,8,16,128]{3,2,1,0:T(8,128)S(1)}, u32[]{:S(2)}, u32[]{:S(2)}) %collective-permute-start.2) | collective-permute-done | bytes 131104 | tf_op jit(solution)/shard_map/ppermute | solution.py:127
  175.2 9.1 %collective-permute-start.3 = (f32[2,4,16,128]{3,2,1,0:T(8,128)S(1)}, f32[2,4,16,128]{3,2,1,0:T(8,128)S(1)}, u32[]{:S(2)}, u32[]{:S(2)}) collective-permute-start(f32[2,4,16,128]{3,2,1,0:T(8,128)S(1)} %get-tuple-element.9), channel_id=1, source_target_pairs={{0,1},{1,2},{2,3},{3,4},{4,5},{5,6},{6,7},{7,8},{8,9},{9,10},{10,1... | collective-permute-start | bytes 196616 | tf_op jit(solution)/shard_map/ppermute | solution.py:26
  184.3 1.9 %collective-permute-start.4 = (f32[2,4,16,128]{3,2,1,0:T(8,128)S(1)}, f32[2,4,16,128]{3,2,1,0:T(8,128)S(1)}, u32[]{:S(2)}, u32[]{:S(2)}) collective-permute-start(f32[2,4,16,128]{3,2,1,0:T(8,128)S(1)} %get-tuple-element.10), channel_id=1, source_target_pairs={{1,0},{2,1},{3,2},{4,3},{5,4},{6,5},{7,6},{8,7},{9,8},{10,9},{11,1... | collective-permute-start | bytes 196616 | tf_op jit(solution)/shard_map/ppermute | solution.py:28
  186.3 3.6 %collective-permute-done.4 = f32[2,4,16,128]{3,2,1,0:T(8,128)S(1)} collective-permute-done((f32[2,4,16,128]{3,2,1,0:T(8,128)S(1)}, f32[2,4,16,128]{3,2,1,0:T(8,128)S(1)}, u32[]{:S(2)}, u32[]{:S(2)}) %collective-permute-start.4) | collective-permute-done | bytes 65568 | tf_op jit(solution)/shard_map/ppermute | solution.py:28
  190.0 0.1 fusion.28
  190.1 1.0 fusion.44
  (12 shorter events, 0.2 us)
Async XLA Ops:
  19.9 125.8 %all-to-all-start = ((bf16[128,304,128]{2,1,0:T(8,128)(2,1)}), bf16[128,304,128]{2,1,0:T(8,128)(2,1)}, u32[]{:S(2)}, u32[]{:S(2)}) async-start(bf16[128,304,128]{2,1,0:T(8,128)(2,1)} %shard_map.64), calls=%async_computation | async-start | bytes 19922944 | tf_op jit(solution)/shard_map/all_to_all | solution.py:185
  148.1 2.3 %copy-start = (bf16[4,36,32,4,128]{4,3,1,2,0:T(4,128)(2,1)S(1)}, bf16[4,36,32,4,128]{4,3,1,2,0:T(4,128)(2,1)}, u32[]{:S(2)}) copy-start(bf16[4,36,32,4,128]{4,3,1,2,0:T(4,128)(2,1)} %copy.19) | copy-start | bytes 14155780
  162.4 9.1 %collective-permute-start = (f32[2,8,16,128]{3,2,1,0:T(8,128)S(1)}, f32[2,8,16,128]{3,2,1,0:T(8,128)S(1)}, u32[]{:S(2)}, u32[]{:S(2)}) collective-permute-start(f32[2,8,16,128]{3,2,1,0:T(8,128)S(1)} %reshape.137), channel_id=1, source_target_pairs={{0,32},{32,64},{64,96},{96,0},{1,33},{33,65},{65,97},{97,1},{2,34}... | collective-permute-start | bytes 393224 | tf_op jit(solution)/shard_map/ppermute | solution.py:127
  162.8 9.2 %collective-permute-start.1 = (f32[2,8,16,128]{3,2,1,0:T(8,128)S(1)}, f32[2,8,16,128]{3,2,1,0:T(8,128)S(1)}, u32[]{:S(2)}, u32[]{:S(2)}) collective-permute-start(f32[2,8,16,128]{3,2,1,0:T(8,128)S(1)} %reshape.137), channel_id=1, source_target_pairs={{0,64},{32,96},{64,0},{96,32},{1,65},{33,97},{65,1},{97,33},{2,66}... | collective-permute-start | bytes 393224 | tf_op jit(solution)/shard_map/ppermute | solution.py:127
  168.5 6.6 %collective-permute-start.2 = (f32[2,8,16,128]{3,2,1,0:T(8,128)S(1)}, f32[2,8,16,128]{3,2,1,0:T(8,128)S(1)}, u32[]{:S(2)}, u32[]{:S(2)}) collective-permute-start(f32[2,8,16,128]{3,2,1,0:T(8,128)S(1)} %reshape.137), channel_id=1, source_target_pairs={{0,96},{32,0},{64,32},{96,64},{1,97},{33,1},{65,33},{97,65},{2,98}... | collective-permute-start | bytes 393224 | tf_op jit(solution)/shard_map/ppermute | solution.py:127
  175.2 11.0 %collective-permute-start.3 = (f32[2,4,16,128]{3,2,1,0:T(8,128)S(1)}, f32[2,4,16,128]{3,2,1,0:T(8,128)S(1)}, u32[]{:S(2)}, u32[]{:S(2)}) collective-permute-start(f32[2,4,16,128]{3,2,1,0:T(8,128)S(1)} %get-tuple-element.9), channel_id=1, source_target_pairs={{0,1},{1,2},{2,3},{3,4},{4,5},{5,6},{6,7},{7,8},{8,9},{9,10},{10,1... | collective-permute-start | bytes 196616 | tf_op jit(solution)/shard_map/ppermute | solution.py:26
  184.3 5.6 %collective-permute-start.4 = (f32[2,4,16,128]{3,2,1,0:T(8,128)S(1)}, f32[2,4,16,128]{3,2,1,0:T(8,128)S(1)}, u32[]{:S(2)}, u32[]{:S(2)}) collective-permute-start(f32[2,4,16,128]{3,2,1,0:T(8,128)S(1)} %get-tuple-element.10), channel_id=1, source_target_pairs={{1,0},{2,1},{3,2},{4,3},{5,4},{6,5},{7,6},{8,7},{9,8},{10,9},{11,1... | collective-permute-start | bytes 196616 | tf_op jit(solution)/shard_map/ppermute | solution.py:28

commit v4 on v3

--- a/solution.py
+++ b/solution.py
@@ -79,45 +79,33 @@
     lax.fori_loop(0, dests, one_dest, 0)
 
 
-def correlate_kernel(pair_ref, arrived_ref, adj_ref, acc_ref):
+def correlate_kernel(pair_ref, arrived_ref, adj_ref, out_ref):
     dests = arrived_ref.shape[0]
     rows = adj_ref.shape[2]
     bricks = adj_ref.shape[1]
     groups = rows // 8
-    step = pl.program_id(0)
-
-    @pl.when(step == 0)
-    def _():
-        acc_ref[...] = jnp.zeros(acc_ref.shape, acc_ref.dtype)
-
-    base = step * dests * 2
+    base = pl.program_id(0) * dests * 2
 
     def one_slot(d, s):
-        pair = pair_ref[base + 2 * d + s]
-
-        @pl.when(pair >= 0)
-        def _():
-            tx = pair // bricks
-            brick = pair % bricks
-            fwd = arrived_ref[d, s * rows : (s + 1) * rows, :].astype(jnp.float32)
-            adj = adj_ref[tx, brick].astype(jnp.float32)
-            prod = (fwd * adj).reshape(groups, 8, LANES)
-            horizontal = None
-            vertical = None
-            for g in range(groups):
-                if g % 3 == 2:
-                    vertical = prod[g] if vertical is None else vertical + prod[g]
-                else:
-                    horizontal = prod[g] if horizontal is None else horizontal + prod[g]
-            acc_ref[brick, 0] += horizontal
-            acc_ref[brick, 1] += vertical
-
-    def one_dest(d, carry):
+        k = 2 * d + s
+        pair = pair_ref[base + k]
+        held = jnp.maximum(pair, 0)
+        fwd = arrived_ref[d, s * rows : (s + 1) * rows, :].astype(jnp.float32)
+        adj = adj_ref[held // bricks, held % bricks].astype(jnp.float32)
+        prod = (fwd * adj).reshape(groups, 8, LANES)
+        horizontal = None
+        vertical = None
+        for g in range(groups):
+            if g % 3 == 2:
+                vertical = prod[g] if vertical is None else vertical + prod[g]
+            else:
+                horizontal = prod[g] if horizontal is None else horizontal + prod[g]
+        out_ref[k, 0] = jnp.where(pair >= 0, horizontal, 0.0)
+        out_ref[k, 1] = jnp.where(pair >= 0, vertical, 0.0)
+
+    for d in range(dests):
         one_slot(d, 0)
         one_slot(d, 1)
-        return carry
-
-    lax.fori_loop(0, dests, one_dest, 0)
 
 
 def src_sum(part):
@@ -192,9 +180,9 @@
         jnp.transpose(adjoint, (0, 2, 1, 3)).reshape(local_tx, channels, local_bricks, cells // LANES, LANES),
         (0, 2, 1, 3, 4),
     ).reshape(local_tx, local_bricks, rows, LANES)
-    acc = pl.pallas_call(
+    per_slot = pl.pallas_call(
         correlate_kernel,
-        out_shape=jax.ShapeDtypeStruct((local_bricks, 2, 8, LANES), jnp.float32),
+        out_shape=jax.ShapeDtypeStruct((slot_total, 2, 8, LANES), jnp.float32),
         grid_spec=pltpu.PrefetchScalarGridSpec(
             num_scalar_prefetch=1,
             grid=(pack_steps,),
@@ -202,12 +190,18 @@
                 pl.BlockSpec((dests_per_step, chunk, LANES), lambda g, p: (g, 0, 0)),
                 pl.BlockSpec((local_tx, local_bricks, rows, LANES), lambda g, p: (0, 0, 0, 0)),
             ],
-            out_specs=pl.BlockSpec((local_bricks, 2, 8, LANES), lambda g, p: (0, 0, 0, 0)),
+            out_specs=pl.BlockSpec((2 * dests_per_step, 2, 8, LANES), lambda g, p: (g, 0, 0, 0)),
         ),
         compiler_params=pltpu.CompilerParams(vmem_limit_bytes=48 * 1024 * 1024),
     )(arrived_pairs, arrived, adj_rows)
 
-    gradient = (acc[:, :, 0:4, :] - acc[:, :, 4:8, :]).reshape(local_bricks, 2, cells)
+    corr = (per_slot[:, :, 0:4, :] - per_slot[:, :, 4:8, :]).reshape(slot_total, 2 * cells)
+    owner_brick = jnp.maximum(arrived_pairs, 0) % local_bricks
+    owner_table = (
+        (owner_brick[None, :] == jnp.arange(local_bricks, dtype=jnp.int32)[:, None])
+        & (arrived_pairs >= 0)[None, :]
+    ).astype(jnp.float32)
+    gradient = jnp.dot(owner_table, corr, precision=lax.Precision.HIGHEST).reshape(local_bricks, 2, cells)
     slab = (
         gradient.reshape(NBY, NBZ, 2, E, E, E)
         .transpose(2, 3, 0, 4, 1, 5)

time: 193 us -> 191 us (0.990)
  local copies, waits for them, and re-layouts: 33.9 us -> 31.2 us
    unnamed x2 -> x0, local copies, waits for them, and re-layouts: 2.33 us -> none
  transfers between devices with their start and end apart: 6 -> 6, of which waited for: 4 -> 3; matrix products, arithmetic and copies ran while one was open for 8% -> 8% of each run, Pallas kernels for 0% -> 0%
where the time goes in v4:
time: 191 us; the launch traced here: 189 us
  waiting for transfers between devices  108 us (57%)
  local copies, waits for them, and re-layouts  31.2 us (16%)
  starting transfers between devices  30.4 us (16%)
  Pallas kernels  15.3 us (8%)
  other arithmetic  3.68 us (2%)
    all_to_all x1, waiting for transfers between devices, local(): lax.all_to_all(payload, ('src', 'vol'), split_axis=0, concat_axis=0, tile...  101 us
    reshape x2, local copies, waits for them, and re-layouts, local(): jnp.transpose(adjoint, (0, 2, 1, 3))  13.8 us
    reshape x2, local copies, waits for them, and re-layouts, local(): jnp.transpose(forward, (1, 0, 2))  11.7 us
    all_to_all x1, starting transfers between devices, local(): lax.all_to_all(payload, ('src', 'vol'), split_axis=0, concat_axis=0, tile...  10.8 us
    ppermute x1, starting transfers between devices, with_halo(): lax.ppermute(tail, axis, [(i, (i + 1) % count) for i in range(ends)])  9.96 us
    pallas_call x1, Pallas kernels, local(): pl.pallas_call(correlate_kernel, out_shape=jax.ShapeDtypeStruct((slot_tot...  9.16 us
    ppermute x3, starting transfers between devices, src_sum(): lax.ppermute(part, 'src', [(i, (i + k) % count) for i in range(count)])  7.72 us
    pallas_call x1, Pallas kernels, local(): pl.pallas_call(pack_kernel, out_shape=jax.ShapeDtypeStruct((devices, chun...  6.13 us
  transfers between devices with their start and end apart: 6, of which 3 were waited for; matrix products, arithmetic and copies ran while one was open for 8% of the time, Pallas kernels for 0%

profile of v4, /device:TPU:57, one launch (start us, length us, event | category | flops | bytes accessed | tf_op | source)
XLA Modules:
  0.0 189.4 jit_solution(13347822001382899269)
XLA Ops:
  0.0 0.9 select_reduce_fusion
  0.9 0.8 select_reduce_fusion.3
  1.7 0.2 convert_reduce_fusion
  1.9 0.1 fusion.54
  2.0 0.2 select_reduce_fusion.1
  2.1 7.7 %reshape.178 = bf16[36,128,4,128]{3,2,1,0:T(4,128)(2,1)} reshape(bf16[36,128,512]{2,1,0:T(8,128)(2,1)} %bitcast.35) | data formatting | bytes 9437184 | tf_op jit(solution)/shard_map/reshape | solution.py:156
  9.8 4.0 %copy.16 = bf16[36,128,4,128]{3,2,0,1:T(4,128)(2,1)S(1)} copy(bf16[36,128,4,128]{3,2,1,0:T(4,128)(2,1)} %reshape.178) | data formatting | bytes 9437184 | tf_op jit(solution)/shard_map/reshape | solution.py:156
  13.8 6.1 %shard_map.64 = bf16[128,304,128]{2,1,0:T(8,128)(2,1)} custom-call(s32[256]{0:T(256)S(1)} %get-tuple-element.14.src_ref, s32[256]{0:T(256)S(1)} %get-tuple-element.13.pair_ref, bf16[128,144,128]{2,1,0:T(8,128)(2,1)S(1)} %bitcast.33), custom_call_target="tpu_custom_call" | custom-call | tf_op jit(solution)/shard_map/pallas_call | solution.py:161
  19.9 10.8 %all-to-all-start = ((bf16[128,304,128]{2,1,0:T(8,128)(2,1)}), bf16[128,304,128]{2,1,0:T(8,128)(2,1)}, u32[]{:S(2)}, u32[]{:S(2)}) async-start(bf16[128,304,128]{2,1,0:T(8,128)(2,1)} %shard_map.64), calls=%async_computation | async-start | bytes 19922944 | tf_op jit(solution)/shard_map/all_to_all | solution.py:173
  30.8 7.7 %reshape.180 = bf16[4,36,32,4,128]{4,3,2,1,0:T(4,128)(2,1)} reshape(bf16[4,36,32,512]{3,2,1,0:T(8,128)(2,1)} %bitcast.36) | data formatting | bytes 9437184 | tf_op jit(solution)/shard_map/reshape | solution.py:180
  38.5 6.1 %copy.18 = bf16[4,36,32,4,128]{4,3,1,2,0:T(4,128)(2,1)} copy(bf16[4,36,32,4,128]{4,3,2,1,0:T(4,128)(2,1)} %reshape.180) | data formatting | bytes 9437184 | tf_op jit(solution)/shard_map/reshape | solution.py:180
  44.6 101.2 %all-to-all-done.arrived_ref = bf16[128,304,128]{2,1,0:T(8,128)(2,1)} async-done(((bf16[128,304,128]{2,1,0:T(8,128)(2,1)}), bf16[128,304,128]{2,1,0:T(8,128)(2,1)}, u32[]{:S(2)}, u32[]{:S(2)}) %all-to-all-start) | async-done | bytes 9961504 | tf_op jit(solution)/shard_map/all_to_all | solution.py:173
  145.8 2.1 %slice_reduce_fusion.1 = (bf16[128]{0:T(256)(128)(2,1)S(1)}, bf16[128]{0:T(256)(128)(2,1)S(1)}) fusion(bf16[128,304,128]{2,1,0:T(8,128)(2,1)} %all-to-all-done.arrived_ref), kind=kLoop, calls=%fused_computation.95 | loop fusion | bytes 1024 | tf_op jit(solution)/shard_map/slice | solution.py:175
  147.9 0.1 copy.17
  148.0 0.1 convert_element_type.27.pair_ref
  148.1 9.2 %shard_map.65 = f32[256,2,8,128]{3,2,1,0:T(8,128)S(1)} custom-call(s32[256]{0:T(256)S(1)} %convert_element_type.27.pair_ref, bf16[128,304,128]{2,1,0:T(8,128)(2,1)} %all-to-all-done.arrived_ref, bf16[4,32,144,128]{3,2,1,0:T(8,128)(2,1)} %bitcast.34), custom_call_target="tpu_custom_call" | custom-call | tf_op jit(solution)/shard_map/pallas_call | solution.py:183
  157.3 0.2 slice_subtract_fusion
  157.5 0.4 reshape.182
  158.0 0.3 copy.19
  158.3 0.7 convolution_bitcast_fusion
  159.0 0.6 copy.20
  159.6 1.0 reshape.183
  160.7 0.3 collective-permute-start
  160.9 5.5 %collective-permute-start.1 = (f32[2,8,16,128]{3,2,1,0:T(8,128)S(1)}, f32[2,8,16,128]{3,2,1,0:T(8,128)S(1)}, u32[]{:S(2)}, u32[]{:S(2)}) collective-permute-start(f32[2,8,16,128]{3,2,1,0:T(8,128)S(1)} %reshape.183), channel_id=1, source_target_pairs={{0,64},{32,96},{64,0},{96,32},{1,65},{33,97},{65,1},{97,33},{2,66}... | collective-permute-start | bytes 393224 | tf_op jit(solution)/shard_map/ppermute | solution.py:115
  166.4 2.0 %collective-permute-start.2 = (f32[2,8,16,128]{3,2,1,0:T(8,128)S(1)}, f32[2,8,16,128]{3,2,1,0:T(8,128)S(1)}, u32[]{:S(2)}, u32[]{:S(2)}) collective-permute-start(f32[2,8,16,128]{3,2,1,0:T(8,128)S(1)} %reshape.183), channel_id=1, source_target_pairs={{0,96},{32,0},{64,32},{96,64},{1,97},{33,1},{65,33},{97,65},{2,98}... | collective-permute-start | bytes 393224 | tf_op jit(solution)/shard_map/ppermute | solution.py:115
  168.4 1.0 stack_reshape.3
  169.4 3.1 %collective-permute-done.2 = f32[2,8,16,128]{3,2,1,0:T(8,128)S(1)} collective-permute-done((f32[2,8,16,128]{3,2,1,0:T(8,128)S(1)}, f32[2,8,16,128]{3,2,1,0:T(8,128)S(1)}, u32[]{:S(2)}, u32[]{:S(2)}) %collective-permute-start.2) | collective-permute-done | bytes 131104 | tf_op jit(solution)/shard_map/ppermute | solution.py:115
  172.6 10.0 %collective-permute-start.3 = (f32[2,4,16,128]{3,2,1,0:T(8,128)S(1)}, f32[2,4,16,128]{3,2,1,0:T(8,128)S(1)}, u32[]{:S(2)}, u32[]{:S(2)}) collective-permute-start(f32[2,4,16,128]{3,2,1,0:T(8,128)S(1)} %get-tuple-element.9), channel_id=1, source_target_pairs={{0,1},{1,2},{2,3},{3,4},{4,5},{5,6},{6,7},{7,8},{8,9},{9,10},{10,1... | collective-permute-start | bytes 196616 | tf_op jit(solution)/shard_map/ppermute | solution.py:26
  182.6 1.9 %collective-permute-start.4 = (f32[2,4,16,128]{3,2,1,0:T(8,128)S(1)}, f32[2,4,16,128]{3,2,1,0:T(8,128)S(1)}, u32[]{:S(2)}, u32[]{:S(2)}) collective-permute-start(f32[2,4,16,128]{3,2,1,0:T(8,128)S(1)} %get-tuple-element.10), channel_id=1, source_target_pairs={{1,0},{2,1},{3,2},{4,3},{5,4},{6,5},{7,6},{8,7},{9,8},{10,9},{11,1... | collective-permute-start | bytes 196616 | tf_op jit(solution)/shard_map/ppermute | solution.py:28
  184.6 3.6 %collective-permute-done.4 = f32[2,4,16,128]{3,2,1,0:T(8,128)S(1)} collective-permute-done((f32[2,4,16,128]{3,2,1,0:T(8,128)S(1)}, f32[2,4,16,128]{3,2,1,0:T(8,128)S(1)}, u32[]{:S(2)}, u32[]{:S(2)}) %collective-permute-start.4) | collective-permute-done | bytes 65568 | tf_op jit(solution)/shard_map/ppermute | solution.py:28
  188.3 0.1 fusion.28
  188.4 1.0 fusion.44
  (14 shorter events, 0.2 us)
Async XLA Ops:
  19.9 125.8 %all-to-all-start = ((bf16[128,304,128]{2,1,0:T(8,128)(2,1)}), bf16[128,304,128]{2,1,0:T(8,128)(2,1)}, u32[]{:S(2)}, u32[]{:S(2)}) async-start(bf16[128,304,128]{2,1,0:T(8,128)(2,1)} %shard_map.64), calls=%async_computation | async-start | bytes 19922944 | tf_op jit(solution)/shard_map/all_to_all | solution.py:173
  160.7 8.8 %collective-permute-start = (f32[2,8,16,128]{3,2,1,0:T(8,128)S(1)}, f32[2,8,16,128]{3,2,1,0:T(8,128)S(1)}, u32[]{:S(2)}, u32[]{:S(2)}) collective-permute-start(f32[2,8,16,128]{3,2,1,0:T(8,128)S(1)} %reshape.183), channel_id=1, source_target_pairs={{0,32},{32,64},{64,96},{96,0},{1,33},{33,65},{65,97},{97,1},{2,34}... | collective-permute-start | bytes 393224 | tf_op jit(solution)/shard_map/ppermute | solution.py:115
  160.9 8.5 %collective-permute-start.1 = (f32[2,8,16,128]{3,2,1,0:T(8,128)S(1)}, f32[2,8,16,128]{3,2,1,0:T(8,128)S(1)}, u32[]{:S(2)}, u32[]{:S(2)}) collective-permute-start(f32[2,8,16,128]{3,2,1,0:T(8,128)S(1)} %reshape.183), channel_id=1, source_target_pairs={{0,64},{32,96},{64,0},{96,32},{1,65},{33,97},{65,1},{97,33},{2,66}... | collective-permute-start | bytes 393224 | tf_op jit(solution)/shard_map/ppermute | solution.py:115
  166.4 6.1 %collective-permute-start.2 = (f32[2,8,16,128]{3,2,1,0:T(8,128)S(1)}, f32[2,8,16,128]{3,2,1,0:T(8,128)S(1)}, u32[]{:S(2)}, u32[]{:S(2)}) collective-permute-start(f32[2,8,16,128]{3,2,1,0:T(8,128)S(1)} %reshape.183), channel_id=1, source_target_pairs={{0,96},{32,0},{64,32},{96,64},{1,97},{33,1},{65,33},{97,65},{2,98}... | collective-permute-start | bytes 393224 | tf_op jit(solution)/shard_map/ppermute | solution.py:115
  172.6 11.9 %collective-permute-start.3 = (f32[2,4,16,128]{3,2,1,0:T(8,128)S(1)}, f32[2,4,16,128]{3,2,1,0:T(8,128)S(1)}, u32[]{:S(2)}, u32[]{:S(2)}) collective-permute-start(f32[2,4,16,128]{3,2,1,0:T(8,128)S(1)} %get-tuple-element.9), channel_id=1, source_target_pairs={{0,1},{1,2},{2,3},{3,4},{4,5},{5,6},{6,7},{7,8},{8,9},{9,10},{10,1... | collective-permute-start | bytes 196616 | tf_op jit(solution)/shard_map/ppermute | solution.py:26
  182.6 5.6 %collective-permute-start.4 = (f32[2,4,16,128]{3,2,1,0:T(8,128)S(1)}, f32[2,4,16,128]{3,2,1,0:T(8,128)S(1)}, u32[]{:S(2)}, u32[]{:S(2)}) collective-permute-start(f32[2,4,16,128]{3,2,1,0:T(8,128)S(1)} %get-tuple-element.10), channel_id=1, source_target_pairs={{1,0},{2,1},{3,2},{4,3},{5,4},{6,5},{7,6},{8,7},{9,8},{10,9},{11,1... | collective-permute-start | bytes 196616 | tf_op jit(solution)/shard_map/ppermute | solution.py:28

commit v5 on v3

--- a/solution.py
+++ b/solution.py
@@ -79,28 +79,37 @@
     lax.fori_loop(0, dests, one_dest, 0)
 
 
-def correlate_kernel(pair_ref, arrived_ref, adj_ref, acc_ref):
-    dests = arrived_ref.shape[0]
-    rows = adj_ref.shape[2]
-    bricks = adj_ref.shape[1]
+def correlate_kernel(pair_ref, arrived_hbm, adj_hbm, out_ref, fwd_buf, adj_buf, fwd_sem, adj_sem):
+    slots = out_ref.shape[0]
+    rows = adj_buf.shape[2]
+    bricks = adj_buf.shape[1]
     groups = rows // 8
-    step = pl.program_id(0)
-
-    @pl.when(step == 0)
-    def _():
-        acc_ref[...] = jnp.zeros(acc_ref.shape, acc_ref.dtype)
-
-    base = step * dests * 2
-
-    def one_slot(d, s):
-        pair = pair_ref[base + 2 * d + s]
+    adj_copy = pltpu.make_async_copy(adj_hbm, adj_buf, adj_sem.at[0])
+    adj_copy.start()
+
+    def slot_copy(k):
+        return pltpu.make_async_copy(
+            arrived_hbm.at[k // 2, pl.ds((k % 2) * rows, rows)], fwd_buf.at[k], fwd_sem.at[k]
+        )
+
+    def start(k, carry):
+        @pl.when(pair_ref[k] >= 0)
+        def _():
+            slot_copy(k).start()
+
+        return carry
+
+    lax.fori_loop(0, slots, start, 0)
+    adj_copy.wait()
+
+    def one_slot(k, carry):
+        pair = pair_ref[k]
 
         @pl.when(pair >= 0)
         def _():
-            tx = pair // bricks
-            brick = pair % bricks
-            fwd = arrived_ref[d, s * rows : (s + 1) * rows, :].astype(jnp.float32)
-            adj = adj_ref[tx, brick].astype(jnp.float32)
+            slot_copy(k).wait()
+            fwd = fwd_buf[k].astype(jnp.float32)
+            adj = adj_buf[pair // bricks, pair % bricks].astype(jnp.float32)
             prod = (fwd * adj).reshape(groups, 8, LANES)
             horizontal = None
             vertical = None
@@ -109,15 +118,16 @@
                     vertical = prod[g] if vertical is None else vertical + prod[g]
                 else:
                     horizontal = prod[g] if horizontal is None else horizontal + prod[g]
-            acc_ref[brick, 0] += horizontal
-            acc_ref[brick, 1] += vertical
-
-    def one_dest(d, carry):
-        one_slot(d, 0)
-        one_slot(d, 1)
+            out_ref[k, 0] = horizontal
+            out_ref[k, 1] = vertical
+
+        @pl.when(pair < 0)
+        def _():
+            out_ref[k] = jnp.zeros(out_ref.shape[1:], out_ref.dtype)
+
         return carry
 
-    lax.fori_loop(0, dests, one_dest, 0)
+    lax.fori_loop(0, slots, one_slot, 0)
 
 
 def src_sum(part):
@@ -192,22 +202,31 @@
         jnp.transpose(adjoint, (0, 2, 1, 3)).reshape(local_tx, channels, local_bricks, cells // LANES, LANES),
         (0, 2, 1, 3, 4),
     ).reshape(local_tx, local_bricks, rows, LANES)
-    acc = pl.pallas_call(
+    per_slot = pl.pallas_call(
         correlate_kernel,
-        out_shape=jax.ShapeDtypeStruct((local_bricks, 2, 8, LANES), jnp.float32),
+        out_shape=jax.ShapeDtypeStruct((slot_total, 2, 8, LANES), jnp.float32),
         grid_spec=pltpu.PrefetchScalarGridSpec(
             num_scalar_prefetch=1,
-            grid=(pack_steps,),
-            in_specs=[
-                pl.BlockSpec((dests_per_step, chunk, LANES), lambda g, p: (g, 0, 0)),
-                pl.BlockSpec((local_tx, local_bricks, rows, LANES), lambda g, p: (0, 0, 0, 0)),
+            grid=(),
+            in_specs=[pl.BlockSpec(memory_space=pl.ANY), pl.BlockSpec(memory_space=pl.ANY)],
+            out_specs=pl.BlockSpec(memory_space=pltpu.VMEM),
+            scratch_shapes=[
+                pltpu.VMEM((slot_total, rows, LANES), forward.dtype),
+                pltpu.VMEM(adj_rows.shape, adj_rows.dtype),
+                pltpu.SemaphoreType.DMA((slot_total,)),
+                pltpu.SemaphoreType.DMA((1,)),
             ],
-            out_specs=pl.BlockSpec((local_bricks, 2, 8, LANES), lambda g, p: (0, 0, 0, 0)),
         ),
         compiler_params=pltpu.CompilerParams(vmem_limit_bytes=48 * 1024 * 1024),
     )(arrived_pairs, arrived, adj_rows)
 
-    gradient = (acc[:, :, 0:4, :] - acc[:, :, 4:8, :]).reshape(local_bricks, 2, cells)
+    corr = (per_slot[:, :, 0:4, :] - per_slot[:, :, 4:8, :]).reshape(slot_total, 2 * cells)
+    owner_brick = jnp.maximum(arrived_pairs, 0) % local_bricks
+    owner_table = (
+        (owner_brick[None, :] == jnp.arange(local_bricks, dtype=jnp.int32)[:, None])
+        & (arrived_pairs >= 0)[None, :]
+    ).astype(jnp.float32)
+    gradient = jnp.dot(owner_table, corr, precision=lax.Precision.HIGHEST).reshape(local_bricks, 2, cells)
     slab = (
         gradient.reshape(NBY, NBZ, 2, E, E, E)
         .transpose(2, 3, 0, 4, 1, 5)

time: 193 us -> 195 us (1.010); the launches traced: 191 us -> 195 us
  Pallas kernels: 15.3 us -> 18.9 us
  local copies, waits for them, and re-layouts: 33.9 us -> 31.2 us
  starting transfers between devices: 29.9 us -> 31.9 us
    pallas_call x1, Pallas kernels: 9.2 us -> 12.7 us  [local(): pl.pallas_call(correlate_kernel, out_shape=jax.ShapeDtypeStruct((slot_tot...]
    unnamed x2 -> x0, local copies, waits for them, and re-layouts: 2.33 us -> none
    ppermute x1, starting transfers between devices: 9.1 us -> 11.1 us  [with_halo(): lax.ppermute(tail, axis, [(i, (i + 1) % count) for i in range(ends)])]
where the time goes in v5:
time: 195 us
  waiting for transfers between devices  109 us (56%)
  starting transfers between devices  31.9 us (16%)
  local copies, waits for them, and re-layouts  31.2 us (16%)
  Pallas kernels  18.9 us (10%)
  other arithmetic  3.68 us (2%)
    all_to_all x1, waiting for transfers between devices, local(): lax.all_to_all(payload, ('src', 'vol'), split_axis=0, concat_axis=0, tile...  101 us
    reshape x2, local copies, waits for them, and re-layouts, local(): jnp.transpose(adjoint, (0, 2, 1, 3))  13.8 us
    pallas_call x1, Pallas kernels, local(): pl.pallas_call(correlate_kernel, out_shape=jax.ShapeDtypeStruct((slot_tot...  12.7 us
    reshape x2, local copies, waits for them, and re-layouts, local(): jnp.transpose(forward, (1, 0, 2))  11.7 us
    ppermute x1, starting transfers between devices, with_halo(): lax.ppermute(tail, axis, [(i, (i + 1) % count) for i in range(ends)])  11.1 us
    all_to_all x1, starting transfers between devices, local(): lax.all_to_all(payload, ('src', 'vol'), split_axis=0, concat_axis=0, tile...  10.8 us
    ppermute x3, starting transfers between devices, src_sum(): lax.ppermute(part, 'src', [(i, (i + k) % count) for i in range(count)])  8.06 us
    pallas_call x1, Pallas kernels, local(): pl.pallas_call(pack_kernel, out_shape=jax.ShapeDtypeStruct((devices, chun...  6.13 us
  transfers between devices with their start and end apart: 6, of which 4 were waited for; matrix products, arithmetic and copies ran while one was open for 8% of the time, Pallas kernels for 0%

profile of v5, /device:TPU:57, one launch (start us, length us, event | category | flops | bytes accessed | tf_op | source)
XLA Modules:
  0.0 195.2 jit_solution(18238245102765904514)
XLA Ops:
  0.0 0.9 select_reduce_fusion
  0.9 0.8 select_reduce_fusion.3
  1.7 0.2 convert_reduce_fusion
  1.9 0.1 fusion.54
  2.0 0.2 select_reduce_fusion.1
  2.1 7.7 %reshape.178 = bf16[36,128,4,128]{3,2,1,0:T(4,128)(2,1)} reshape(bf16[36,128,512]{2,1,0:T(8,128)(2,1)} %bitcast.35) | data formatting | bytes 9437184 | tf_op jit(solution)/shard_map/reshape | solution.py:178
  9.8 4.0 %copy.16 = bf16[36,128,4,128]{3,2,0,1:T(4,128)(2,1)S(1)} copy(bf16[36,128,4,128]{3,2,1,0:T(4,128)(2,1)} %reshape.178) | data formatting | bytes 9437184 | tf_op jit(solution)/shard_map/reshape | solution.py:178
  13.8 6.1 %shard_map.64 = bf16[128,304,128]{2,1,0:T(8,128)(2,1)} custom-call(s32[256]{0:T(256)S(1)} %get-tuple-element.14.src_ref, s32[256]{0:T(256)S(1)} %get-tuple-element.13.pair_ref, bf16[128,144,128]{2,1,0:T(8,128)(2,1)S(1)} %bitcast.33), custom_call_target="tpu_custom_call" | custom-call | tf_op jit(solution)/shard_map/pallas_call | solution.py:183
  19.9 10.8 %all-to-all-start = ((bf16[128,304,128]{2,1,0:T(8,128)(2,1)}), bf16[128,304,128]{2,1,0:T(8,128)(2,1)}, u32[]{:S(2)}, u32[]{:S(2)}) async-start(bf16[128,304,128]{2,1,0:T(8,128)(2,1)} %shard_map.64), calls=%async_computation | async-start | bytes 19922944 | tf_op jit(solution)/shard_map/all_to_all | solution.py:195
  30.8 7.7 %reshape.180 = bf16[4,36,32,4,128]{4,3,2,1,0:T(4,128)(2,1)} reshape(bf16[4,36,32,512]{3,2,1,0:T(8,128)(2,1)} %bitcast.36) | data formatting | bytes 9437184 | tf_op jit(solution)/shard_map/reshape | solution.py:202
  38.5 6.1 %copy.18 = bf16[4,36,32,4,128]{4,3,1,2,0:T(4,128)(2,1)} copy(bf16[4,36,32,4,128]{4,3,2,1,0:T(4,128)(2,1)} %reshape.180) | data formatting | bytes 9437184 | tf_op jit(solution)/shard_map/reshape | solution.py:202
  44.6 101.2 %all-to-all-done.arrived_hbm = bf16[128,304,128]{2,1,0:T(8,128)(2,1)} async-done(((bf16[128,304,128]{2,1,0:T(8,128)(2,1)}), bf16[128,304,128]{2,1,0:T(8,128)(2,1)}, u32[]{:S(2)}, u32[]{:S(2)}) %all-to-all-start) | async-done | bytes 9961504 | tf_op jit(solution)/shard_map/all_to_all | solution.py:195
  145.8 2.1 %slice_reduce_fusion.1 = (bf16[128]{0:T(256)(128)(2,1)S(1)}, bf16[128]{0:T(256)(128)(2,1)S(1)}) fusion(bf16[128,304,128]{2,1,0:T(8,128)(2,1)} %all-to-all-done.arrived_hbm), kind=kLoop, calls=%fused_computation.95 | loop fusion | bytes 1024 | tf_op jit(solution)/shard_map/slice | solution.py:197
  148.0 0.1 convert_element_type.27.pair_ref
  148.1 12.7 %shard_map.65 = f32[256,2,8,128]{3,2,1,0:T(8,128)S(1)} custom-call(s32[256]{0:T(256)S(1)} %convert_element_type.27.pair_ref, bf16[128,304,128]{2,1,0:T(8,128)(2,1)} %all-to-all-done.arrived_hbm, bf16[4,32,144,128]{3,2,1,0:T(8,128)(2,1)} %bitcast.34), custom_call_target="tpu_custom_call" | custom-call | tf_op jit(solution)/shard_map/pallas_call | solution.py:205
  160.9 0.2 slice_subtract_fusion
  161.1 0.4 reshape.182
  161.6 0.3 copy.19
  161.9 0.7 convolution_bitcast_fusion
  162.6 0.6 copy.20
  163.2 1.0 reshape.183
  164.2 0.4 collective-permute-start
  164.7 5.6 %collective-permute-start.1 = (f32[2,8,16,128]{3,2,1,0:T(8,128)S(1)}, f32[2,8,16,128]{3,2,1,0:T(8,128)S(1)}, u32[]{:S(2)}, u32[]{:S(2)}) collective-permute-start(f32[2,8,16,128]{3,2,1,0:T(8,128)S(1)} %reshape.183), channel_id=1, source_target_pairs={{0,64},{32,96},{64,0},{96,32},{1,65},{33,97},{65,1},{97,33},{2,66}... | collective-permute-start | bytes 393224 | tf_op jit(solution)/shard_map/ppermute | solution.py:137
  170.3 2.0 %collective-permute-start.2 = (f32[2,8,16,128]{3,2,1,0:T(8,128)S(1)}, f32[2,8,16,128]{3,2,1,0:T(8,128)S(1)}, u32[]{:S(2)}, u32[]{:S(2)}) collective-permute-start(f32[2,8,16,128]{3,2,1,0:T(8,128)S(1)} %reshape.183), channel_id=1, source_target_pairs={{0,96},{32,0},{64,32},{96,64},{1,97},{33,1},{65,33},{97,65},{2,98}... | collective-permute-start | bytes 393224 | tf_op jit(solution)/shard_map/ppermute | solution.py:137
  172.3 1.0 stack_reshape.3
  173.4 0.7 collective-permute-done.1
  174.0 3.1 %collective-permute-done.2 = f32[2,8,16,128]{3,2,1,0:T(8,128)S(1)} collective-permute-done((f32[2,8,16,128]{3,2,1,0:T(8,128)S(1)}, f32[2,8,16,128]{3,2,1,0:T(8,128)S(1)}, u32[]{:S(2)}, u32[]{:S(2)}) %collective-permute-start.2) | collective-permute-done | bytes 131104 | tf_op jit(solution)/shard_map/ppermute | solution.py:137
  177.2 11.1 %collective-permute-start.3 = (f32[2,4,16,128]{3,2,1,0:T(8,128)S(1)}, f32[2,4,16,128]{3,2,1,0:T(8,128)S(1)}, u32[]{:S(2)}, u32[]{:S(2)}) collective-permute-start(f32[2,4,16,128]{3,2,1,0:T(8,128)S(1)} %get-tuple-element.9), channel_id=1, source_target_pairs={{0,1},{1,2},{2,3},{3,4},{4,5},{5,6},{6,7},{7,8},{8,9},{9,10},{10,1... | collective-permute-start | bytes 196616 | tf_op jit(solution)/shard_map/ppermute | solution.py:26
  188.3 1.9 collective-permute-start.4
  190.3 3.6 %collective-permute-done.4 = f32[2,4,16,128]{3,2,1,0:T(8,128)S(1)} collective-permute-done((f32[2,4,16,128]{3,2,1,0:T(8,128)S(1)}, f32[2,4,16,128]{3,2,1,0:T(8,128)S(1)}, u32[]{:S(2)}, u32[]{:S(2)}) %collective-permute-start.4) | collective-permute-done | bytes 65568 | tf_op jit(solution)/shard_map/ppermute | solution.py:28
  194.0 0.1 fusion.28
  194.2 1.0 fusion.44
  (14 shorter events, 0.3 us)
Async XLA Ops:
  19.9 125.8 %all-to-all-start = ((bf16[128,304,128]{2,1,0:T(8,128)(2,1)}), bf16[128,304,128]{2,1,0:T(8,128)(2,1)}, u32[]{:S(2)}, u32[]{:S(2)}) async-start(bf16[128,304,128]{2,1,0:T(8,128)(2,1)} %shard_map.64), calls=%async_computation | async-start | bytes 19922944 | tf_op jit(solution)/shard_map/all_to_all | solution.py:195
  164.2 9.1 %collective-permute-start = (f32[2,8,16,128]{3,2,1,0:T(8,128)S(1)}, f32[2,8,16,128]{3,2,1,0:T(8,128)S(1)}, u32[]{:S(2)}, u32[]{:S(2)}) collective-permute-start(f32[2,8,16,128]{3,2,1,0:T(8,128)S(1)} %reshape.183), channel_id=1, source_target_pairs={{0,32},{32,64},{64,96},{96,0},{1,33},{33,65},{65,97},{97,1},{2,34}... | collective-permute-start | bytes 393224 | tf_op jit(solution)/shard_map/ppermute | solution.py:137
  164.7 9.3 %collective-permute-start.1 = (f32[2,8,16,128]{3,2,1,0:T(8,128)S(1)}, f32[2,8,16,128]{3,2,1,0:T(8,128)S(1)}, u32[]{:S(2)}, u32[]{:S(2)}) collective-permute-start(f32[2,8,16,128]{3,2,1,0:T(8,128)S(1)} %reshape.183), channel_id=1, source_target_pairs={{0,64},{32,96},{64,0},{96,32},{1,65},{33,97},{65,1},{97,33},{2,66}... | collective-permute-start | bytes 393224 | tf_op jit(solution)/shard_map/ppermute | solution.py:137
  170.3 6.8 %collective-permute-start.2 = (f32[2,8,16,128]{3,2,1,0:T(8,128)S(1)}, f32[2,8,16,128]{3,2,1,0:T(8,128)S(1)}, u32[]{:S(2)}, u32[]{:S(2)}) collective-permute-start(f32[2,8,16,128]{3,2,1,0:T(8,128)S(1)} %reshape.183), channel_id=1, source_target_pairs={{0,96},{32,0},{64,32},{96,64},{1,97},{33,1},{65,33},{97,65},{2,98}... | collective-permute-start | bytes 393224 | tf_op jit(solution)/shard_map/ppermute | solution.py:137
  177.2 13.1 %collective-permute-start.3 = (f32[2,4,16,128]{3,2,1,0:T(8,128)S(1)}, f32[2,4,16,128]{3,2,1,0:T(8,128)S(1)}, u32[]{:S(2)}, u32[]{:S(2)}) collective-permute-start(f32[2,4,16,128]{3,2,1,0:T(8,128)S(1)} %get-tuple-element.9), channel_id=1, source_target_pairs={{0,1},{1,2},{2,3},{3,4},{4,5},{5,6},{6,7},{7,8},{8,9},{9,10},{10,1... | collective-permute-start | bytes 196616 | tf_op jit(solution)/shard_map/ppermute | solution.py:26
  188.3 5.6 %collective-permute-start.4 = (f32[2,4,16,128]{3,2,1,0:T(8,128)S(1)}, f32[2,4,16,128]{3,2,1,0:T(8,128)S(1)}, u32[]{:S(2)}, u32[]{:S(2)}) collective-permute-start(f32[2,4,16,128]{3,2,1,0:T(8,128)S(1)} %get-tuple-element.10), channel_id=1, source_target_pairs={{1,0},{2,1},{3,2},{4,3},{5,4},{6,5},{7,6},{8,7},{9,8},{10,9},{11,1... | collective-permute-start | bytes 196616 | tf_op jit(solution)/shard_map/ppermute | solution.py:28

commit v6 on v4

--- a/solution.py
+++ b/solution.py
@@ -71,8 +71,8 @@
         second = src_ref[slot + 1]
         out_ref[d, 0:rows, :] = fwd_ref[jnp.maximum(first, 0)]
         out_ref[d, rows : 2 * rows, :] = fwd_ref[jnp.maximum(second, 0)]
-        row_at = lax.broadcasted_iota(jnp.int32, (META, LANES), 0)
-        tags = jnp.where(row_at < META // 2, pair_ref[slot], pair_ref[slot + 1])
+        lane_at = lax.broadcasted_iota(jnp.int32, (META, LANES), 1)
+        tags = jnp.where(lane_at == 0, pair_ref[slot], pair_ref[slot + 1])
         out_ref[d, 2 * rows : 2 * rows + META, :] = tags.astype(jnp.float32).astype(out_ref.dtype)
         return carry
 
@@ -157,6 +157,7 @@
     ).reshape(stored, rows, LANES)
     chunk = 2 * rows + META
     pack_steps = 8
+    correlate_steps = 4
     dests_per_step = devices // pack_steps
     payload = pl.pallas_call(
         pack_kernel,
@@ -171,9 +172,7 @@
     )(src_of_slot, pair_of_slot, fwd_rows)
 
     arrived = lax.all_to_all(payload, ("src", "vol"), split_axis=0, concat_axis=0, tiled=True)
-    tags = jnp.stack(
-        [arrived[:, 2 * rows, 0], arrived[:, 2 * rows + META // 2, 0]], axis=1
-    ).reshape(slot_total)
+    tags = arrived[:, 2 * rows, 0:2].reshape(slot_total)
     arrived_pairs = tags.astype(jnp.float32).astype(jnp.int32)
 
     adj_rows = jnp.transpose(
@@ -185,12 +184,12 @@
         out_shape=jax.ShapeDtypeStruct((slot_total, 2, 8, LANES), jnp.float32),
         grid_spec=pltpu.PrefetchScalarGridSpec(
             num_scalar_prefetch=1,
-            grid=(pack_steps,),
+            grid=(correlate_steps,),
             in_specs=[
-                pl.BlockSpec((dests_per_step, chunk, LANES), lambda g, p: (g, 0, 0)),
+                pl.BlockSpec((devices // correlate_steps, chunk, LANES), lambda g, p: (g, 0, 0)),
                 pl.BlockSpec((local_tx, local_bricks, rows, LANES), lambda g, p: (0, 0, 0, 0)),
             ],
-            out_specs=pl.BlockSpec((2 * dests_per_step, 2, 8, LANES), lambda g, p: (g, 0, 0, 0)),
+            out_specs=pl.BlockSpec((2 * devices // correlate_steps, 2, 8, LANES), lambda g, p: (g, 0, 0, 0)),
         ),
         compiler_params=pltpu.CompilerParams(vmem_limit_bytes=48 * 1024 * 1024),
     )(arrived_pairs, arrived, adj_rows)

time: 191 us -> 188 us (0.984)
  local copies, waits for them, and re-layouts: 31.2 us -> 29.1 us
    slice x1 -> x0, local copies, waits for them, and re-layouts: 2.07 us -> none  [local(): arrived[:, 2 * rows, 0]]
where the time goes in v6:
time: 188 us; the launch traced here: 187 us
  waiting for transfers between devices  108 us (57%)
  starting transfers between devices  30.4 us (16%)
  local copies, waits for them, and re-layouts  29.1 us (15%)
  Pallas kernels  13.7 us (7%)
  other arithmetic  4.83 us (3%)
    all_to_all x1, waiting for transfers between devices, local(): lax.all_to_all(payload, ('src', 'vol'), split_axis=0, concat_axis=0, tile...  101 us
    reshape x2, local copies, waits for them, and re-layouts, local(): jnp.transpose(adjoint, (0, 2, 1, 3))  13.8 us
    reshape x2, local copies, waits for them, and re-layouts, local(): jnp.transpose(forward, (1, 0, 2))  11.7 us
    all_to_all x1, starting transfers between devices, local(): lax.all_to_all(payload, ('src', 'vol'), split_axis=0, concat_axis=0, tile...  10.8 us
    ppermute x1, starting transfers between devices, with_halo(): lax.ppermute(tail, axis, [(i, (i + 1) % count) for i in range(ends)])  9.96 us
    ppermute x3, starting transfers between devices, src_sum(): lax.ppermute(part, 'src', [(i, (i + k) % count) for i in range(count)])  7.72 us
    pallas_call x1, Pallas kernels, local(): pl.pallas_call(correlate_kernel, out_shape=jax.ShapeDtypeStruct((slot_tot...  7.59 us
    pallas_call x1, Pallas kernels, local(): pl.pallas_call(pack_kernel, out_shape=jax.ShapeDtypeStruct((devices, chun...  6.1 us
  transfers between devices with their start and end apart: 6, of which 3 were waited for; matrix products, arithmetic and copies ran while one was open for 8% of the time, Pallas kernels for 0%

profile of v6, /device:TPU:57, one launch (start us, length us, event | category | flops | bytes accessed | tf_op | source)
XLA Modules:
  0.0 186.8 jit_solution(9005302446479639205)
XLA Ops:
  0.0 0.9 select_reduce_fusion
  0.9 0.8 select_reduce_fusion.3
  1.7 0.2 convert_reduce_fusion
  1.9 0.1 fusion.54
  2.0 0.2 select_reduce_fusion.1
  2.1 7.7 %reshape.177 = bf16[36,128,4,128]{3,2,1,0:T(4,128)(2,1)} reshape(bf16[36,128,512]{2,1,0:T(8,128)(2,1)} %bitcast.33) | data formatting | bytes 9437184 | tf_op jit(solution)/shard_map/reshape | solution.py:156
  9.8 4.0 %copy.15 = bf16[36,128,4,128]{3,2,0,1:T(4,128)(2,1)S(1)} copy(bf16[36,128,4,128]{3,2,1,0:T(4,128)(2,1)} %reshape.177) | data formatting | bytes 9437184 | tf_op jit(solution)/shard_map/reshape | solution.py:156
  13.8 6.1 %shard_map.64 = bf16[128,304,128]{2,1,0:T(8,128)(2,1)} custom-call(s32[256]{0:T(256)S(1)} %get-tuple-element.12.src_ref, s32[256]{0:T(256)S(1)} %get-tuple-element.11.pair_ref, bf16[128,144,128]{2,1,0:T(8,128)(2,1)S(1)} %bitcast.31), custom_call_target="tpu_custom_call" | custom-call | tf_op jit(solution)/shard_map/pallas_call | solution.py:162
  19.9 10.8 %all-to-all-start = ((bf16[128,304,128]{2,1,0:T(8,128)(2,1)}), bf16[128,304,128]{2,1,0:T(8,128)(2,1)}, u32[]{:S(2)}, u32[]{:S(2)}) async-start(bf16[128,304,128]{2,1,0:T(8,128)(2,1)} %shard_map.64), calls=%async_computation | async-start | bytes 19922944 | tf_op jit(solution)/shard_map/all_to_all | solution.py:174
  30.7 7.7 %reshape.179 = bf16[4,36,32,4,128]{4,3,2,1,0:T(4,128)(2,1)} reshape(bf16[4,36,32,512]{3,2,1,0:T(8,128)(2,1)} %bitcast.34) | data formatting | bytes 9437184 | tf_op jit(solution)/shard_map/reshape | solution.py:179
  38.4 6.1 %copy.16 = bf16[4,36,32,4,128]{4,3,1,2,0:T(4,128)(2,1)} copy(bf16[4,36,32,4,128]{4,3,2,1,0:T(4,128)(2,1)} %reshape.179) | data formatting | bytes 9437184 | tf_op jit(solution)/shard_map/reshape | solution.py:179
  44.5 101.2 %all-to-all-done.arrived_ref = bf16[128,304,128]{2,1,0:T(8,128)(2,1)} async-done(((bf16[128,304,128]{2,1,0:T(8,128)(2,1)}), bf16[128,304,128]{2,1,0:T(8,128)(2,1)}, u32[]{:S(2)}, u32[]{:S(2)}) %all-to-all-start) | async-done | bytes 9961504 | tf_op jit(solution)/shard_map/all_to_all | solution.py:174
  145.7 1.2 fusion.56
  146.9 0.1 convert_element_type.27.pair_ref
  147.1 7.6 %shard_map.65 = f32[256,2,8,128]{3,2,1,0:T(8,128)S(1)} custom-call(s32[256]{0:T(256)S(1)} %convert_element_type.27.pair_ref, bf16[128,304,128]{2,1,0:T(8,128)(2,1)} %all-to-all-done.arrived_ref, bf16[4,32,144,128]{3,2,1,0:T(8,128)(2,1)} %bitcast.32), custom_call_target="tpu_custom_call" | custom-call | tf_op jit(solution)/shard_map/pallas_call | solution.py:182
  154.7 0.2 slice_subtract_fusion
  154.9 0.4 reshape.181
  155.3 0.3 copy.17
  155.7 0.7 convolution_bitcast_fusion
  156.4 0.6 copy.18
  157.0 1.0 reshape.182
  158.0 0.3 collective-permute-start
  158.3 5.5 %collective-permute-start.1 = (f32[2,8,16,128]{3,2,1,0:T(8,128)S(1)}, f32[2,8,16,128]{3,2,1,0:T(8,128)S(1)}, u32[]{:S(2)}, u32[]{:S(2)}) collective-permute-start(f32[2,8,16,128]{3,2,1,0:T(8,128)S(1)} %reshape.182), channel_id=1, source_target_pairs={{0,64},{32,96},{64,0},{96,32},{1,65},{33,97},{65,1},{97,33},{2,66}... | collective-permute-start | bytes 393224 | tf_op jit(solution)/shard_map/ppermute | solution.py:115
  163.8 2.0 %collective-permute-start.2 = (f32[2,8,16,128]{3,2,1,0:T(8,128)S(1)}, f32[2,8,16,128]{3,2,1,0:T(8,128)S(1)}, u32[]{:S(2)}, u32[]{:S(2)}) collective-permute-start(f32[2,8,16,128]{3,2,1,0:T(8,128)S(1)} %reshape.182), channel_id=1, source_target_pairs={{0,96},{32,0},{64,32},{96,64},{1,97},{33,1},{65,33},{97,65},{2,98}... | collective-permute-start | bytes 393224 | tf_op jit(solution)/shard_map/ppermute | solution.py:115
  165.7 1.0 stack_reshape.3
  166.8 3.1 %collective-permute-done.2 = f32[2,8,16,128]{3,2,1,0:T(8,128)S(1)} collective-permute-done((f32[2,8,16,128]{3,2,1,0:T(8,128)S(1)}, f32[2,8,16,128]{3,2,1,0:T(8,128)S(1)}, u32[]{:S(2)}, u32[]{:S(2)}) %collective-permute-start.2) | collective-permute-done | bytes 131104 | tf_op jit(solution)/shard_map/ppermute | solution.py:115
  170.0 10.0 %collective-permute-start.3 = (f32[2,4,16,128]{3,2,1,0:T(8,128)S(1)}, f32[2,4,16,128]{3,2,1,0:T(8,128)S(1)}, u32[]{:S(2)}, u32[]{:S(2)}) collective-permute-start(f32[2,4,16,128]{3,2,1,0:T(8,128)S(1)} %get-tuple-element.7), channel_id=1, source_target_pairs={{0,1},{1,2},{2,3},{3,4},{4,5},{5,6},{6,7},{7,8},{8,9},{9,10},{10,1... | collective-permute-start | bytes 196616 | tf_op jit(solution)/shard_map/ppermute | solution.py:26
  180.0 1.9 %collective-permute-start.4 = (f32[2,4,16,128]{3,2,1,0:T(8,128)S(1)}, f32[2,4,16,128]{3,2,1,0:T(8,128)S(1)}, u32[]{:S(2)}, u32[]{:S(2)}) collective-permute-start(f32[2,4,16,128]{3,2,1,0:T(8,128)S(1)} %get-tuple-element.8), channel_id=1, source_target_pairs={{1,0},{2,1},{3,2},{4,3},{5,4},{6,5},{7,6},{8,7},{9,8},{10,9},{11,1... | collective-permute-start | bytes 196616 | tf_op jit(solution)/shard_map/ppermute | solution.py:28
  181.9 3.6 %collective-permute-done.4 = f32[2,4,16,128]{3,2,1,0:T(8,128)S(1)} collective-permute-done((f32[2,4,16,128]{3,2,1,0:T(8,128)S(1)}, f32[2,4,16,128]{3,2,1,0:T(8,128)S(1)}, u32[]{:S(2)}, u32[]{:S(2)}) %collective-permute-start.4) | collective-permute-done | bytes 65568 | tf_op jit(solution)/shard_map/ppermute | solution.py:28
  185.6 0.1 fusion.3
  185.6 0.1 fusion.28
  185.8 1.0 fusion.44
  (12 shorter events, 0.1 us)
Async XLA Ops:
  19.9 125.8 %all-to-all-start = ((bf16[128,304,128]{2,1,0:T(8,128)(2,1)}), bf16[128,304,128]{2,1,0:T(8,128)(2,1)}, u32[]{:S(2)}, u32[]{:S(2)}) async-start(bf16[128,304,128]{2,1,0:T(8,128)(2,1)} %shard_map.64), calls=%async_computation | async-start | bytes 19922944 | tf_op jit(solution)/shard_map/all_to_all | solution.py:174
  158.0 8.8 %collective-permute-start = (f32[2,8,16,128]{3,2,1,0:T(8,128)S(1)}, f32[2,8,16,128]{3,2,1,0:T(8,128)S(1)}, u32[]{:S(2)}, u32[]{:S(2)}) collective-permute-start(f32[2,8,16,128]{3,2,1,0:T(8,128)S(1)} %reshape.182), channel_id=1, source_target_pairs={{0,32},{32,64},{64,96},{96,0},{1,33},{33,65},{65,97},{97,1},{2,34}... | collective-permute-start | bytes 393224 | tf_op jit(solution)/shard_map/ppermute | solution.py:115
  158.3 8.5 %collective-permute-start.1 = (f32[2,8,16,128]{3,2,1,0:T(8,128)S(1)}, f32[2,8,16,128]{3,2,1,0:T(8,128)S(1)}, u32[]{:S(2)}, u32[]{:S(2)}) collective-permute-start(f32[2,8,16,128]{3,2,1,0:T(8,128)S(1)} %reshape.182), channel_id=1, source_target_pairs={{0,64},{32,96},{64,0},{96,32},{1,65},{33,97},{65,1},{97,33},{2,66}... | collective-permute-start | bytes 393224 | tf_op jit(solution)/shard_map/ppermute | solution.py:115
  163.8 6.1 %collective-permute-start.2 = (f32[2,8,16,128]{3,2,1,0:T(8,128)S(1)}, f32[2,8,16,128]{3,2,1,0:T(8,128)S(1)}, u32[]{:S(2)}, u32[]{:S(2)}) collective-permute-start(f32[2,8,16,128]{3,2,1,0:T(8,128)S(1)} %reshape.182), channel_id=1, source_target_pairs={{0,96},{32,0},{64,32},{96,64},{1,97},{33,1},{65,33},{97,65},{2,98}... | collective-permute-start | bytes 393224 | tf_op jit(solution)/shard_map/ppermute | solution.py:115
  170.0 11.9 %collective-permute-start.3 = (f32[2,4,16,128]{3,2,1,0:T(8,128)S(1)}, f32[2,4,16,128]{3,2,1,0:T(8,128)S(1)}, u32[]{:S(2)}, u32[]{:S(2)}) collective-permute-start(f32[2,4,16,128]{3,2,1,0:T(8,128)S(1)} %get-tuple-element.7), channel_id=1, source_target_pairs={{0,1},{1,2},{2,3},{3,4},{4,5},{5,6},{6,7},{7,8},{8,9},{9,10},{10,1... | collective-permute-start | bytes 196616 | tf_op jit(solution)/shard_map/ppermute | solution.py:26
  180.0 5.6 %collective-permute-start.4 = (f32[2,4,16,128]{3,2,1,0:T(8,128)S(1)}, f32[2,4,16,128]{3,2,1,0:T(8,128)S(1)}, u32[]{:S(2)}, u32[]{:S(2)}) collective-permute-start(f32[2,4,16,128]{3,2,1,0:T(8,128)S(1)} %get-tuple-element.8), channel_id=1, source_target_pairs={{1,0},{2,1},{3,2},{4,3},{5,4},{6,5},{7,6},{8,7},{9,8},{10,9},{11,1... | collective-permute-start | bytes 196616 | tf_op jit(solution)/shard_map/ppermute | solution.py:28

commit v7 on v6

--- a/solution.py
+++ b/solution.py
@@ -157,7 +157,7 @@
     ).reshape(stored, rows, LANES)
     chunk = 2 * rows + META
     pack_steps = 8
-    correlate_steps = 4
+    correlate_steps = 2
     dests_per_step = devices // pack_steps
     payload = pl.pallas_call(
         pack_kernel,

time: 188 us -> 187 us (level)
  no operation moved by 1% of the time
where the time goes in v7:
time: 187 us; the launch traced here: 186 us
  waiting for transfers between devices  108 us (58%)
  starting transfers between devices  30.4 us (16%)
  local copies, waits for them, and re-layouts  29.1 us (16%)
  Pallas kernels  13.2 us (7%)
  other arithmetic  4.83 us (3%)
    all_to_all x1, waiting for transfers between devices, local(): lax.all_to_all(payload, ('src', 'vol'), split_axis=0, concat_axis=0, tile...  101 us
    reshape x2, local copies, waits for them, and re-layouts, local(): jnp.transpose(adjoint, (0, 2, 1, 3))  13.8 us
    reshape x2, local copies, waits for them, and re-layouts, local(): jnp.transpose(forward, (1, 0, 2))  11.7 us
    all_to_all x1, starting transfers between devices, local(): lax.all_to_all(payload, ('src', 'vol'), split_axis=0, concat_axis=0, tile...  10.8 us
    ppermute x1, starting transfers between devices, with_halo(): lax.ppermute(tail, axis, [(i, (i + 1) % count) for i in range(ends)])  9.98 us
    ppermute x3, starting transfers between devices, src_sum(): lax.ppermute(part, 'src', [(i, (i + k) % count) for i in range(count)])  7.71 us
    pallas_call x1, Pallas kernels, local(): pl.pallas_call(correlate_kernel, out_shape=jax.ShapeDtypeStruct((slot_tot...  7.12 us
    pallas_call x1, Pallas kernels, local(): pl.pallas_call(pack_kernel, out_shape=jax.ShapeDtypeStruct((devices, chun...  6.1 us
  transfers between devices with their start and end apart: 6, of which 3 were waited for; matrix products, arithmetic and copies ran while one was open for 8% of the time, Pallas kernels for 0%

profile of v7, /device:TPU:57, one launch (start us, length us, event | category | flops | bytes accessed | tf_op | source)
XLA Modules:
  0.0 186.3 jit_solution(14350859383253177933)
XLA Ops:
  0.0 0.9 select_reduce_fusion
  0.9 0.8 select_reduce_fusion.3
  1.7 0.2 convert_reduce_fusion
  1.9 0.1 fusion.54
  2.0 0.2 select_reduce_fusion.1
  2.1 7.7 %reshape.177 = bf16[36,128,4,128]{3,2,1,0:T(4,128)(2,1)} reshape(bf16[36,128,512]{2,1,0:T(8,128)(2,1)} %bitcast.33) | data formatting | bytes 9437184 | tf_op jit(solution)/shard_map/reshape | solution.py:156
  9.8 4.0 %copy.15 = bf16[36,128,4,128]{3,2,0,1:T(4,128)(2,1)S(1)} copy(bf16[36,128,4,128]{3,2,1,0:T(4,128)(2,1)} %reshape.177) | data formatting | bytes 9437184 | tf_op jit(solution)/shard_map/reshape | solution.py:156
  13.8 6.1 %shard_map.64 = bf16[128,304,128]{2,1,0:T(8,128)(2,1)} custom-call(s32[256]{0:T(256)S(1)} %get-tuple-element.12.src_ref, s32[256]{0:T(256)S(1)} %get-tuple-element.11.pair_ref, bf16[128,144,128]{2,1,0:T(8,128)(2,1)S(1)} %bitcast.31), custom_call_target="tpu_custom_call" | custom-call | tf_op jit(solution)/shard_map/pallas_call | solution.py:162
  19.9 10.8 %all-to-all-start = ((bf16[128,304,128]{2,1,0:T(8,128)(2,1)}), bf16[128,304,128]{2,1,0:T(8,128)(2,1)}, u32[]{:S(2)}, u32[]{:S(2)}) async-start(bf16[128,304,128]{2,1,0:T(8,128)(2,1)} %shard_map.64), calls=%async_computation | async-start | bytes 19922944 | tf_op jit(solution)/shard_map/all_to_all | solution.py:174
  30.7 7.7 %reshape.179 = bf16[4,36,32,4,128]{4,3,2,1,0:T(4,128)(2,1)} reshape(bf16[4,36,32,512]{3,2,1,0:T(8,128)(2,1)} %bitcast.34) | data formatting | bytes 9437184 | tf_op jit(solution)/shard_map/reshape | solution.py:179
  38.4 6.1 %copy.16 = bf16[4,36,32,4,128]{4,3,1,2,0:T(4,128)(2,1)} copy(bf16[4,36,32,4,128]{4,3,2,1,0:T(4,128)(2,1)} %reshape.179) | data formatting | bytes 9437184 | tf_op jit(solution)/shard_map/reshape | solution.py:179
  44.5 101.2 %all-to-all-done.arrived_ref = bf16[128,304,128]{2,1,0:T(8,128)(2,1)} async-done(((bf16[128,304,128]{2,1,0:T(8,128)(2,1)}), bf16[128,304,128]{2,1,0:T(8,128)(2,1)}, u32[]{:S(2)}, u32[]{:S(2)}) %all-to-all-start) | async-done | bytes 9961504 | tf_op jit(solution)/shard_map/all_to_all | solution.py:174
  145.7 1.2 fusion.56
  146.9 0.1 convert_element_type.27.pair_ref
  147.1 7.1 %shard_map.65 = f32[256,2,8,128]{3,2,1,0:T(8,128)S(1)} custom-call(s32[256]{0:T(256)S(1)} %convert_element_type.27.pair_ref, bf16[128,304,128]{2,1,0:T(8,128)(2,1)} %all-to-all-done.arrived_ref, bf16[4,32,144,128]{3,2,1,0:T(8,128)(2,1)} %bitcast.32), custom_call_target="tpu_custom_call" | custom-call | tf_op jit(solution)/shard_map/pallas_call | solution.py:182
  154.2 0.2 slice_subtract_fusion
  154.4 0.4 reshape.181
  154.9 0.3 copy.17
  155.2 0.7 convolution_bitcast_fusion
  155.9 0.6 copy.18
  156.5 1.0 reshape.182
  157.5 0.3 collective-permute-start
  157.8 5.5 %collective-permute-start.1 = (f32[2,8,16,128]{3,2,1,0:T(8,128)S(1)}, f32[2,8,16,128]{3,2,1,0:T(8,128)S(1)}, u32[]{:S(2)}, u32[]{:S(2)}) collective-permute-start(f32[2,8,16,128]{3,2,1,0:T(8,128)S(1)} %reshape.182), channel_id=1, source_target_pairs={{0,64},{32,96},{64,0},{96,32},{1,65},{33,97},{65,1},{97,33},{2,66}... | collective-permute-start | bytes 393224 | tf_op jit(solution)/shard_map/ppermute | solution.py:115
  163.3 2.0 %collective-permute-start.2 = (f32[2,8,16,128]{3,2,1,0:T(8,128)S(1)}, f32[2,8,16,128]{3,2,1,0:T(8,128)S(1)}, u32[]{:S(2)}, u32[]{:S(2)}) collective-permute-start(f32[2,8,16,128]{3,2,1,0:T(8,128)S(1)} %reshape.182), channel_id=1, source_target_pairs={{0,96},{32,0},{64,32},{96,64},{1,97},{33,1},{65,33},{97,65},{2,98}... | collective-permute-start | bytes 393224 | tf_op jit(solution)/shard_map/ppermute | solution.py:115
  165.3 1.0 stack_reshape.3
  166.3 3.1 %collective-permute-done.2 = f32[2,8,16,128]{3,2,1,0:T(8,128)S(1)} collective-permute-done((f32[2,8,16,128]{3,2,1,0:T(8,128)S(1)}, f32[2,8,16,128]{3,2,1,0:T(8,128)S(1)}, u32[]{:S(2)}, u32[]{:S(2)}) %collective-permute-start.2) | collective-permute-done | bytes 131104 | tf_op jit(solution)/shard_map/ppermute | solution.py:115
  169.5 10.0 %collective-permute-start.3 = (f32[2,4,16,128]{3,2,1,0:T(8,128)S(1)}, f32[2,4,16,128]{3,2,1,0:T(8,128)S(1)}, u32[]{:S(2)}, u32[]{:S(2)}) collective-permute-start(f32[2,4,16,128]{3,2,1,0:T(8,128)S(1)} %get-tuple-element.7), channel_id=1, source_target_pairs={{0,1},{1,2},{2,3},{3,4},{4,5},{5,6},{6,7},{7,8},{8,9},{9,10},{10,1... | collective-permute-start | bytes 196616 | tf_op jit(solution)/shard_map/ppermute | solution.py:26
  179.5 1.9 %collective-permute-start.4 = (f32[2,4,16,128]{3,2,1,0:T(8,128)S(1)}, f32[2,4,16,128]{3,2,1,0:T(8,128)S(1)}, u32[]{:S(2)}, u32[]{:S(2)}) collective-permute-start(f32[2,4,16,128]{3,2,1,0:T(8,128)S(1)} %get-tuple-element.8), channel_id=1, source_target_pairs={{1,0},{2,1},{3,2},{4,3},{5,4},{6,5},{7,6},{8,7},{9,8},{10,9},{11,1... | collective-permute-start | bytes 196616 | tf_op jit(solution)/shard_map/ppermute | solution.py:28
  181.4 3.6 %collective-permute-done.4 = f32[2,4,16,128]{3,2,1,0:T(8,128)S(1)} collective-permute-done((f32[2,4,16,128]{3,2,1,0:T(8,128)S(1)}, f32[2,4,16,128]{3,2,1,0:T(8,128)S(1)}, u32[]{:S(2)}, u32[]{:S(2)}) %collective-permute-start.4) | collective-permute-done | bytes 65568 | tf_op jit(solution)/shard_map/ppermute | solution.py:28
  185.1 0.1 fusion.3
  185.2 0.1 fusion.28
  185.3 1.0 fusion.44
  (12 shorter events, 0.1 us)
Async XLA Ops:
  19.9 125.8 %all-to-all-start = ((bf16[128,304,128]{2,1,0:T(8,128)(2,1)}), bf16[128,304,128]{2,1,0:T(8,128)(2,1)}, u32[]{:S(2)}, u32[]{:S(2)}) async-start(bf16[128,304,128]{2,1,0:T(8,128)(2,1)} %shard_map.64), calls=%async_computation | async-start | bytes 19922944 | tf_op jit(solution)/shard_map/all_to_all | solution.py:174
  157.5 8.8 %collective-permute-start = (f32[2,8,16,128]{3,2,1,0:T(8,128)S(1)}, f32[2,8,16,128]{3,2,1,0:T(8,128)S(1)}, u32[]{:S(2)}, u32[]{:S(2)}) collective-permute-start(f32[2,8,16,128]{3,2,1,0:T(8,128)S(1)} %reshape.182), channel_id=1, source_target_pairs={{0,32},{32,64},{64,96},{96,0},{1,33},{33,65},{65,97},{97,1},{2,34}... | collective-permute-start | bytes 393224 | tf_op jit(solution)/shard_map/ppermute | solution.py:115
  157.8 8.5 %collective-permute-start.1 = (f32[2,8,16,128]{3,2,1,0:T(8,128)S(1)}, f32[2,8,16,128]{3,2,1,0:T(8,128)S(1)}, u32[]{:S(2)}, u32[]{:S(2)}) collective-permute-start(f32[2,8,16,128]{3,2,1,0:T(8,128)S(1)} %reshape.182), channel_id=1, source_target_pairs={{0,64},{32,96},{64,0},{96,32},{1,65},{33,97},{65,1},{97,33},{2,66}... | collective-permute-start | bytes 393224 | tf_op jit(solution)/shard_map/ppermute | solution.py:115
  163.3 6.1 %collective-permute-start.2 = (f32[2,8,16,128]{3,2,1,0:T(8,128)S(1)}, f32[2,8,16,128]{3,2,1,0:T(8,128)S(1)}, u32[]{:S(2)}, u32[]{:S(2)}) collective-permute-start(f32[2,8,16,128]{3,2,1,0:T(8,128)S(1)} %reshape.182), channel_id=1, source_target_pairs={{0,96},{32,0},{64,32},{96,64},{1,97},{33,1},{65,33},{97,65},{2,98}... | collective-permute-start | bytes 393224 | tf_op jit(solution)/shard_map/ppermute | solution.py:115
  169.5 11.9 %collective-permute-start.3 = (f32[2,4,16,128]{3,2,1,0:T(8,128)S(1)}, f32[2,4,16,128]{3,2,1,0:T(8,128)S(1)}, u32[]{:S(2)}, u32[]{:S(2)}) collective-permute-start(f32[2,4,16,128]{3,2,1,0:T(8,128)S(1)} %get-tuple-element.7), channel_id=1, source_target_pairs={{0,1},{1,2},{2,3},{3,4},{4,5},{5,6},{6,7},{7,8},{8,9},{9,10},{10,1... | collective-permute-start | bytes 196616 | tf_op jit(solution)/shard_map/ppermute | solution.py:26
  179.5 5.6 %collective-permute-start.4 = (f32[2,4,16,128]{3,2,1,0:T(8,128)S(1)}, f32[2,4,16,128]{3,2,1,0:T(8,128)S(1)}, u32[]{:S(2)}, u32[]{:S(2)}) collective-permute-start(f32[2,4,16,128]{3,2,1,0:T(8,128)S(1)} %get-tuple-element.8), channel_id=1, source_target_pairs={{1,0},{2,1},{3,2},{4,3},{5,4},{6,5},{7,6},{8,7},{9,8},{10,9},{11,1... | collective-permute-start | bytes 196616 | tf_op jit(solution)/shard_map/ppermute | solution.py:28

commit v8 on v7

--- a/solution.py
+++ b/solution.py
@@ -62,15 +62,15 @@
 
 def pack_kernel(src_ref, pair_ref, fwd_ref, out_ref):
     dests = out_ref.shape[0]
-    rows = fwd_ref.shape[1]
+    rows = fwd_ref.shape[1] * fwd_ref.shape[2] // LANES
     base = pl.program_id(0) * dests * 2
 
     def one_dest(d, carry):
         slot = base + 2 * d
         first = src_ref[slot]
         second = src_ref[slot + 1]
-        out_ref[d, 0:rows, :] = fwd_ref[jnp.maximum(first, 0)]
-        out_ref[d, rows : 2 * rows, :] = fwd_ref[jnp.maximum(second, 0)]
+        out_ref[d, 0:rows, :] = fwd_ref[jnp.maximum(first, 0)].reshape(rows, LANES)
+        out_ref[d, rows : 2 * rows, :] = fwd_ref[jnp.maximum(second, 0)].reshape(rows, LANES)
         lane_at = lax.broadcasted_iota(jnp.int32, (META, LANES), 1)
         tags = jnp.where(lane_at == 0, pair_ref[slot], pair_ref[slot + 1])
         out_ref[d, 2 * rows : 2 * rows + META, :] = tags.astype(jnp.float32).astype(out_ref.dtype)
@@ -152,9 +152,6 @@
         filled, jnp.sum(jnp.where(slot_hits, pair_index[None, :], 0), axis=1), -1
     ).astype(jnp.int32)
 
-    fwd_rows = jnp.transpose(
-        jnp.transpose(forward, (1, 0, 2)).reshape(channels, stored, cells // LANES, LANES), (1, 0, 2, 3)
-    ).reshape(stored, rows, LANES)
     chunk = 2 * rows + META
     pack_steps = 8
     correlate_steps = 2
@@ -165,11 +162,11 @@
         grid_spec=pltpu.PrefetchScalarGridSpec(
             num_scalar_prefetch=2,
             grid=(pack_steps,),
-            in_specs=[pl.BlockSpec((stored, rows, LANES), lambda g, s, p: (0, 0, 0))],
+            in_specs=[pl.BlockSpec((stored, channels, cells), lambda g, s, p: (0, 0, 0))],
             out_specs=pl.BlockSpec((dests_per_step, chunk, LANES), lambda g, s, p: (g, 0, 0)),
         ),
         compiler_params=pltpu.CompilerParams(vmem_limit_bytes=48 * 1024 * 1024),
-    )(src_of_slot, pair_of_slot, fwd_rows)
+    )(src_of_slot, pair_of_slot, forward)
 
     arrived = lax.all_to_all(payload, ("src", "vol"), split_axis=0, concat_axis=0, tiled=True)
     tags = arrived[:, 2 * rows, 0:2].reshape(slot_total)

time: 187 us -> 183 us (0.979)
  local copies, waits for them, and re-layouts: 29.1 us -> 22.4 us
    reshape x2 -> x0, local copies, waits for them, and re-layouts: 11.7 us -> none  [local(): jnp.transpose(forward, (1, 0, 2))]
    unnamed x0 -> x1, local copies, waits for them, and re-layouts: none -> 5.02 us
  transfers between devices with their start and end apart: 6 -> 6, of which waited for: 3 -> 4; matrix products, arithmetic and copies ran while one was open for 8% -> 8% of each run, Pallas kernels for 0% -> 0%
where the time goes in v8:
time: 183 us; the launch traced here: 181 us
  waiting for transfers between devices  108 us (59%)
  starting transfers between devices  30.1 us (16%)
  local copies, waits for them, and re-layouts  22.4 us (12%)
  Pallas kernels  14.6 us (8%)
  other arithmetic  4.83 us (3%)
    all_to_all x1, waiting for transfers between devices, local(): lax.all_to_all(payload, ('src', 'vol'), split_axis=0, concat_axis=0, tile...  101 us
    reshape x2, local copies, waits for them, and re-layouts, local(): jnp.transpose(adjoint, (0, 2, 1, 3))  13.8 us
    all_to_all x1, starting transfers between devices, local(): lax.all_to_all(payload, ('src', 'vol'), split_axis=0, concat_axis=0, tile...  10.8 us
    ppermute x1, starting transfers between devices, with_halo(): lax.ppermute(tail, axis, [(i, (i + 1) % count) for i in range(ends)])  10.3 us
    pallas_call x1, Pallas kernels, local(): pl.pallas_call(pack_kernel, out_shape=jax.ShapeDtypeStruct((devices, chun...  7.46 us
    ppermute x3, starting transfers between devices, src_sum(): lax.ppermute(part, 'src', [(i, (i + k) % count) for i in range(count)])  7.13 us
    pallas_call x1, Pallas kernels, local(): pl.pallas_call(correlate_kernel, out_shape=jax.ShapeDtypeStruct((slot_tot...  7.11 us
    unnamed x1, local copies, waits for them, and re-layouts  5.02 us
  transfers between devices with their start and end apart: 6, of which 4 were waited for; matrix products, arithmetic and copies ran while one was open for 8% of the time, Pallas kernels for 0%

profile of v8, /device:TPU:57, one launch (start us, length us, event | category | flops | bytes accessed | tf_op | source)
XLA Modules:
  0.0 181.3 jit_solution(3044484596894676802)
XLA Ops:
  0.0 0.9 select_reduce_fusion
  0.9 0.8 select_reduce_fusion.3
  1.7 0.2 convert_reduce_fusion
  1.9 0.1 fusion.54
  2.0 0.2 select_reduce_fusion.1
  2.1 5.0 %copy.15.fwd_ref = bf16[128,36,512]{2,1,0:T(8,128)(2,1)S(1)} copy(bf16[128,36,512]{2,0,1:T(8,128)(2,1)} %param.6) | data formatting | bytes 9437184 | tf_op args[0]
  7.2 7.5 %shard_map.64 = bf16[128,304,128]{2,1,0:T(8,128)(2,1)} custom-call(s32[256]{0:T(256)S(1)} %get-tuple-element.12.src_ref, s32[256]{0:T(256)S(1)} %get-tuple-element.11.pair_ref, bf16[128,36,512]{2,1,0:T(8,128)(2,1)S(1)} %copy.15.fwd_ref), custom_call_target="tpu_custom_call" | custom-call | tf_op jit(solution)/shard_map/pallas_call | solution.py:159
  14.6 10.8 %all-to-all-start = ((bf16[128,304,128]{2,1,0:T(8,128)(2,1)}), bf16[128,304,128]{2,1,0:T(8,128)(2,1)}, u32[]{:S(2)}, u32[]{:S(2)}) async-start(bf16[128,304,128]{2,1,0:T(8,128)(2,1)} %shard_map.64), calls=%async_computation | async-start | bytes 19922944 | tf_op jit(solution)/shard_map/all_to_all | solution.py:171
  25.4 7.7 %reshape.171 = bf16[4,36,32,4,128]{4,3,2,1,0:T(4,128)(2,1)} reshape(bf16[4,36,32,512]{3,2,1,0:T(8,128)(2,1)} %bitcast.28) | data formatting | bytes 9437184 | tf_op jit(solution)/shard_map/reshape | solution.py:176
  33.1 6.1 %copy.16 = bf16[4,36,32,4,128]{4,3,1,2,0:T(4,128)(2,1)} copy(bf16[4,36,32,4,128]{4,3,2,1,0:T(4,128)(2,1)} %reshape.171) | data formatting | bytes 9437184 | tf_op jit(solution)/shard_map/reshape | solution.py:176
  39.2 101.2 %all-to-all-done.arrived_ref = bf16[128,304,128]{2,1,0:T(8,128)(2,1)} async-done(((bf16[128,304,128]{2,1,0:T(8,128)(2,1)}), bf16[128,304,128]{2,1,0:T(8,128)(2,1)}, u32[]{:S(2)}, u32[]{:S(2)}) %all-to-all-start) | async-done | bytes 9961504 | tf_op jit(solution)/shard_map/all_to_all | solution.py:171
  140.5 1.2 fusion.56
  141.6 0.1 convert_element_type.27.pair_ref
  141.8 7.1 %shard_map.65 = f32[256,2,8,128]{3,2,1,0:T(8,128)S(1)} custom-call(s32[256]{0:T(256)S(1)} %convert_element_type.27.pair_ref, bf16[128,304,128]{2,1,0:T(8,128)(2,1)} %all-to-all-done.arrived_ref, bf16[4,32,144,128]{3,2,1,0:T(8,128)(2,1)} %bitcast.27), custom_call_target="tpu_custom_call" | custom-call | tf_op jit(solution)/shard_map/pallas_call | solution.py:179
  148.9 0.2 slice_subtract_fusion
  149.1 0.4 reshape.173
  149.6 0.3 copy.17
  149.9 0.7 convolution_bitcast_fusion
  150.6 0.6 copy.18
  151.2 1.0 reshape.174
  152.3 5.7 %collective-permute-start.1 = (f32[2,8,16,128]{3,2,1,0:T(8,128)S(1)}, f32[2,8,16,128]{3,2,1,0:T(8,128)S(1)}, u32[]{:S(2)}, u32[]{:S(2)}) collective-permute-start(f32[2,8,16,128]{3,2,1,0:T(8,128)S(1)} %reshape.174), channel_id=1, source_target_pairs={{0,64},{32,96},{64,0},{96,32},{1,65},{33,97},{65,1},{97,33},{2,66}... | collective-permute-start | bytes 393224 | tf_op jit(solution)/shard_map/ppermute | solution.py:115
  157.9 1.5 collective-permute-start
  159.4 1.0 stack_reshape.3
  160.4 0.5 collective-permute-done.1
  160.9 3.1 %collective-permute-done.2 = f32[2,8,16,128]{3,2,1,0:T(8,128)S(1)} collective-permute-done((f32[2,8,16,128]{3,2,1,0:T(8,128)S(1)}, f32[2,8,16,128]{3,2,1,0:T(8,128)S(1)}, u32[]{:S(2)}, u32[]{:S(2)}) %collective-permute-start.2) | collective-permute-done | bytes 131104 | tf_op jit(solution)/shard_map/ppermute | solution.py:115
  164.2 10.3 %collective-permute-start.3 = (f32[2,4,16,128]{3,2,1,0:T(8,128)S(1)}, f32[2,4,16,128]{3,2,1,0:T(8,128)S(1)}, u32[]{:S(2)}, u32[]{:S(2)}) collective-permute-start(f32[2,4,16,128]{3,2,1,0:T(8,128)S(1)} %get-tuple-element.7), channel_id=1, source_target_pairs={{0,1},{1,2},{2,3},{3,4},{4,5},{5,6},{6,7},{7,8},{8,9},{9,10},{10,1... | collective-permute-start | bytes 196616 | tf_op jit(solution)/shard_map/ppermute | solution.py:26
  174.5 1.9 %collective-permute-start.4 = (f32[2,4,16,128]{3,2,1,0:T(8,128)S(1)}, f32[2,4,16,128]{3,2,1,0:T(8,128)S(1)}, u32[]{:S(2)}, u32[]{:S(2)}) collective-permute-start(f32[2,4,16,128]{3,2,1,0:T(8,128)S(1)} %get-tuple-element.8), channel_id=1, source_target_pairs={{1,0},{2,1},{3,2},{4,3},{5,4},{6,5},{7,6},{8,7},{9,8},{10,9},{11,1... | collective-permute-start | bytes 196616 | tf_op jit(solution)/shard_map/ppermute | solution.py:28
  176.4 0.0 collective-permute-done.3
  176.4 3.6 %collective-permute-done.4 = f32[2,4,16,128]{3,2,1,0:T(8,128)S(1)} collective-permute-done((f32[2,4,16,128]{3,2,1,0:T(8,128)S(1)}, f32[2,4,16,128]{3,2,1,0:T(8,128)S(1)}, u32[]{:S(2)}, u32[]{:S(2)}) %collective-permute-start.4) | collective-permute-done | bytes 65568 | tf_op jit(solution)/shard_map/ppermute | solution.py:28
  180.0 0.1 fusion.3
  180.1 0.1 fusion.28
  180.3 1.0 fusion.44
  (11 shorter events, 0.1 us)
Async XLA Ops:
  14.6 125.8 %all-to-all-start = ((bf16[128,304,128]{2,1,0:T(8,128)(2,1)}), bf16[128,304,128]{2,1,0:T(8,128)(2,1)}, u32[]{:S(2)}, u32[]{:S(2)}) async-start(bf16[128,304,128]{2,1,0:T(8,128)(2,1)} %shard_map.64), calls=%async_computation | async-start | bytes 19922944 | tf_op jit(solution)/shard_map/all_to_all | solution.py:171
  152.3 8.7 %collective-permute-start.1 = (f32[2,8,16,128]{3,2,1,0:T(8,128)S(1)}, f32[2,8,16,128]{3,2,1,0:T(8,128)S(1)}, u32[]{:S(2)}, u32[]{:S(2)}) collective-permute-start(f32[2,8,16,128]{3,2,1,0:T(8,128)S(1)} %reshape.174), channel_id=1, source_target_pairs={{0,64},{32,96},{64,0},{96,32},{1,65},{33,97},{65,1},{97,33},{2,66}... | collective-permute-start | bytes 393224 | tf_op jit(solution)/shard_map/ppermute | solution.py:115
  157.9 6.1 %collective-permute-start.2 = (f32[2,8,16,128]{3,2,1,0:T(8,128)S(1)}, f32[2,8,16,128]{3,2,1,0:T(8,128)S(1)}, u32[]{:S(2)}, u32[]{:S(2)}) collective-permute-start(f32[2,8,16,128]{3,2,1,0:T(8,128)S(1)} %reshape.174), channel_id=1, source_target_pairs={{0,96},{32,0},{64,32},{96,64},{1,97},{33,1},{65,33},{97,65},{2,98}... | collective-permute-start | bytes 393224 | tf_op jit(solution)/shard_map/ppermute | solution.py:115
  157.9 6.1 %collective-permute-start = (f32[2,8,16,128]{3,2,1,0:T(8,128)S(1)}, f32[2,8,16,128]{3,2,1,0:T(8,128)S(1)}, u32[]{:S(2)}, u32[]{:S(2)}) collective-permute-start(f32[2,8,16,128]{3,2,1,0:T(8,128)S(1)} %reshape.174), channel_id=1, source_target_pairs={{0,32},{32,64},{64,96},{96,0},{1,33},{33,65},{65,97},{97,1},{2,34}... | collective-permute-start | bytes 393224 | tf_op jit(solution)/shard_map/ppermute | solution.py:115
  164.2 12.2 %collective-permute-start.3 = (f32[2,4,16,128]{3,2,1,0:T(8,128)S(1)}, f32[2,4,16,128]{3,2,1,0:T(8,128)S(1)}, u32[]{:S(2)}, u32[]{:S(2)}) collective-permute-start(f32[2,4,16,128]{3,2,1,0:T(8,128)S(1)} %get-tuple-element.7), channel_id=1, source_target_pairs={{0,1},{1,2},{2,3},{3,4},{4,5},{5,6},{6,7},{7,8},{8,9},{9,10},{10,1... | collective-permute-start | bytes 196616 | tf_op jit(solution)/shard_map/ppermute | solution.py:26
  174.5 5.6 %collective-permute-start.4 = (f32[2,4,16,128]{3,2,1,0:T(8,128)S(1)}, f32[2,4,16,128]{3,2,1,0:T(8,128)S(1)}, u32[]{:S(2)}, u32[]{:S(2)}) collective-permute-start(f32[2,4,16,128]{3,2,1,0:T(8,128)S(1)} %get-tuple-element.8), channel_id=1, source_target_pairs={{1,0},{2,1},{3,2},{4,3},{5,4},{6,5},{7,6},{8,7},{9,8},{10,9},{11,1... | collective-permute-start | bytes 196616 | tf_op jit(solution)/shard_map/ppermute | solution.py:28

commit v9 on v8

--- a/solution.py
+++ b/solution.py
@@ -60,17 +60,25 @@
     return jnp.sum(jnp.where(hits, table[None, :], 0), axis=1)
 
 
-def pack_kernel(src_ref, pair_ref, fwd_ref, out_ref):
+def pack_kernel(src_ref, pair_ref, fwd_ref, out_ref, bricks_ref):
     dests = out_ref.shape[0]
-    rows = fwd_ref.shape[1] * fwd_ref.shape[2] // LANES
+    rows = bricks_ref.shape[1]
+    group = 16
     base = pl.program_id(0) * dests * 2
+
+    @pl.when(pl.program_id(0) == 0)
+    def _():
+        for start in range(0, bricks_ref.shape[0], group):
+            block = jnp.swapaxes(fwd_ref[:, start : start + group, :], 0, 1)
+            for j in range(group):
+                bricks_ref[start + j] = block[j].reshape(rows, LANES)
 
     def one_dest(d, carry):
         slot = base + 2 * d
         first = src_ref[slot]
         second = src_ref[slot + 1]
-        out_ref[d, 0:rows, :] = fwd_ref[jnp.maximum(first, 0)].reshape(rows, LANES)
-        out_ref[d, rows : 2 * rows, :] = fwd_ref[jnp.maximum(second, 0)].reshape(rows, LANES)
+        out_ref[d, 0:rows, :] = bricks_ref[jnp.maximum(first, 0)]
+        out_ref[d, rows : 2 * rows, :] = bricks_ref[jnp.maximum(second, 0)]
         lane_at = lax.broadcasted_iota(jnp.int32, (META, LANES), 1)
         tags = jnp.where(lane_at == 0, pair_ref[slot], pair_ref[slot + 1])
         out_ref[d, 2 * rows : 2 * rows + META, :] = tags.astype(jnp.float32).astype(out_ref.dtype)
@@ -162,11 +170,12 @@
         grid_spec=pltpu.PrefetchScalarGridSpec(
             num_scalar_prefetch=2,
             grid=(pack_steps,),
-            in_specs=[pl.BlockSpec((stored, channels, cells), lambda g, s, p: (0, 0, 0))],
+            in_specs=[pl.BlockSpec((channels, stored, cells), lambda g, s, p: (0, 0, 0))],
             out_specs=pl.BlockSpec((dests_per_step, chunk, LANES), lambda g, s, p: (g, 0, 0)),
+            scratch_shapes=[pltpu.VMEM((stored, rows, LANES), forward.dtype)],
         ),
         compiler_params=pltpu.CompilerParams(vmem_limit_bytes=48 * 1024 * 1024),
-    )(src_of_slot, pair_of_slot, forward)
+    )(src_of_slot, pair_of_slot, jnp.transpose(forward, (1, 0, 2)))
 
     arrived = lax.all_to_all(payload, ("src", "vol"), split_axis=0, concat_axis=0, tiled=True)
     tags = arrived[:, 2 * rows, 0:2].reshape(slot_total)

time: 183 us -> 180 us (0.984)
  local copies, waits for them, and re-layouts: 22.4 us -> 19.7 us
    unnamed x1 -> x2, local copies, waits for them, and re-layouts: 5.02 us -> 2.33 us
  transfers between devices with their start and end apart: 6 -> 6, of which waited for: 4 -> 3; matrix products, arithmetic and copies ran while one was open for 8% -> 8% of each run, Pallas kernels for 0% -> 0%
where the time goes in v9:
time: 180 us; the launch traced here: 179 us
  waiting for transfers between devices  108 us (60%)
  starting transfers between devices  30.4 us (17%)
  local copies, waits for them, and re-layouts  19.7 us (11%)
  Pallas kernels  15.2 us (8%)
  other arithmetic  4.83 us (3%)
    all_to_all x1, waiting for transfers between devices, local(): lax.all_to_all(payload, ('src', 'vol'), split_axis=0, concat_axis=0, tile...  101 us
    reshape x2, local copies, waits for them, and re-layouts, local(): jnp.transpose(adjoint, (0, 2, 1, 3))  13.8 us
    all_to_all x1, starting transfers between devices, local(): lax.all_to_all(payload, ('src', 'vol'), split_axis=0, concat_axis=0, tile...  10.8 us
    ppermute x1, starting transfers between devices, with_halo(): lax.ppermute(tail, axis, [(i, (i + 1) % count) for i in range(ends)])  9.95 us
    pallas_call x1, Pallas kernels, local(): pl.pallas_call(pack_kernel, out_shape=jax.ShapeDtypeStruct((devices, chun...  8.12 us
    ppermute x3, starting transfers between devices, src_sum(): lax.ppermute(part, 'src', [(i, (i + k) % count) for i in range(count)])  7.72 us
    pallas_call x1, Pallas kernels, local(): pl.pallas_call(correlate_kernel, out_shape=jax.ShapeDtypeStruct((slot_tot...  7.12 us
    ppermute x1, waiting for transfers between devices, with_halo(): lax.ppermute(head, axis, [((i + 1) % count, i) for i in range(ends)])  3.65 us
  transfers between devices with their start and end apart: 6, of which 3 were waited for; matrix products, arithmetic and copies ran while one was open for 8% of the time, Pallas kernels for 0%

profile of v9, /device:TPU:57, one launch (start us, length us, event | category | flops | bytes accessed | tf_op | source)
XLA Modules:
  0.0 179.0 jit_solution(4247984311919749885)
XLA Ops:
  0.0 0.9 select_reduce_fusion
  0.9 0.8 select_reduce_fusion.3
  1.7 0.2 convert_reduce_fusion
  1.9 0.1 fusion.54
  2.0 0.2 select_reduce_fusion.1
  2.1 0.0 copy-start
  2.2 2.3 %copy-done = bf16[128,36,512]{2,0,1:T(8,128)(2,1)S(1)} copy-done((bf16[128,36,512]{2,0,1:T(8,128)(2,1)S(1)}, bf16[128,36,512]{2,0,1:T(8,128)(2,1)}, u32[]{:S(2)}) %copy-start) | copy-done | bytes 4718616
  4.5 8.1 %shard_map.64 = bf16[128,304,128]{2,1,0:T(8,128)(2,1)} custom-call(s32[256]{0:T(256)S(1)} %get-tuple-element.12.src_ref, s32[256]{0:T(256)S(1)} %get-tuple-element.11.pair_ref, bf16[36,128,512]{2,1,0:T(8,128)(2,1)S(1)} %bitcast.28), custom_call_target="tpu_custom_call" | custom-call | tf_op jit(solution)/shard_map/pallas_call | solution.py:167
  12.6 10.8 %all-to-all-start = ((bf16[128,304,128]{2,1,0:T(8,128)(2,1)}), bf16[128,304,128]{2,1,0:T(8,128)(2,1)}, u32[]{:S(2)}, u32[]{:S(2)}) async-start(bf16[128,304,128]{2,1,0:T(8,128)(2,1)} %shard_map.64), calls=%async_computation | async-start | bytes 19922944 | tf_op jit(solution)/shard_map/all_to_all | solution.py:180
  23.4 7.7 %reshape.171 = bf16[4,36,32,4,128]{4,3,2,1,0:T(4,128)(2,1)} reshape(bf16[4,36,32,512]{3,2,1,0:T(8,128)(2,1)} %bitcast.30) | data formatting | bytes 9437184 | tf_op jit(solution)/shard_map/reshape | solution.py:185
  31.1 6.1 %copy.13 = bf16[4,36,32,4,128]{4,3,1,2,0:T(4,128)(2,1)} copy(bf16[4,36,32,4,128]{4,3,2,1,0:T(4,128)(2,1)} %reshape.171) | data formatting | bytes 9437184 | tf_op jit(solution)/shard_map/reshape | solution.py:185
  37.2 101.2 %all-to-all-done.arrived_ref = bf16[128,304,128]{2,1,0:T(8,128)(2,1)} async-done(((bf16[128,304,128]{2,1,0:T(8,128)(2,1)}), bf16[128,304,128]{2,1,0:T(8,128)(2,1)}, u32[]{:S(2)}, u32[]{:S(2)}) %all-to-all-start) | async-done | bytes 9961504 | tf_op jit(solution)/shard_map/all_to_all | solution.py:180
  138.4 1.2 fusion.56
  139.6 0.1 convert_element_type.27.pair_ref
  139.8 7.1 %shard_map.65 = f32[256,2,8,128]{3,2,1,0:T(8,128)S(1)} custom-call(s32[256]{0:T(256)S(1)} %convert_element_type.27.pair_ref, bf16[128,304,128]{2,1,0:T(8,128)(2,1)} %all-to-all-done.arrived_ref, bf16[4,32,144,128]{3,2,1,0:T(8,128)(2,1)} %bitcast.29), custom_call_target="tpu_custom_call" | custom-call | tf_op jit(solution)/shard_map/pallas_call | solution.py:188
  146.9 0.2 slice_subtract_fusion
  147.1 0.4 reshape.173
  147.6 0.3 copy.14
  147.9 0.7 convolution_bitcast_fusion
  148.6 0.6 copy.15
  149.2 1.0 reshape.174
  150.2 0.3 collective-permute-start
  150.5 5.5 %collective-permute-start.1 = (f32[2,8,16,128]{3,2,1,0:T(8,128)S(1)}, f32[2,8,16,128]{3,2,1,0:T(8,128)S(1)}, u32[]{:S(2)}, u32[]{:S(2)}) collective-permute-start(f32[2,8,16,128]{3,2,1,0:T(8,128)S(1)} %reshape.174), channel_id=1, source_target_pairs={{0,64},{32,96},{64,0},{96,32},{1,65},{33,97},{65,1},{97,33},{2,66}... | collective-permute-start | bytes 393224 | tf_op jit(solution)/shard_map/ppermute | solution.py:123
  156.0 2.0 %collective-permute-start.2 = (f32[2,8,16,128]{3,2,1,0:T(8,128)S(1)}, f32[2,8,16,128]{3,2,1,0:T(8,128)S(1)}, u32[]{:S(2)}, u32[]{:S(2)}) collective-permute-start(f32[2,8,16,128]{3,2,1,0:T(8,128)S(1)} %reshape.174), channel_id=1, source_target_pairs={{0,96},{32,0},{64,32},{96,64},{1,97},{33,1},{65,33},{97,65},{2,98}... | collective-permute-start | bytes 393224 | tf_op jit(solution)/shard_map/ppermute | solution.py:123
  158.0 1.0 stack_reshape.3
  159.0 3.1 %collective-permute-done.2 = f32[2,8,16,128]{3,2,1,0:T(8,128)S(1)} collective-permute-done((f32[2,8,16,128]{3,2,1,0:T(8,128)S(1)}, f32[2,8,16,128]{3,2,1,0:T(8,128)S(1)}, u32[]{:S(2)}, u32[]{:S(2)}) %collective-permute-start.2) | collective-permute-done | bytes 131104 | tf_op jit(solution)/shard_map/ppermute | solution.py:123
  162.2 10.0 %collective-permute-start.3 = (f32[2,4,16,128]{3,2,1,0:T(8,128)S(1)}, f32[2,4,16,128]{3,2,1,0:T(8,128)S(1)}, u32[]{:S(2)}, u32[]{:S(2)}) collective-permute-start(f32[2,4,16,128]{3,2,1,0:T(8,128)S(1)} %get-tuple-element.7), channel_id=1, source_target_pairs={{0,1},{1,2},{2,3},{3,4},{4,5},{5,6},{6,7},{7,8},{8,9},{9,10},{10,1... | collective-permute-start | bytes 196616 | tf_op jit(solution)/shard_map/ppermute | solution.py:26
  172.2 1.9 %collective-permute-start.4 = (f32[2,4,16,128]{3,2,1,0:T(8,128)S(1)}, f32[2,4,16,128]{3,2,1,0:T(8,128)S(1)}, u32[]{:S(2)}, u32[]{:S(2)}) collective-permute-start(f32[2,4,16,128]{3,2,1,0:T(8,128)S(1)} %get-tuple-element.8), channel_id=1, source_target_pairs={{1,0},{2,1},{3,2},{4,3},{5,4},{6,5},{7,6},{8,7},{9,8},{10,9},{11,1... | collective-permute-start | bytes 196616 | tf_op jit(solution)/shard_map/ppermute | solution.py:28
  174.1 3.6 %collective-permute-done.4 = f32[2,4,16,128]{3,2,1,0:T(8,128)S(1)} collective-permute-done((f32[2,4,16,128]{3,2,1,0:T(8,128)S(1)}, f32[2,4,16,128]{3,2,1,0:T(8,128)S(1)}, u32[]{:S(2)}, u32[]{:S(2)}) %collective-permute-start.4) | collective-permute-done | bytes 65568 | tf_op jit(solution)/shard_map/ppermute | solution.py:28
  177.8 0.1 fusion.3
  177.9 0.1 fusion.28
  178.0 1.0 fusion.44
  (12 shorter events, 0.1 us)
Async XLA Ops:
  2.1 2.3 %copy-start = (bf16[128,36,512]{2,0,1:T(8,128)(2,1)S(1)}, bf16[128,36,512]{2,0,1:T(8,128)(2,1)}, u32[]{:S(2)}) copy-start(bf16[128,36,512]{2,0,1:T(8,128)(2,1)} %param.6) | copy-start | bytes 14155780
  12.6 125.8 %all-to-all-start = ((bf16[128,304,128]{2,1,0:T(8,128)(2,1)}), bf16[128,304,128]{2,1,0:T(8,128)(2,1)}, u32[]{:S(2)}, u32[]{:S(2)}) async-start(bf16[128,304,128]{2,1,0:T(8,128)(2,1)} %shard_map.64), calls=%async_computation | async-start | bytes 19922944 | tf_op jit(solution)/shard_map/all_to_all | solution.py:180
  150.2 8.8 %collective-permute-start = (f32[2,8,16,128]{3,2,1,0:T(8,128)S(1)}, f32[2,8,16,128]{3,2,1,0:T(8,128)S(1)}, u32[]{:S(2)}, u32[]{:S(2)}) collective-permute-start(f32[2,8,16,128]{3,2,1,0:T(8,128)S(1)} %reshape.174), channel_id=1, source_target_pairs={{0,32},{32,64},{64,96},{96,0},{1,33},{33,65},{65,97},{97,1},{2,34}... | collective-permute-start | bytes 393224 | tf_op jit(solution)/shard_map/ppermute | solution.py:123
  150.5 8.5 %collective-permute-start.1 = (f32[2,8,16,128]{3,2,1,0:T(8,128)S(1)}, f32[2,8,16,128]{3,2,1,0:T(8,128)S(1)}, u32[]{:S(2)}, u32[]{:S(2)}) collective-permute-start(f32[2,8,16,128]{3,2,1,0:T(8,128)S(1)} %reshape.174), channel_id=1, source_target_pairs={{0,64},{32,96},{64,0},{96,32},{1,65},{33,97},{65,1},{97,33},{2,66}... | collective-permute-start | bytes 393224 | tf_op jit(solution)/shard_map/ppermute | solution.py:123
  156.0 6.1 %collective-permute-start.2 = (f32[2,8,16,128]{3,2,1,0:T(8,128)S(1)}, f32[2,8,16,128]{3,2,1,0:T(8,128)S(1)}, u32[]{:S(2)}, u32[]{:S(2)}) collective-permute-start(f32[2,8,16,128]{3,2,1,0:T(8,128)S(1)} %reshape.174), channel_id=1, source_target_pairs={{0,96},{32,0},{64,32},{96,64},{1,97},{33,1},{65,33},{97,65},{2,98}... | collective-permute-start | bytes 393224 | tf_op jit(solution)/shard_map/ppermute | solution.py:123
  162.2 11.9 %collective-permute-start.3 = (f32[2,4,16,128]{3,2,1,0:T(8,128)S(1)}, f32[2,4,16,128]{3,2,1,0:T(8,128)S(1)}, u32[]{:S(2)}, u32[]{:S(2)}) collective-permute-start(f32[2,4,16,128]{3,2,1,0:T(8,128)S(1)} %get-tuple-element.7), channel_id=1, source_target_pairs={{0,1},{1,2},{2,3},{3,4},{4,5},{5,6},{6,7},{7,8},{8,9},{9,10},{10,1... | collective-permute-start | bytes 196616 | tf_op jit(solution)/shard_map/ppermute | solution.py:26
  172.2 5.6 %collective-permute-start.4 = (f32[2,4,16,128]{3,2,1,0:T(8,128)S(1)}, f32[2,4,16,128]{3,2,1,0:T(8,128)S(1)}, u32[]{:S(2)}, u32[]{:S(2)}) collective-permute-start(f32[2,4,16,128]{3,2,1,0:T(8,128)S(1)} %get-tuple-element.8), channel_id=1, source_target_pairs={{1,0},{2,1},{3,2},{4,3},{5,4},{6,5},{7,6},{8,7},{9,8},{10,9},{11,1... | collective-permute-start | bytes 196616 | tf_op jit(solution)/shard_map/ppermute | solution.py:28

commit v10 on v9

--- a/solution.py
+++ b/solution.py
@@ -84,7 +84,7 @@
         out_ref[d, 2 * rows : 2 * rows + META, :] = tags.astype(jnp.float32).astype(out_ref.dtype)
         return carry
 
-    lax.fori_loop(0, dests, one_dest, 0)
+    lax.fori_loop(0, dests, one_dest, 0, unroll=True)
 
 
 def correlate_kernel(pair_ref, arrived_ref, adj_ref, out_ref):

time: 180 us -> 180 us (level)
  no operation moved by 1% of the time
where the time goes in v10:
time: 180 us; the launch traced here: 179 us
  waiting for transfers between devices  108 us (60%)
  starting transfers between devices  30.4 us (17%)
  local copies, waits for them, and re-layouts  19.7 us (11%)
  Pallas kernels  14.8 us (8%)
  other arithmetic  4.83 us (3%)
    all_to_all x1, waiting for transfers between devices, local(): lax.all_to_all(payload, ('src', 'vol'), split_axis=0, concat_axis=0, tile...  101 us
    reshape x2, local copies, waits for them, and re-layouts, local(): jnp.transpose(adjoint, (0, 2, 1, 3))  13.8 us
    all_to_all x1, starting transfers between devices, local(): lax.all_to_all(payload, ('src', 'vol'), split_axis=0, concat_axis=0, tile...  10.8 us
    ppermute x1, starting transfers between devices, with_halo(): lax.ppermute(tail, axis, [(i, (i + 1) % count) for i in range(ends)])  9.95 us
    ppermute x3, starting transfers between devices, src_sum(): lax.ppermute(part, 'src', [(i, (i + k) % count) for i in range(count)])  7.72 us
    pallas_call x1, Pallas kernels, local(): pl.pallas_call(pack_kernel, out_shape=jax.ShapeDtypeStruct((devices, chun...  7.65 us
    pallas_call x1, Pallas kernels, local(): pl.pallas_call(correlate_kernel, out_shape=jax.ShapeDtypeStruct((slot_tot...  7.12 us
    ppermute x1, waiting for transfers between devices, with_halo(): lax.ppermute(head, axis, [((i + 1) % count, i) for i in range(ends)])  3.65 us
  transfers between devices with their start and end apart: 6, of which 3 were waited for; matrix products, arithmetic and copies ran while one was open for 8% of the time, Pallas kernels for 0%

profile of v10, /device:TPU:57, one launch (start us, length us, event | category | flops | bytes accessed | tf_op | source)
XLA Modules:
  0.0 178.5 jit_solution(14212809393402003371)
XLA Ops:
  0.0 0.9 select_reduce_fusion
  0.9 0.8 select_reduce_fusion.3
  1.7 0.2 convert_reduce_fusion
  1.9 0.1 fusion.54
  2.0 0.2 select_reduce_fusion.1
  2.1 0.0 copy-start
  2.2 2.3 %copy-done = bf16[128,36,512]{2,0,1:T(8,128)(2,1)S(1)} copy-done((bf16[128,36,512]{2,0,1:T(8,128)(2,1)S(1)}, bf16[128,36,512]{2,0,1:T(8,128)(2,1)}, u32[]{:S(2)}) %copy-start) | copy-done | bytes 4718616
  4.5 7.7 %shard_map.64 = bf16[128,304,128]{2,1,0:T(8,128)(2,1)} custom-call(s32[256]{0:T(256)S(1)} %get-tuple-element.12.src_ref, s32[256]{0:T(256)S(1)} %get-tuple-element.11.pair_ref, bf16[36,128,512]{2,1,0:T(8,128)(2,1)S(1)} %bitcast.28), custom_call_target="tpu_custom_call" | custom-call | tf_op jit(solution)/shard_map/pallas_call | solution.py:167
  12.1 10.8 %all-to-all-start = ((bf16[128,304,128]{2,1,0:T(8,128)(2,1)}), bf16[128,304,128]{2,1,0:T(8,128)(2,1)}, u32[]{:S(2)}, u32[]{:S(2)}) async-start(bf16[128,304,128]{2,1,0:T(8,128)(2,1)} %shard_map.64), calls=%async_computation | async-start | bytes 19922944 | tf_op jit(solution)/shard_map/all_to_all | solution.py:180
  22.9 7.7 %reshape.171 = bf16[4,36,32,4,128]{4,3,2,1,0:T(4,128)(2,1)} reshape(bf16[4,36,32,512]{3,2,1,0:T(8,128)(2,1)} %bitcast.30) | data formatting | bytes 9437184 | tf_op jit(solution)/shard_map/reshape | solution.py:185
  30.7 6.1 %copy.13 = bf16[4,36,32,4,128]{4,3,1,2,0:T(4,128)(2,1)} copy(bf16[4,36,32,4,128]{4,3,2,1,0:T(4,128)(2,1)} %reshape.171) | data formatting | bytes 9437184 | tf_op jit(solution)/shard_map/reshape | solution.py:185
  36.8 101.2 %all-to-all-done.arrived_ref = bf16[128,304,128]{2,1,0:T(8,128)(2,1)} async-done(((bf16[128,304,128]{2,1,0:T(8,128)(2,1)}), bf16[128,304,128]{2,1,0:T(8,128)(2,1)}, u32[]{:S(2)}, u32[]{:S(2)}) %all-to-all-start) | async-done | bytes 9961504 | tf_op jit(solution)/shard_map/all_to_all | solution.py:180
  138.0 1.2 fusion.56
  139.1 0.1 convert_element_type.27.pair_ref
  139.3 7.1 %shard_map.65 = f32[256,2,8,128]{3,2,1,0:T(8,128)S(1)} custom-call(s32[256]{0:T(256)S(1)} %convert_element_type.27.pair_ref, bf16[128,304,128]{2,1,0:T(8,128)(2,1)} %all-to-all-done.arrived_ref, bf16[4,32,144,128]{3,2,1,0:T(8,128)(2,1)} %bitcast.29), custom_call_target="tpu_custom_call" | custom-call | tf_op jit(solution)/shard_map/pallas_call | solution.py:188
  146.4 0.2 slice_subtract_fusion
  146.7 0.4 reshape.173
  147.1 0.3 copy.14
  147.4 0.7 convolution_bitcast_fusion
  148.1 0.6 copy.15
  148.7 1.0 reshape.174
  149.8 0.3 collective-permute-start
  150.0 5.5 %collective-permute-start.1 = (f32[2,8,16,128]{3,2,1,0:T(8,128)S(1)}, f32[2,8,16,128]{3,2,1,0:T(8,128)S(1)}, u32[]{:S(2)}, u32[]{:S(2)}) collective-permute-start(f32[2,8,16,128]{3,2,1,0:T(8,128)S(1)} %reshape.174), channel_id=1, source_target_pairs={{0,64},{32,96},{64,0},{96,32},{1,65},{33,97},{65,1},{97,33},{2,66}... | collective-permute-start | bytes 393224 | tf_op jit(solution)/shard_map/ppermute | solution.py:123
  155.5 2.0 %collective-permute-start.2 = (f32[2,8,16,128]{3,2,1,0:T(8,128)S(1)}, f32[2,8,16,128]{3,2,1,0:T(8,128)S(1)}, u32[]{:S(2)}, u32[]{:S(2)}) collective-permute-start(f32[2,8,16,128]{3,2,1,0:T(8,128)S(1)} %reshape.174), channel_id=1, source_target_pairs={{0,96},{32,0},{64,32},{96,64},{1,97},{33,1},{65,33},{97,65},{2,98}... | collective-permute-start | bytes 393224 | tf_op jit(solution)/shard_map/ppermute | solution.py:123
  157.5 1.0 stack_reshape.3
  158.6 3.1 %collective-permute-done.2 = f32[2,8,16,128]{3,2,1,0:T(8,128)S(1)} collective-permute-done((f32[2,8,16,128]{3,2,1,0:T(8,128)S(1)}, f32[2,8,16,128]{3,2,1,0:T(8,128)S(1)}, u32[]{:S(2)}, u32[]{:S(2)}) %collective-permute-start.2) | collective-permute-done | bytes 131104 | tf_op jit(solution)/shard_map/ppermute | solution.py:123
  161.8 10.0 %collective-permute-start.3 = (f32[2,4,16,128]{3,2,1,0:T(8,128)S(1)}, f32[2,4,16,128]{3,2,1,0:T(8,128)S(1)}, u32[]{:S(2)}, u32[]{:S(2)}) collective-permute-start(f32[2,4,16,128]{3,2,1,0:T(8,128)S(1)} %get-tuple-element.7), channel_id=1, source_target_pairs={{0,1},{1,2},{2,3},{3,4},{4,5},{5,6},{6,7},{7,8},{8,9},{9,10},{10,1... | collective-permute-start | bytes 196616 | tf_op jit(solution)/shard_map/ppermute | solution.py:26
  171.7 1.9 %collective-permute-start.4 = (f32[2,4,16,128]{3,2,1,0:T(8,128)S(1)}, f32[2,4,16,128]{3,2,1,0:T(8,128)S(1)}, u32[]{:S(2)}, u32[]{:S(2)}) collective-permute-start(f32[2,4,16,128]{3,2,1,0:T(8,128)S(1)} %get-tuple-element.8), channel_id=1, source_target_pairs={{1,0},{2,1},{3,2},{4,3},{5,4},{6,5},{7,6},{8,7},{9,8},{10,9},{11,1... | collective-permute-start | bytes 196616 | tf_op jit(solution)/shard_map/ppermute | solution.py:28
  173.7 3.6 %collective-permute-done.4 = f32[2,4,16,128]{3,2,1,0:T(8,128)S(1)} collective-permute-done((f32[2,4,16,128]{3,2,1,0:T(8,128)S(1)}, f32[2,4,16,128]{3,2,1,0:T(8,128)S(1)}, u32[]{:S(2)}, u32[]{:S(2)}) %collective-permute-start.4) | collective-permute-done | bytes 65568 | tf_op jit(solution)/shard_map/ppermute | solution.py:28
  177.3 0.1 fusion.3
  177.4 0.1 fusion.28
  177.5 1.0 fusion.44
  (12 shorter events, 0.1 us)
Async XLA Ops:
  2.1 2.3 %copy-start = (bf16[128,36,512]{2,0,1:T(8,128)(2,1)S(1)}, bf16[128,36,512]{2,0,1:T(8,128)(2,1)}, u32[]{:S(2)}) copy-start(bf16[128,36,512]{2,0,1:T(8,128)(2,1)} %param.6) | copy-start | bytes 14155780
  12.1 125.8 %all-to-all-start = ((bf16[128,304,128]{2,1,0:T(8,128)(2,1)}), bf16[128,304,128]{2,1,0:T(8,128)(2,1)}, u32[]{:S(2)}, u32[]{:S(2)}) async-start(bf16[128,304,128]{2,1,0:T(8,128)(2,1)} %shard_map.64), calls=%async_computation | async-start | bytes 19922944 | tf_op jit(solution)/shard_map/all_to_all | solution.py:180
  149.8 8.8 %collective-permute-start = (f32[2,8,16,128]{3,2,1,0:T(8,128)S(1)}, f32[2,8,16,128]{3,2,1,0:T(8,128)S(1)}, u32[]{:S(2)}, u32[]{:S(2)}) collective-permute-start(f32[2,8,16,128]{3,2,1,0:T(8,128)S(1)} %reshape.174), channel_id=1, source_target_pairs={{0,32},{32,64},{64,96},{96,0},{1,33},{33,65},{65,97},{97,1},{2,34}... | collective-permute-start | bytes 393224 | tf_op jit(solution)/shard_map/ppermute | solution.py:123
  150.0 8.5 %collective-permute-start.1 = (f32[2,8,16,128]{3,2,1,0:T(8,128)S(1)}, f32[2,8,16,128]{3,2,1,0:T(8,128)S(1)}, u32[]{:S(2)}, u32[]{:S(2)}) collective-permute-start(f32[2,8,16,128]{3,2,1,0:T(8,128)S(1)} %reshape.174), channel_id=1, source_target_pairs={{0,64},{32,96},{64,0},{96,32},{1,65},{33,97},{65,1},{97,33},{2,66}... | collective-permute-start | bytes 393224 | tf_op jit(solution)/shard_map/ppermute | solution.py:123
  155.5 6.1 %collective-permute-start.2 = (f32[2,8,16,128]{3,2,1,0:T(8,128)S(1)}, f32[2,8,16,128]{3,2,1,0:T(8,128)S(1)}, u32[]{:S(2)}, u32[]{:S(2)}) collective-permute-start(f32[2,8,16,128]{3,2,1,0:T(8,128)S(1)} %reshape.174), channel_id=1, source_target_pairs={{0,96},{32,0},{64,32},{96,64},{1,97},{33,1},{65,33},{97,65},{2,98}... | collective-permute-start | bytes 393224 | tf_op jit(solution)/shard_map/ppermute | solution.py:123
  161.8 11.9 %collective-permute-start.3 = (f32[2,4,16,128]{3,2,1,0:T(8,128)S(1)}, f32[2,4,16,128]{3,2,1,0:T(8,128)S(1)}, u32[]{:S(2)}, u32[]{:S(2)}) collective-permute-start(f32[2,4,16,128]{3,2,1,0:T(8,128)S(1)} %get-tuple-element.7), channel_id=1, source_target_pairs={{0,1},{1,2},{2,3},{3,4},{4,5},{5,6},{6,7},{7,8},{8,9},{9,10},{10,1... | collective-permute-start | bytes 196616 | tf_op jit(solution)/shard_map/ppermute | solution.py:26
  171.7 5.6 %collective-permute-start.4 = (f32[2,4,16,128]{3,2,1,0:T(8,128)S(1)}, f32[2,4,16,128]{3,2,1,0:T(8,128)S(1)}, u32[]{:S(2)}, u32[]{:S(2)}) collective-permute-start(f32[2,4,16,128]{3,2,1,0:T(8,128)S(1)} %get-tuple-element.8), channel_id=1, source_target_pairs={{1,0},{2,1},{3,2},{4,3},{5,4},{6,5},{7,6},{8,7},{9,8},{10,9},{11,1... | collective-permute-start | bytes 196616 | tf_op jit(solution)/shard_map/ppermute | solution.py:28

commit v11 on v10

--- a/solution.py
+++ b/solution.py
@@ -118,15 +118,11 @@
 
 def src_sum(part):
     count = lax.axis_size("src")
-    me = lax.axis_index("src")
-    parts = [part] + [
-        lax.ppermute(part, "src", [(i, (i + k) % count) for i in range(count)])
-        for k in range(1, count)
-    ]
-    stacked = jnp.stack(parts)
-    total = lax.dynamic_index_in_dim(stacked, me % count, keepdims=False)
-    for j in range(1, count):
-        total = total + lax.dynamic_index_in_dim(stacked, (me - j) % count, keepdims=False)
+    total = part
+    step = 1
+    while step < count:
+        total = total + lax.ppermute(total, "src", [(i, i ^ step) for i in range(count)])
+        step *= 2
     return total
 
 

time: 180 us -> 181 us (level)
  waiting for transfers between devices: 108 us -> 110 us
    ppermute x3 -> x2, waiting for transfers between devices: 3.11 us -> 5.16 us  [src_sum(): lax.ppermute(total, 'src', [(i, i ^ step) for i in range(count)])]
    ppermute x3 -> x2, starting transfers between devices: 7.72 us -> 7.06 us  [src_sum(): lax.ppermute(total, 'src', [(i, i ^ step) for i in range(count)])]
  transfers between devices with their start and end apart: 6 -> 5, of which waited for: 3 -> 4; matrix products, arithmetic and copies ran while one was open for 8% -> 8% of each run, Pallas kernels for 0% -> 0%
where the time goes in v11:
time: 181 us; the launch traced here: 179 us
  waiting for transfers between devices  110 us (61%)
  starting transfers between devices  29.5 us (16%)
  local copies, waits for them, and re-layouts  18.7 us (10%)
  Pallas kernels  14.8 us (8%)
  other arithmetic  4.79 us (3%)
    all_to_all x1, waiting for transfers between devices, local(): lax.all_to_all(payload, ('src', 'vol'), split_axis=0, concat_axis=0, tile...  101 us
    reshape x2, local copies, waits for them, and re-layouts, local(): jnp.transpose(adjoint, (0, 2, 1, 3))  13.8 us
    all_to_all x1, starting transfers between devices, local(): lax.all_to_all(payload, ('src', 'vol'), split_axis=0, concat_axis=0, tile...  10.8 us
    ppermute x1, starting transfers between devices, with_halo(): lax.ppermute(tail, axis, [(i, (i + 1) % count) for i in range(ends)])  9.72 us
    pallas_call x1, Pallas kernels, local(): pl.pallas_call(pack_kernel, out_shape=jax.ShapeDtypeStruct((devices, chun...  7.65 us
    pallas_call x1, Pallas kernels, local(): pl.pallas_call(correlate_kernel, out_shape=jax.ShapeDtypeStruct((slot_tot...  7.13 us
    ppermute x2, starting transfers between devices, src_sum(): lax.ppermute(total, 'src', [(i, i ^ step) for i in range(count)])  7.06 us
    ppermute x2, waiting for transfers between devices, src_sum(): lax.ppermute(total, 'src', [(i, i ^ step) for i in range(count)])  5.16 us
  transfers between devices with their start and end apart: 5, of which 4 were waited for; matrix products, arithmetic and copies ran while one was open for 8% of the time, Pallas kernels for 0%

profile of v11, /device:TPU:57, one launch (start us, length us, event | category | flops | bytes accessed | tf_op | source)
XLA Modules:
  0.0 178.6 jit_solution(18202863920596911734)
XLA Ops:
  0.0 0.9 select_reduce_fusion
  0.9 0.8 select_reduce_fusion.3
  1.7 0.2 convert_reduce_fusion
  1.9 0.1 fusion.54
  2.0 0.2 select_reduce_fusion.1
  2.1 0.0 copy-start
  2.2 2.3 %copy-done = bf16[128,36,512]{2,0,1:T(8,128)(2,1)S(1)} copy-done((bf16[128,36,512]{2,0,1:T(8,128)(2,1)S(1)}, bf16[128,36,512]{2,0,1:T(8,128)(2,1)}, u32[]{:S(2)}) %copy-start) | copy-done | bytes 4718616
  4.5 7.7 %shard_map.64 = bf16[128,304,128]{2,1,0:T(8,128)(2,1)} custom-call(s32[256]{0:T(256)S(1)} %get-tuple-element.12.src_ref, s32[256]{0:T(256)S(1)} %get-tuple-element.11.pair_ref, bf16[36,128,512]{2,1,0:T(8,128)(2,1)S(1)} %bitcast.21), custom_call_target="tpu_custom_call" | custom-call | tf_op jit(solution)/shard_map/pallas_call | solution.py:163
  12.1 10.8 %all-to-all-start = ((bf16[128,304,128]{2,1,0:T(8,128)(2,1)}), bf16[128,304,128]{2,1,0:T(8,128)(2,1)}, u32[]{:S(2)}, u32[]{:S(2)}) async-start(bf16[128,304,128]{2,1,0:T(8,128)(2,1)} %shard_map.64), calls=%async_computation | async-start | bytes 19922944 | tf_op jit(solution)/shard_map/all_to_all | solution.py:176
  22.9 7.7 %reshape.168 = bf16[4,36,32,4,128]{4,3,2,1,0:T(4,128)(2,1)} reshape(bf16[4,36,32,512]{3,2,1,0:T(8,128)(2,1)} %bitcast.23) | data formatting | bytes 9437184 | tf_op jit(solution)/shard_map/reshape | solution.py:181
  30.7 6.1 %copy.12 = bf16[4,36,32,4,128]{4,3,1,2,0:T(4,128)(2,1)} copy(bf16[4,36,32,4,128]{4,3,2,1,0:T(4,128)(2,1)} %reshape.168) | data formatting | bytes 9437184 | tf_op jit(solution)/shard_map/reshape | solution.py:181
  36.8 101.2 %all-to-all-done.arrived_ref = bf16[128,304,128]{2,1,0:T(8,128)(2,1)} async-done(((bf16[128,304,128]{2,1,0:T(8,128)(2,1)}), bf16[128,304,128]{2,1,0:T(8,128)(2,1)}, u32[]{:S(2)}, u32[]{:S(2)}) %all-to-all-start) | async-done | bytes 9961504 | tf_op jit(solution)/shard_map/all_to_all | solution.py:176
  138.0 1.2 fusion.56
  139.1 0.1 convert_element_type.27.pair_ref
  139.3 7.1 %shard_map.65 = f32[256,2,8,128]{3,2,1,0:T(8,128)S(1)} custom-call(s32[256]{0:T(256)S(1)} %convert_element_type.27.pair_ref, bf16[128,304,128]{2,1,0:T(8,128)(2,1)} %all-to-all-done.arrived_ref, bf16[4,32,144,128]{3,2,1,0:T(8,128)(2,1)} %bitcast.22), custom_call_target="tpu_custom_call" | custom-call | tf_op jit(solution)/shard_map/pallas_call | solution.py:184
  146.4 0.2 slice_subtract_fusion
  146.7 0.4 reshape.170
  147.1 0.3 copy.13
  147.4 0.7 convolution_bitcast_fusion
  148.1 0.6 copy.14
  148.8 1.0 reshape.171
  149.8 1.4 collective-permute-start
  151.2 2.8 %collective-permute-done = f32[2,8,16,128]{3,2,1,0:T(8,128)S(1)} collective-permute-done((f32[2,8,16,128]{3,2,1,0:T(8,128)S(1)}, f32[2,8,16,128]{3,2,1,0:T(8,128)S(1)}, u32[]{:S(2)}, u32[]{:S(2)}) %collective-permute-start) | collective-permute-done | bytes 131104 | tf_op jit(solution)/shard_map/ppermute | solution.py:124
  154.0 5.6 %collective-permute-start.1 = (f32[2,8,16,128]{3,2,1,0:T(8,128)S(1)}, f32[2,8,16,128]{3,2,1,0:T(8,128)S(1)}, u32[]{:S(2)}, u32[]{:S(2)}) collective-permute-start(f32[2,8,16,128]{3,2,1,0:T(8,128)S(1)} %add.172), channel_id=1, source_target_pairs={{0,64},{32,96},{64,0},{96,32},{1,65},{33,97},{65,1},{97,33},{2,66}... | collective-permute-start | bytes 393224 | tf_op jit(solution)/shard_map/ppermute | solution.py:124
  159.7 2.4 %collective-permute-done.1 = f32[2,8,16,128]{3,2,1,0:T(8,128)S(1)} collective-permute-done((f32[2,8,16,128]{3,2,1,0:T(8,128)S(1)}, f32[2,8,16,128]{3,2,1,0:T(8,128)S(1)}, u32[]{:S(2)}, u32[]{:S(2)}) %collective-permute-start.1) | collective-permute-done | bytes 131104 | tf_op jit(solution)/shard_map/ppermute | solution.py:124
  162.1 9.7 %collective-permute-start.2 = (f32[2,4,16,128]{3,2,1,0:T(8,128)S(1)}, f32[2,4,16,128]{3,2,1,0:T(8,128)S(1)}, u32[]{:S(2)}, u32[]{:S(2)}) collective-permute-start(f32[2,4,16,128]{3,2,1,0:T(8,128)S(1)} %get-tuple-element.7), channel_id=1, source_target_pairs={{0,1},{1,2},{2,3},{3,4},{4,5},{5,6},{6,7},{7,8},{8,9},{9,10},{10,1... | collective-permute-start | bytes 196616 | tf_op jit(solution)/shard_map/ppermute | solution.py:26
  171.8 1.9 %collective-permute-start.3 = (f32[2,4,16,128]{3,2,1,0:T(8,128)S(1)}, f32[2,4,16,128]{3,2,1,0:T(8,128)S(1)}, u32[]{:S(2)}, u32[]{:S(2)}) collective-permute-start(f32[2,4,16,128]{3,2,1,0:T(8,128)S(1)} %get-tuple-element.8), channel_id=1, source_target_pairs={{1,0},{2,1},{3,2},{4,3},{5,4},{6,5},{7,6},{8,7},{9,8},{10,9},{11,1... | collective-permute-start | bytes 196616 | tf_op jit(solution)/shard_map/ppermute | solution.py:28
  173.7 0.0 collective-permute-done.2
  173.8 3.6 %collective-permute-done.3 = f32[2,4,16,128]{3,2,1,0:T(8,128)S(1)} collective-permute-done((f32[2,4,16,128]{3,2,1,0:T(8,128)S(1)}, f32[2,4,16,128]{3,2,1,0:T(8,128)S(1)}, u32[]{:S(2)}, u32[]{:S(2)}) %collective-permute-start.3) | collective-permute-done | bytes 65568 | tf_op jit(solution)/shard_map/ppermute | solution.py:28
  177.4 0.1 fusion.3
  177.5 0.1 fusion.28
  177.6 1.0 fusion.44
  (9 shorter events, 0.1 us)
Async XLA Ops:
  2.1 2.3 %copy-start = (bf16[128,36,512]{2,0,1:T(8,128)(2,1)S(1)}, bf16[128,36,512]{2,0,1:T(8,128)(2,1)}, u32[]{:S(2)}) copy-start(bf16[128,36,512]{2,0,1:T(8,128)(2,1)} %param.6) | copy-start | bytes 14155780
  12.1 125.8 %all-to-all-start = ((bf16[128,304,128]{2,1,0:T(8,128)(2,1)}), bf16[128,304,128]{2,1,0:T(8,128)(2,1)}, u32[]{:S(2)}, u32[]{:S(2)}) async-start(bf16[128,304,128]{2,1,0:T(8,128)(2,1)} %shard_map.64), calls=%async_computation | async-start | bytes 19922944 | tf_op jit(solution)/shard_map/all_to_all | solution.py:176
  149.8 4.2 %collective-permute-start = (f32[2,8,16,128]{3,2,1,0:T(8,128)S(1)}, f32[2,8,16,128]{3,2,1,0:T(8,128)S(1)}, u32[]{:S(2)}, u32[]{:S(2)}) collective-permute-start(f32[2,8,16,128]{3,2,1,0:T(8,128)S(1)} %reshape.171), channel_id=1, source_target_pairs={{0,32},{32,0},{64,96},{96,64},{1,33},{33,1},{65,97},{97,65},{2,34}... | collective-permute-start | bytes 393224 | tf_op jit(solution)/shard_map/ppermute | solution.py:124
  154.0 8.0 %collective-permute-start.1 = (f32[2,8,16,128]{3,2,1,0:T(8,128)S(1)}, f32[2,8,16,128]{3,2,1,0:T(8,128)S(1)}, u32[]{:S(2)}, u32[]{:S(2)}) collective-permute-start(f32[2,8,16,128]{3,2,1,0:T(8,128)S(1)} %add.172), channel_id=1, source_target_pairs={{0,64},{32,96},{64,0},{96,32},{1,65},{33,97},{65,1},{97,33},{2,66}... | collective-permute-start | bytes 393224 | tf_op jit(solution)/shard_map/ppermute | solution.py:124
  162.1 11.7 %collective-permute-start.2 = (f32[2,4,16,128]{3,2,1,0:T(8,128)S(1)}, f32[2,4,16,128]{3,2,1,0:T(8,128)S(1)}, u32[]{:S(2)}, u32[]{:S(2)}) collective-permute-start(f32[2,4,16,128]{3,2,1,0:T(8,128)S(1)} %get-tuple-element.7), channel_id=1, source_target_pairs={{0,1},{1,2},{2,3},{3,4},{4,5},{5,6},{6,7},{7,8},{8,9},{9,10},{10,1... | collective-permute-start | bytes 196616 | tf_op jit(solution)/shard_map/ppermute | solution.py:26
  171.8 5.6 %collective-permute-start.3 = (f32[2,4,16,128]{3,2,1,0:T(8,128)S(1)}, f32[2,4,16,128]{3,2,1,0:T(8,128)S(1)}, u32[]{:S(2)}, u32[]{:S(2)}) collective-permute-start(f32[2,4,16,128]{3,2,1,0:T(8,128)S(1)} %get-tuple-element.8), channel_id=1, source_target_pairs={{1,0},{2,1},{3,2},{4,3},{5,4},{6,5},{7,6},{8,7},{9,8},{10,9},{11,1... | collective-permute-start | bytes 196616 | tf_op jit(solution)/shard_map/ppermute | solution.py:28

commit v12 on v10

--- a/solution.py
+++ b/solution.py
@@ -212,8 +212,7 @@
         .transpose(2, 3, 0, 4, 1, 5)
         .reshape(2, E, NBY * E, NBZ * E)
     )
-    summed = src_sum(slab)
-    padded = with_halo(summed, (("vol", 1),), 4)
+    padded = src_sum(with_halo(slab, (("vol", 1),), 4))
     field = smooth_axis(padded, 1)
     for axis in (2, 3):
         field = smooth_axis(pad_axis(field, axis), axis)

time: 180 us -> 183 us (1.017)
  waiting for transfers between devices: 108 us -> 115 us
  starting transfers between devices: 30.4 us -> 28.4 us
    ppermute x3, waiting for transfers between devices: 3.11 us -> 10.4 us  [src_sum(): lax.ppermute(part, 'src', [(i, (i + k) % count) for i in range(count)])]
  transfers between devices with their start and end apart: 6 -> 6, of which waited for: 3 -> 4; matrix products, arithmetic and copies ran while one was open for 8% -> 8% of each run, Pallas kernels for 0% -> 0%
where the time goes in v12:
time: 183 us
  waiting for transfers between devices  115 us (63%)
  starting transfers between devices  28.4 us (16%)
  local copies, waits for them, and re-layouts  18.7 us (10%)
  Pallas kernels  14.8 us (8%)
  other arithmetic  4.93 us (3%)
    all_to_all x1, waiting for transfers between devices, local(): lax.all_to_all(payload, ('src', 'vol'), split_axis=0, concat_axis=0, tile...  101 us
    reshape x2, local copies, waits for them, and re-layouts, local(): jnp.transpose(adjoint, (0, 2, 1, 3))  13.8 us
    all_to_all x1, starting transfers between devices, local(): lax.all_to_all(payload, ('src', 'vol'), split_axis=0, concat_axis=0, tile...  10.8 us
    ppermute x3, waiting for transfers between devices, src_sum(): lax.ppermute(part, 'src', [(i, (i + k) % count) for i in range(count)])  10.4 us
    ppermute x1, starting transfers between devices, with_halo(): lax.ppermute(tail, axis, [(i, (i + 1) % count) for i in range(ends)])  9.29 us
    pallas_call x1, Pallas kernels, local(): pl.pallas_call(pack_kernel, out_shape=jax.ShapeDtypeStruct((devices, chun...  7.66 us
    pallas_call x1, Pallas kernels, local(): pl.pallas_call(correlate_kernel, out_shape=jax.ShapeDtypeStruct((slot_tot...  7.12 us
    ppermute x3, starting transfers between devices, src_sum(): lax.ppermute(part, 'src', [(i, (i + k) % count) for i in range(count)])  6.42 us
  transfers between devices with their start and end apart: 6, of which 4 were waited for; matrix products, arithmetic and copies ran while one was open for 8% of the time, Pallas kernels for 0%

profile of v12, /device:TPU:57, one launch (start us, length us, event | category | flops | bytes accessed | tf_op | source)
XLA Modules:
  0.0 182.9 jit_solution(13392275736745043578)
XLA Ops:
  0.0 0.9 select_reduce_fusion
  0.9 0.8 select_reduce_fusion.3
  1.7 0.2 convert_reduce_fusion
  1.9 0.1 fusion.40
  2.0 0.2 select_reduce_fusion.1
  2.2 2.3 %copy-done = bf16[128,36,512]{2,0,1:T(8,128)(2,1)S(1)} copy-done((bf16[128,36,512]{2,0,1:T(8,128)(2,1)S(1)}, bf16[128,36,512]{2,0,1:T(8,128)(2,1)}, u32[]{:S(2)}) %copy-start) | copy-done | bytes 4718616
  4.5 7.7 %shard_map.64 = bf16[128,304,128]{2,1,0:T(8,128)(2,1)} custom-call(s32[256]{0:T(256)S(1)} %get-tuple-element.12.src_ref, s32[256]{0:T(256)S(1)} %get-tuple-element.11.pair_ref, bf16[36,128,512]{2,1,0:T(8,128)(2,1)S(1)} %bitcast.27), custom_call_target="tpu_custom_call" | custom-call | tf_op jit(solution)/shard_map/pallas_call | solution.py:167
  12.1 10.8 %all-to-all-start = ((bf16[128,304,128]{2,1,0:T(8,128)(2,1)}), bf16[128,304,128]{2,1,0:T(8,128)(2,1)}, u32[]{:S(2)}, u32[]{:S(2)}) async-start(bf16[128,304,128]{2,1,0:T(8,128)(2,1)} %shard_map.64), calls=%async_computation | async-start | bytes 19922944 | tf_op jit(solution)/shard_map/all_to_all | solution.py:180
  22.9 7.7 %reshape.171 = bf16[4,36,32,4,128]{4,3,2,1,0:T(4,128)(2,1)} reshape(bf16[4,36,32,512]{3,2,1,0:T(8,128)(2,1)} %bitcast.29) | data formatting | bytes 9437184 | tf_op jit(solution)/shard_map/reshape | solution.py:185
  30.7 6.1 %copy.12 = bf16[4,36,32,4,128]{4,3,1,2,0:T(4,128)(2,1)} copy(bf16[4,36,32,4,128]{4,3,2,1,0:T(4,128)(2,1)} %reshape.171) | data formatting | bytes 9437184 | tf_op jit(solution)/shard_map/reshape | solution.py:185
  36.8 101.2 %all-to-all-done.arrived_ref = bf16[128,304,128]{2,1,0:T(8,128)(2,1)} async-done(((bf16[128,304,128]{2,1,0:T(8,128)(2,1)}), bf16[128,304,128]{2,1,0:T(8,128)(2,1)}, u32[]{:S(2)}, u32[]{:S(2)}) %all-to-all-start) | async-done | bytes 9961504 | tf_op jit(solution)/shard_map/all_to_all | solution.py:180
  138.0 1.2 fusion.42
  139.1 0.1 convert_element_type.27.pair_ref
  139.3 7.1 %shard_map.65 = f32[256,2,8,128]{3,2,1,0:T(8,128)S(1)} custom-call(s32[256]{0:T(256)S(1)} %convert_element_type.27.pair_ref, bf16[128,304,128]{2,1,0:T(8,128)(2,1)} %all-to-all-done.arrived_ref, bf16[4,32,144,128]{3,2,1,0:T(8,128)(2,1)} %bitcast.28), custom_call_target="tpu_custom_call" | custom-call | tf_op jit(solution)/shard_map/pallas_call | solution.py:188
  146.4 0.2 slice_subtract_fusion
  146.7 0.4 reshape.173
  147.1 0.3 copy.13
  147.4 0.7 convolution_bitcast_fusion
  148.1 0.6 copy.14
  148.7 1.0 reshape.174
  149.8 9.3 %collective-permute-start = (f32[2,4,16,128]{3,2,1,0:T(8,128)S(1)}, f32[2,4,16,128]{3,2,1,0:T(8,128)S(1)}, u32[]{:S(2)}, u32[]{:S(2)}) collective-permute-start(f32[2,4,16,128]{3,2,1,0:T(8,128)S(1)} %get-tuple-element.8), channel_id=1, source_target_pairs={{0,1},{1,2},{2,3},{3,4},{4,5},{5,6},{6,7},{7,8},{8,9},{9,10},{10,1... | collective-permute-start | bytes 196616 | tf_op jit(solution)/shard_map/ppermute | solution.py:26
  159.1 1.9 %collective-permute-start.1 = (f32[2,4,16,128]{3,2,1,0:T(8,128)S(1)}, f32[2,4,16,128]{3,2,1,0:T(8,128)S(1)}, u32[]{:S(2)}, u32[]{:S(2)}) collective-permute-start(f32[2,4,16,128]{3,2,1,0:T(8,128)S(1)} %get-tuple-element.7), channel_id=1, source_target_pairs={{1,0},{2,1},{3,2},{4,3},{5,4},{6,5},{7,6},{8,7},{9,8},{10,9},{11,1... | collective-permute-start | bytes 196616 | tf_op jit(solution)/shard_map/ppermute | solution.py:28
  161.1 3.6 %collective-permute-done.1 = f32[2,4,16,128]{3,2,1,0:T(8,128)S(1)} collective-permute-done((f32[2,4,16,128]{3,2,1,0:T(8,128)S(1)}, f32[2,4,16,128]{3,2,1,0:T(8,128)S(1)}, u32[]{:S(2)}, u32[]{:S(2)}) %collective-permute-start.1) | collective-permute-done | bytes 65568 | tf_op jit(solution)/shard_map/ppermute | solution.py:28
  164.7 4.5 %collective-permute-start.2 = (f32[2,16,16,128]{3,2,1,0:T(8,128)S(1)}, f32[2,16,16,128]{3,2,1,0:T(8,128)S(1)}, u32[]{:S(2)}, u32[]{:S(2)}) collective-permute-start(f32[2,16,16,128]{3,2,1,0:T(8,128)S(1)} %constant_dynamic-update-slice_fusion), channel_id=1, source_target_pairs={{0,32},{32,64},{64,96},{96,0},{1,33},{33,65},{65,97},{97,1},{2,34}... | collective-permute-start | bytes 786440 | tf_op jit(solution)/shard_map/ppermute | solution.py:123
  169.3 1.8 %collective-permute-start.4 = (f32[2,16,16,128]{3,2,1,0:T(8,128)S(1)}, f32[2,16,16,128]{3,2,1,0:T(8,128)S(1)}, u32[]{:S(2)}, u32[]{:S(2)}) collective-permute-start(f32[2,16,16,128]{3,2,1,0:T(8,128)S(1)} %constant_dynamic-update-slice_fusion), channel_id=1, source_target_pairs={{0,96},{32,0},{64,32},{96,64},{1,97},{33,1},{65,33},{97,65},{2,98}... | collective-permute-start | bytes 786440 | tf_op jit(solution)/shard_map/ppermute | solution.py:123
  171.1 7.9 %collective-permute-done.2 = f32[2,16,16,128]{3,2,1,0:T(8,128)S(1)} collective-permute-done((f32[2,16,16,128]{3,2,1,0:T(8,128)S(1)}, f32[2,16,16,128]{3,2,1,0:T(8,128)S(1)}, u32[]{:S(2)}, u32[]{:S(2)}) %collective-permute-start.2) | collective-permute-done | bytes 262176 | tf_op jit(solution)/shard_map/ppermute | solution.py:123
  179.0 2.5 %collective-permute-done.4 = f32[2,16,16,128]{3,2,1,0:T(8,128)S(1)} collective-permute-done((f32[2,16,16,128]{3,2,1,0:T(8,128)S(1)}, f32[2,16,16,128]{3,2,1,0:T(8,128)S(1)}, u32[]{:S(2)}, u32[]{:S(2)}) %collective-permute-start.4) | collective-permute-done | bytes 262176 | tf_op jit(solution)/shard_map/ppermute | solution.py:123
  181.5 0.1 pad_maximum_fusion
  181.6 0.1 add_bitcast_fusion
  181.7 0.1 fusion.32
  181.8 0.1 fusion.8
  181.9 1.0 fusion.24
  (14 shorter events, 0.1 us)
Async XLA Ops:
  2.1 2.3 %copy-start = (bf16[128,36,512]{2,0,1:T(8,128)(2,1)S(1)}, bf16[128,36,512]{2,0,1:T(8,128)(2,1)}, u32[]{:S(2)}) copy-start(bf16[128,36,512]{2,0,1:T(8,128)(2,1)} %param.6) | copy-start | bytes 14155780
  12.1 125.8 %all-to-all-start = ((bf16[128,304,128]{2,1,0:T(8,128)(2,1)}), bf16[128,304,128]{2,1,0:T(8,128)(2,1)}, u32[]{:S(2)}, u32[]{:S(2)}) async-start(bf16[128,304,128]{2,1,0:T(8,128)(2,1)} %shard_map.64), calls=%async_computation | async-start | bytes 19922944 | tf_op jit(solution)/shard_map/all_to_all | solution.py:180
  149.8 11.2 %collective-permute-start = (f32[2,4,16,128]{3,2,1,0:T(8,128)S(1)}, f32[2,4,16,128]{3,2,1,0:T(8,128)S(1)}, u32[]{:S(2)}, u32[]{:S(2)}) collective-permute-start(f32[2,4,16,128]{3,2,1,0:T(8,128)S(1)} %get-tuple-element.8), channel_id=1, source_target_pairs={{0,1},{1,2},{2,3},{3,4},{4,5},{5,6},{6,7},{7,8},{8,9},{9,10},{10,1... | collective-permute-start | bytes 196616 | tf_op jit(solution)/shard_map/ppermute | solution.py:26
  159.1 5.6 %collective-permute-start.1 = (f32[2,4,16,128]{3,2,1,0:T(8,128)S(1)}, f32[2,4,16,128]{3,2,1,0:T(8,128)S(1)}, u32[]{:S(2)}, u32[]{:S(2)}) collective-permute-start(f32[2,4,16,128]{3,2,1,0:T(8,128)S(1)} %get-tuple-element.7), channel_id=1, source_target_pairs={{1,0},{2,1},{3,2},{4,3},{5,4},{6,5},{7,6},{8,7},{9,8},{10,9},{11,1... | collective-permute-start | bytes 196616 | tf_op jit(solution)/shard_map/ppermute | solution.py:28
  164.7 14.3 %collective-permute-start.2 = (f32[2,16,16,128]{3,2,1,0:T(8,128)S(1)}, f32[2,16,16,128]{3,2,1,0:T(8,128)S(1)}, u32[]{:S(2)}, u32[]{:S(2)}) collective-permute-start(f32[2,16,16,128]{3,2,1,0:T(8,128)S(1)} %constant_dynamic-update-slice_fusion), channel_id=1, source_target_pairs={{0,32},{32,64},{64,96},{96,0},{1,33},{33,65},{65,97},{97,1},{2,34}... | collective-permute-start | bytes 786440 | tf_op jit(solution)/shard_map/ppermute | solution.py:123
  169.2 9.8 %collective-permute-start.3 = (f32[2,16,16,128]{3,2,1,0:T(8,128)S(1)}, f32[2,16,16,128]{3,2,1,0:T(8,128)S(1)}, u32[]{:S(2)}, u32[]{:S(2)}) collective-permute-start(f32[2,16,16,128]{3,2,1,0:T(8,128)S(1)} %constant_dynamic-update-slice_fusion), channel_id=1, source_target_pairs={{0,64},{32,96},{64,0},{96,32},{1,65},{33,97},{65,1},{97,33},{2,66}... | collective-permute-start | bytes 786440 | tf_op jit(solution)/shard_map/ppermute | solution.py:123
  169.3 12.2 %collective-permute-start.4 = (f32[2,16,16,128]{3,2,1,0:T(8,128)S(1)}, f32[2,16,16,128]{3,2,1,0:T(8,128)S(1)}, u32[]{:S(2)}, u32[]{:S(2)}) collective-permute-start(f32[2,16,16,128]{3,2,1,0:T(8,128)S(1)} %constant_dynamic-update-slice_fusion), channel_id=1, source_target_pairs={{0,96},{32,0},{64,32},{96,64},{1,97},{33,1},{65,33},{97,65},{2,98}... | collective-permute-start | bytes 786440 | tf_op jit(solution)/shard_map/ppermute | solution.py:123

commit v13 on v10

--- a/solution.py
+++ b/solution.py
@@ -108,8 +108,13 @@
                 vertical = prod[g] if vertical is None else vertical + prod[g]
             else:
                 horizontal = prod[g] if horizontal is None else horizontal + prod[g]
-        out_ref[k, 0] = jnp.where(pair >= 0, horizontal, 0.0)
-        out_ref[k, 1] = jnp.where(pair >= 0, vertical, 0.0)
+        brick = held % bricks
+        out_ref[brick, 0] += jnp.where(pair >= 0, horizontal, 0.0)
+        out_ref[brick, 1] += jnp.where(pair >= 0, vertical, 0.0)
+
+    @pl.when(pl.program_id(0) == 0)
+    def _():
+        out_ref[...] = jnp.zeros(out_ref.shape, out_ref.dtype)
 
     for d in range(dests):
         one_slot(d, 0)
@@ -187,7 +192,7 @@
     ).reshape(local_tx, local_bricks, rows, LANES)
     per_slot = pl.pallas_call(
         correlate_kernel,
-        out_shape=jax.ShapeDtypeStruct((slot_total, 2, 8, LANES), jnp.float32),
+        out_shape=jax.ShapeDtypeStruct((local_bricks, 2, 8, LANES), jnp.float32),
         grid_spec=pltpu.PrefetchScalarGridSpec(
             num_scalar_prefetch=1,
             grid=(correlate_steps,),
@@ -195,18 +200,12 @@
                 pl.BlockSpec((devices // correlate_steps, chunk, LANES), lambda g, p: (g, 0, 0)),
                 pl.BlockSpec((local_tx, local_bricks, rows, LANES), lambda g, p: (0, 0, 0, 0)),
             ],
-            out_specs=pl.BlockSpec((2 * devices // correlate_steps, 2, 8, LANES), lambda g, p: (g, 0, 0, 0)),
+            out_specs=pl.BlockSpec((local_bricks, 2, 8, LANES), lambda g, p: (0, 0, 0, 0)),
         ),
         compiler_params=pltpu.CompilerParams(vmem_limit_bytes=48 * 1024 * 1024),
     )(arrived_pairs, arrived, adj_rows)
 
-    corr = (per_slot[:, :, 0:4, :] - per_slot[:, :, 4:8, :]).reshape(slot_total, 2 * cells)
-    owner_brick = jnp.maximum(arrived_pairs, 0) % local_bricks
-    owner_table = (
-        (owner_brick[None, :] == jnp.arange(local_bricks, dtype=jnp.int32)[:, None])
-        & (arrived_pairs >= 0)[None, :]
-    ).astype(jnp.float32)
-    gradient = jnp.dot(owner_table, corr, precision=lax.Precision.HIGHEST).reshape(local_bricks, 2, cells)
+    gradient = (per_slot[:, :, 0:4, :] - per_slot[:, :, 4:8, :]).reshape(local_bricks, 2, cells)
     slab = (
         gradient.reshape(NBY, NBZ, 2, E, E, E)
         .transpose(2, 3, 0, 4, 1, 5)

time: 180 us -> 180 us (level)
  local copies, waits for them, and re-layouts: 19.7 us -> 22.4 us
    unnamed x2 -> x4, local copies, waits for them, and re-layouts: 2.33 us -> 4.67 us
where the time goes in v13:
time: 180 us; the launch traced here: 179 us
  waiting for transfers between devices  108 us (60%)
  starting transfers between devices  30.4 us (17%)
  local copies, waits for them, and re-layouts  22.4 us (12%)
  Pallas kernels  13.5 us (8%)
  other arithmetic  4.62 us (3%)
    all_to_all x1, waiting for transfers between devices, local(): lax.all_to_all(payload, ('src', 'vol'), split_axis=0, concat_axis=0, tile...  101 us
    reshape x2, local copies, waits for them, and re-layouts, local(): jnp.transpose(adjoint, (0, 2, 1, 3))  13.8 us
    all_to_all x1, starting transfers between devices, local(): lax.all_to_all(payload, ('src', 'vol'), split_axis=0, concat_axis=0, tile...  10.8 us
    ppermute x1, starting transfers between devices, with_halo(): lax.ppermute(tail, axis, [(i, (i + 1) % count) for i in range(ends)])  9.95 us
    ppermute x3, starting transfers between devices, src_sum(): lax.ppermute(part, 'src', [(i, (i + k) % count) for i in range(count)])  7.72 us
    pallas_call x1, Pallas kernels, local(): pl.pallas_call(pack_kernel, out_shape=jax.ShapeDtypeStruct((devices, chun...  7.65 us
    pallas_call x1, Pallas kernels, local(): pl.pallas_call(correlate_kernel, out_shape=jax.ShapeDtypeStruct((local_br...  5.83 us
    unnamed x4, local copies, waits for them, and re-layouts  4.67 us
  transfers between devices with their start and end apart: 6, of which 3 were waited for; matrix products, arithmetic and copies ran while one was open for 8% of the time, Pallas kernels for 0%

profile of v13, /device:TPU:57, one launch (start us, length us, event | category | flops | bytes accessed | tf_op | source)
XLA Modules:
  0.0 179.0 jit_solution(466222160267491151)
XLA Ops:
  0.0 0.9 select_reduce_fusion
  0.9 0.8 select_reduce_fusion.3
  1.7 0.2 convert_reduce_fusion
  1.9 0.1 fusion.54
  2.0 0.2 select_reduce_fusion.1
  2.1 0.0 copy-start.1
  2.2 2.3 %copy-done.1 = bf16[128,36,512]{2,0,1:T(8,128)(2,1)S(1)} copy-done((bf16[128,36,512]{2,0,1:T(8,128)(2,1)S(1)}, bf16[128,36,512]{2,0,1:T(8,128)(2,1)}, u32[]{:S(2)}) %copy-start.1) | copy-done | bytes 4718616
  4.5 7.7 %shard_map.64 = bf16[128,304,128]{2,1,0:T(8,128)(2,1)} custom-call(s32[256]{0:T(256)S(1)} %get-tuple-element.12.src_ref, s32[256]{0:T(256)S(1)} %get-tuple-element.11.pair_ref, bf16[36,128,512]{2,1,0:T(8,128)(2,1)S(1)} %bitcast.22), custom_call_target="tpu_custom_call" | custom-call | tf_op jit(solution)/shard_map/pallas_call | solution.py:172
  12.1 10.8 %all-to-all-start = ((bf16[128,304,128]{2,1,0:T(8,128)(2,1)}), bf16[128,304,128]{2,1,0:T(8,128)(2,1)}, u32[]{:S(2)}, u32[]{:S(2)}) async-start(bf16[128,304,128]{2,1,0:T(8,128)(2,1)} %shard_map.64), calls=%async_computation | async-start | bytes 19922944 | tf_op jit(solution)/shard_map/all_to_all | solution.py:185
  22.9 7.7 %reshape.126 = bf16[4,36,32,4,128]{4,3,2,1,0:T(4,128)(2,1)} reshape(bf16[4,36,32,512]{3,2,1,0:T(8,128)(2,1)} %bitcast.23) | data formatting | bytes 9437184 | tf_op jit(solution)/shard_map/reshape | solution.py:190
  30.7 6.1 %copy.14 = bf16[4,36,32,4,128]{4,3,1,2,0:T(4,128)(2,1)} copy(bf16[4,36,32,4,128]{4,3,2,1,0:T(4,128)(2,1)} %reshape.126) | data formatting | bytes 9437184 | tf_op jit(solution)/shard_map/reshape | solution.py:190
  36.7 101.2 %all-to-all-done.arrived_ref = bf16[128,304,128]{2,1,0:T(8,128)(2,1)} async-done(((bf16[128,304,128]{2,1,0:T(8,128)(2,1)}), bf16[128,304,128]{2,1,0:T(8,128)(2,1)}, u32[]{:S(2)}, u32[]{:S(2)}) %all-to-all-start) | async-done | bytes 9961504 | tf_op jit(solution)/shard_map/all_to_all | solution.py:185
  138.0 1.2 fusion.56
  139.1 0.1 convert_element_type.19.pair_ref
  139.3 2.3 %copy-done = bf16[4,36,32,4,128]{4,3,1,2,0:T(4,128)(2,1)S(1)} copy-done((bf16[4,36,32,4,128]{4,3,1,2,0:T(4,128)(2,1)S(1)}, bf16[4,36,32,4,128]{4,3,1,2,0:T(4,128)(2,1)}, u32[]{:S(2)}) %copy-start) | copy-done | bytes 4718616
  141.6 5.8 %shard_map.65 = f32[32,2,8,128]{3,2,1,0:T(8,128)S(1)} custom-call(s32[256]{0:T(256)S(1)} %convert_element_type.19.pair_ref, bf16[128,304,128]{2,1,0:T(8,128)(2,1)} %all-to-all-done.arrived_ref, bf16[4,32,144,128]{3,2,1,0:T(8,128)(2,1)S(1)} %bitcast.21), custom_call_target="tpu_custom_call" | custom-call | tf_op jit(solution)/shard_map/pallas_call | solution.py:193
  147.5 0.2 copy.15
  147.7 0.6 reshape_reshape.3
  148.3 0.9 copy.16
  149.2 1.0 reshape.128
  150.2 0.3 collective-permute-start
  150.5 5.5 %collective-permute-start.1 = (f32[2,8,16,128]{3,2,1,0:T(8,128)S(1)}, f32[2,8,16,128]{3,2,1,0:T(8,128)S(1)}, u32[]{:S(2)}, u32[]{:S(2)}) collective-permute-start(f32[2,8,16,128]{3,2,1,0:T(8,128)S(1)} %reshape.128), channel_id=1, source_target_pairs={{0,64},{32,96},{64,0},{96,32},{1,65},{33,97},{65,1},{97,33},{2,66}... | collective-permute-start | bytes 393224 | tf_op jit(solution)/shard_map/ppermute | solution.py:128
  156.0 2.0 %collective-permute-start.2 = (f32[2,8,16,128]{3,2,1,0:T(8,128)S(1)}, f32[2,8,16,128]{3,2,1,0:T(8,128)S(1)}, u32[]{:S(2)}, u32[]{:S(2)}) collective-permute-start(f32[2,8,16,128]{3,2,1,0:T(8,128)S(1)} %reshape.128), channel_id=1, source_target_pairs={{0,96},{32,0},{64,32},{96,64},{1,97},{33,1},{65,33},{97,65},{2,98}... | collective-permute-start | bytes 393224 | tf_op jit(solution)/shard_map/ppermute | solution.py:128
  157.9 1.0 stack_reshape.3
  159.0 0.0 collective-permute-done
  159.0 3.1 %collective-permute-done.2 = f32[2,8,16,128]{3,2,1,0:T(8,128)S(1)} collective-permute-done((f32[2,8,16,128]{3,2,1,0:T(8,128)S(1)}, f32[2,8,16,128]{3,2,1,0:T(8,128)S(1)}, u32[]{:S(2)}, u32[]{:S(2)}) %collective-permute-start.2) | collective-permute-done | bytes 131104 | tf_op jit(solution)/shard_map/ppermute | solution.py:128
  162.2 10.0 %collective-permute-start.3 = (f32[2,4,16,128]{3,2,1,0:T(8,128)S(1)}, f32[2,4,16,128]{3,2,1,0:T(8,128)S(1)}, u32[]{:S(2)}, u32[]{:S(2)}) collective-permute-start(f32[2,4,16,128]{3,2,1,0:T(8,128)S(1)} %get-tuple-element.7), channel_id=1, source_target_pairs={{0,1},{1,2},{2,3},{3,4},{4,5},{5,6},{6,7},{7,8},{8,9},{9,10},{10,1... | collective-permute-start | bytes 196616 | tf_op jit(solution)/shard_map/ppermute | solution.py:26
  172.2 1.9 %collective-permute-start.4 = (f32[2,4,16,128]{3,2,1,0:T(8,128)S(1)}, f32[2,4,16,128]{3,2,1,0:T(8,128)S(1)}, u32[]{:S(2)}, u32[]{:S(2)}) collective-permute-start(f32[2,4,16,128]{3,2,1,0:T(8,128)S(1)} %get-tuple-element.8), channel_id=1, source_target_pairs={{1,0},{2,1},{3,2},{4,3},{5,4},{6,5},{7,6},{8,7},{9,8},{10,9},{11,1... | collective-permute-start | bytes 196616 | tf_op jit(solution)/shard_map/ppermute | solution.py:28
  174.1 3.6 %collective-permute-done.4 = f32[2,4,16,128]{3,2,1,0:T(8,128)S(1)} collective-permute-done((f32[2,4,16,128]{3,2,1,0:T(8,128)S(1)}, f32[2,4,16,128]{3,2,1,0:T(8,128)S(1)}, u32[]{:S(2)}, u32[]{:S(2)}) %collective-permute-start.4) | collective-permute-done | bytes 65568 | tf_op jit(solution)/shard_map/ppermute | solution.py:28
  177.8 0.1 fusion.3
  177.9 0.1 fusion.28
  178.0 1.0 fusion.44
  (10 shorter events, 0.2 us)
Async XLA Ops:
  2.1 2.3 %copy-start.1 = (bf16[128,36,512]{2,0,1:T(8,128)(2,1)S(1)}, bf16[128,36,512]{2,0,1:T(8,128)(2,1)}, u32[]{:S(2)}) copy-start(bf16[128,36,512]{2,0,1:T(8,128)(2,1)} %param.6) | copy-start | bytes 14155780
  12.1 125.8 %all-to-all-start = ((bf16[128,304,128]{2,1,0:T(8,128)(2,1)}), bf16[128,304,128]{2,1,0:T(8,128)(2,1)}, u32[]{:S(2)}, u32[]{:S(2)}) async-start(bf16[128,304,128]{2,1,0:T(8,128)(2,1)} %shard_map.64), calls=%async_computation | async-start | bytes 19922944 | tf_op jit(solution)/shard_map/all_to_all | solution.py:185
  139.3 2.3 %copy-start = (bf16[4,36,32,4,128]{4,3,1,2,0:T(4,128)(2,1)S(1)}, bf16[4,36,32,4,128]{4,3,1,2,0:T(4,128)(2,1)}, u32[]{:S(2)}) copy-start(bf16[4,36,32,4,128]{4,3,1,2,0:T(4,128)(2,1)} %copy.14) | copy-start | bytes 14155780
  150.2 8.8 %collective-permute-start = (f32[2,8,16,128]{3,2,1,0:T(8,128)S(1)}, f32[2,8,16,128]{3,2,1,0:T(8,128)S(1)}, u32[]{:S(2)}, u32[]{:S(2)}) collective-permute-start(f32[2,8,16,128]{3,2,1,0:T(8,128)S(1)} %reshape.128), channel_id=1, source_target_pairs={{0,32},{32,64},{64,96},{96,0},{1,33},{33,65},{65,97},{97,1},{2,34}... | collective-permute-start | bytes 393224 | tf_op jit(solution)/shard_map/ppermute | solution.py:128
  150.5 8.5 %collective-permute-start.1 = (f32[2,8,16,128]{3,2,1,0:T(8,128)S(1)}, f32[2,8,16,128]{3,2,1,0:T(8,128)S(1)}, u32[]{:S(2)}, u32[]{:S(2)}) collective-permute-start(f32[2,8,16,128]{3,2,1,0:T(8,128)S(1)} %reshape.128), channel_id=1, source_target_pairs={{0,64},{32,96},{64,0},{96,32},{1,65},{33,97},{65,1},{97,33},{2,66}... | collective-permute-start | bytes 393224 | tf_op jit(solution)/shard_map/ppermute | solution.py:128
  156.0 6.1 %collective-permute-start.2 = (f32[2,8,16,128]{3,2,1,0:T(8,128)S(1)}, f32[2,8,16,128]{3,2,1,0:T(8,128)S(1)}, u32[]{:S(2)}, u32[]{:S(2)}) collective-permute-start(f32[2,8,16,128]{3,2,1,0:T(8,128)S(1)} %reshape.128), channel_id=1, source_target_pairs={{0,96},{32,0},{64,32},{96,64},{1,97},{33,1},{65,33},{97,65},{2,98}... | collective-permute-start | bytes 393224 | tf_op jit(solution)/shard_map/ppermute | solution.py:128
  162.2 11.9 %collective-permute-start.3 = (f32[2,4,16,128]{3,2,1,0:T(8,128)S(1)}, f32[2,4,16,128]{3,2,1,0:T(8,128)S(1)}, u32[]{:S(2)}, u32[]{:S(2)}) collective-permute-start(f32[2,4,16,128]{3,2,1,0:T(8,128)S(1)} %get-tuple-element.7), channel_id=1, source_target_pairs={{0,1},{1,2},{2,3},{3,4},{4,5},{5,6},{6,7},{7,8},{8,9},{9,10},{10,1... | collective-permute-start | bytes 196616 | tf_op jit(solution)/shard_map/ppermute | solution.py:26
  172.2 5.6 %collective-permute-start.4 = (f32[2,4,16,128]{3,2,1,0:T(8,128)S(1)}, f32[2,4,16,128]{3,2,1,0:T(8,128)S(1)}, u32[]{:S(2)}, u32[]{:S(2)}) collective-permute-start(f32[2,4,16,128]{3,2,1,0:T(8,128)S(1)} %get-tuple-element.8), channel_id=1, source_target_pairs={{1,0},{2,1},{3,2},{4,3},{5,4},{6,5},{7,6},{8,7},{9,8},{10,9},{11,1... | collective-permute-start | bytes 196616 | tf_op jit(solution)/shard_map/ppermute | solution.py:28

commit v14 on v10

--- a/solution.py
+++ b/solution.py
@@ -161,7 +161,7 @@
     ).astype(jnp.int32)
 
     chunk = 2 * rows + META
-    pack_steps = 8
+    pack_steps = 4
     correlate_steps = 2
     dests_per_step = devices // pack_steps
     payload = pl.pallas_call(

time: 180 us -> 179 us (level)
  no operation moved by 1% of the time
where the time goes in v14:
time: 179 us; the launch traced here: 178 us
  waiting for transfers between devices  108 us (60%)
  starting transfers between devices  30.4 us (17%)
  local copies, waits for them, and re-layouts  19.7 us (11%)
  Pallas kernels  13.8 us (8%)
  other arithmetic  4.83 us (3%)
    all_to_all x1, waiting for transfers between devices, local(): lax.all_to_all(payload, ('src', 'vol'), split_axis=0, concat_axis=0, tile...  101 us
    reshape x2, local copies, waits for them, and re-layouts, local(): jnp.transpose(adjoint, (0, 2, 1, 3))  13.8 us
    all_to_all x1, starting transfers between devices, local(): lax.all_to_all(payload, ('src', 'vol'), split_axis=0, concat_axis=0, tile...  10.8 us
    ppermute x1, starting transfers between devices, with_halo(): lax.ppermute(tail, axis, [(i, (i + 1) % count) for i in range(ends)])  9.96 us
    ppermute x3, starting transfers between devices, src_sum(): lax.ppermute(part, 'src', [(i, (i + k) % count) for i in range(count)])  7.71 us
    pallas_call x1, Pallas kernels, local(): pl.pallas_call(correlate_kernel, out_shape=jax.ShapeDtypeStruct((slot_tot...  7.12 us
    pallas_call x1, Pallas kernels, local(): pl.pallas_call(pack_kernel, out_shape=jax.ShapeDtypeStruct((devices, chun...  6.72 us
    ppermute x1, waiting for transfers between devices, with_halo(): lax.ppermute(head, axis, [((i + 1) % count, i) for i in range(ends)])  3.65 us
  transfers between devices with their start and end apart: 6, of which 3 were waited for; matrix products, arithmetic and copies ran while one was open for 8% of the time, Pallas kernels for 0%

profile of v14, /device:TPU:57, one launch (start us, length us, event | category | flops | bytes accessed | tf_op | source)
XLA Modules:
  0.0 177.6 jit_solution(14850046511475378315)
XLA Ops:
  0.0 0.9 select_reduce_fusion
  0.9 0.8 select_reduce_fusion.3
  1.7 0.2 convert_reduce_fusion
  1.9 0.1 fusion.54
  2.0 0.2 select_reduce_fusion.1
  2.1 0.0 copy-start
  2.2 2.3 %copy-done = bf16[128,36,512]{2,0,1:T(8,128)(2,1)S(1)} copy-done((bf16[128,36,512]{2,0,1:T(8,128)(2,1)S(1)}, bf16[128,36,512]{2,0,1:T(8,128)(2,1)}, u32[]{:S(2)}) %copy-start) | copy-done | bytes 4718616
  4.5 6.7 %shard_map.64 = bf16[128,304,128]{2,1,0:T(8,128)(2,1)} custom-call(s32[256]{0:T(256)S(1)} %get-tuple-element.12.src_ref, s32[256]{0:T(256)S(1)} %get-tuple-element.11.pair_ref, bf16[36,128,512]{2,1,0:T(8,128)(2,1)S(1)} %bitcast.28), custom_call_target="tpu_custom_call" | custom-call | tf_op jit(solution)/shard_map/pallas_call | solution.py:167
  11.2 10.8 %all-to-all-start = ((bf16[128,304,128]{2,1,0:T(8,128)(2,1)}), bf16[128,304,128]{2,1,0:T(8,128)(2,1)}, u32[]{:S(2)}, u32[]{:S(2)}) async-start(bf16[128,304,128]{2,1,0:T(8,128)(2,1)} %shard_map.64), calls=%async_computation | async-start | bytes 19922944 | tf_op jit(solution)/shard_map/all_to_all | solution.py:180
  22.0 7.7 %reshape.171 = bf16[4,36,32,4,128]{4,3,2,1,0:T(4,128)(2,1)} reshape(bf16[4,36,32,512]{3,2,1,0:T(8,128)(2,1)} %bitcast.30) | data formatting | bytes 9437184 | tf_op jit(solution)/shard_map/reshape | solution.py:185
  29.7 6.1 %copy.13 = bf16[4,36,32,4,128]{4,3,1,2,0:T(4,128)(2,1)} copy(bf16[4,36,32,4,128]{4,3,2,1,0:T(4,128)(2,1)} %reshape.171) | data formatting | bytes 9437184 | tf_op jit(solution)/shard_map/reshape | solution.py:185
  35.8 101.2 %all-to-all-done.arrived_ref = bf16[128,304,128]{2,1,0:T(8,128)(2,1)} async-done(((bf16[128,304,128]{2,1,0:T(8,128)(2,1)}), bf16[128,304,128]{2,1,0:T(8,128)(2,1)}, u32[]{:S(2)}, u32[]{:S(2)}) %all-to-all-start) | async-done | bytes 9961504 | tf_op jit(solution)/shard_map/all_to_all | solution.py:180
  137.0 1.2 fusion.56
  138.2 0.1 convert_element_type.27.pair_ref
  138.4 7.1 %shard_map.65 = f32[256,2,8,128]{3,2,1,0:T(8,128)S(1)} custom-call(s32[256]{0:T(256)S(1)} %convert_element_type.27.pair_ref, bf16[128,304,128]{2,1,0:T(8,128)(2,1)} %all-to-all-done.arrived_ref, bf16[4,32,144,128]{3,2,1,0:T(8,128)(2,1)} %bitcast.29), custom_call_target="tpu_custom_call" | custom-call | tf_op jit(solution)/shard_map/pallas_call | solution.py:188
  145.5 0.2 slice_subtract_fusion
  145.7 0.4 reshape.173
  146.2 0.3 copy.14
  146.5 0.7 convolution_bitcast_fusion
  147.2 0.6 copy.15
  147.8 1.0 reshape.174
  148.9 0.3 collective-permute-start
  149.1 5.5 %collective-permute-start.1 = (f32[2,8,16,128]{3,2,1,0:T(8,128)S(1)}, f32[2,8,16,128]{3,2,1,0:T(8,128)S(1)}, u32[]{:S(2)}, u32[]{:S(2)}) collective-permute-start(f32[2,8,16,128]{3,2,1,0:T(8,128)S(1)} %reshape.174), channel_id=1, source_target_pairs={{0,64},{32,96},{64,0},{96,32},{1,65},{33,97},{65,1},{97,33},{2,66}... | collective-permute-start | bytes 393224 | tf_op jit(solution)/shard_map/ppermute | solution.py:123
  154.6 2.0 %collective-permute-start.2 = (f32[2,8,16,128]{3,2,1,0:T(8,128)S(1)}, f32[2,8,16,128]{3,2,1,0:T(8,128)S(1)}, u32[]{:S(2)}, u32[]{:S(2)}) collective-permute-start(f32[2,8,16,128]{3,2,1,0:T(8,128)S(1)} %reshape.174), channel_id=1, source_target_pairs={{0,96},{32,0},{64,32},{96,64},{1,97},{33,1},{65,33},{97,65},{2,98}... | collective-permute-start | bytes 393224 | tf_op jit(solution)/shard_map/ppermute | solution.py:123
  156.6 1.0 stack_reshape.3
  157.6 3.1 %collective-permute-done.2 = f32[2,8,16,128]{3,2,1,0:T(8,128)S(1)} collective-permute-done((f32[2,8,16,128]{3,2,1,0:T(8,128)S(1)}, f32[2,8,16,128]{3,2,1,0:T(8,128)S(1)}, u32[]{:S(2)}, u32[]{:S(2)}) %collective-permute-start.2) | collective-permute-done | bytes 131104 | tf_op jit(solution)/shard_map/ppermute | solution.py:123
  160.8 10.0 %collective-permute-start.3 = (f32[2,4,16,128]{3,2,1,0:T(8,128)S(1)}, f32[2,4,16,128]{3,2,1,0:T(8,128)S(1)}, u32[]{:S(2)}, u32[]{:S(2)}) collective-permute-start(f32[2,4,16,128]{3,2,1,0:T(8,128)S(1)} %get-tuple-element.7), channel_id=1, source_target_pairs={{0,1},{1,2},{2,3},{3,4},{4,5},{5,6},{6,7},{7,8},{8,9},{9,10},{10,1... | collective-permute-start | bytes 196616 | tf_op jit(solution)/shard_map/ppermute | solution.py:26
  170.8 1.9 %collective-permute-start.4 = (f32[2,4,16,128]{3,2,1,0:T(8,128)S(1)}, f32[2,4,16,128]{3,2,1,0:T(8,128)S(1)}, u32[]{:S(2)}, u32[]{:S(2)}) collective-permute-start(f32[2,4,16,128]{3,2,1,0:T(8,128)S(1)} %get-tuple-element.8), channel_id=1, source_target_pairs={{1,0},{2,1},{3,2},{4,3},{5,4},{6,5},{7,6},{8,7},{9,8},{10,9},{11,1... | collective-permute-start | bytes 196616 | tf_op jit(solution)/shard_map/ppermute | solution.py:28
  172.7 3.6 %collective-permute-done.4 = f32[2,4,16,128]{3,2,1,0:T(8,128)S(1)} collective-permute-done((f32[2,4,16,128]{3,2,1,0:T(8,128)S(1)}, f32[2,4,16,128]{3,2,1,0:T(8,128)S(1)}, u32[]{:S(2)}, u32[]{:S(2)}) %collective-permute-start.4) | collective-permute-done | bytes 65568 | tf_op jit(solution)/shard_map/ppermute | solution.py:28
  176.4 0.1 fusion.3
  176.5 0.1 fusion.28
  176.6 1.0 fusion.44
  (12 shorter events, 0.1 us)
Async XLA Ops:
  2.1 2.3 %copy-start = (bf16[128,36,512]{2,0,1:T(8,128)(2,1)S(1)}, bf16[128,36,512]{2,0,1:T(8,128)(2,1)}, u32[]{:S(2)}) copy-start(bf16[128,36,512]{2,0,1:T(8,128)(2,1)} %param.6) | copy-start | bytes 14155780
  11.2 125.8 %all-to-all-start = ((bf16[128,304,128]{2,1,0:T(8,128)(2,1)}), bf16[128,304,128]{2,1,0:T(8,128)(2,1)}, u32[]{:S(2)}, u32[]{:S(2)}) async-start(bf16[128,304,128]{2,1,0:T(8,128)(2,1)} %shard_map.64), calls=%async_computation | async-start | bytes 19922944 | tf_op jit(solution)/shard_map/all_to_all | solution.py:180
  148.9 8.8 %collective-permute-start = (f32[2,8,16,128]{3,2,1,0:T(8,128)S(1)}, f32[2,8,16,128]{3,2,1,0:T(8,128)S(1)}, u32[]{:S(2)}, u32[]{:S(2)}) collective-permute-start(f32[2,8,16,128]{3,2,1,0:T(8,128)S(1)} %reshape.174), channel_id=1, source_target_pairs={{0,32},{32,64},{64,96},{96,0},{1,33},{33,65},{65,97},{97,1},{2,34}... | collective-permute-start | bytes 393224 | tf_op jit(solution)/shard_map/ppermute | solution.py:123
  149.1 8.5 %collective-permute-start.1 = (f32[2,8,16,128]{3,2,1,0:T(8,128)S(1)}, f32[2,8,16,128]{3,2,1,0:T(8,128)S(1)}, u32[]{:S(2)}, u32[]{:S(2)}) collective-permute-start(f32[2,8,16,128]{3,2,1,0:T(8,128)S(1)} %reshape.174), channel_id=1, source_target_pairs={{0,64},{32,96},{64,0},{96,32},{1,65},{33,97},{65,1},{97,33},{2,66}... | collective-permute-start | bytes 393224 | tf_op jit(solution)/shard_map/ppermute | solution.py:123
  154.6 6.1 %collective-permute-start.2 = (f32[2,8,16,128]{3,2,1,0:T(8,128)S(1)}, f32[2,8,16,128]{3,2,1,0:T(8,128)S(1)}, u32[]{:S(2)}, u32[]{:S(2)}) collective-permute-start(f32[2,8,16,128]{3,2,1,0:T(8,128)S(1)} %reshape.174), channel_id=1, source_target_pairs={{0,96},{32,0},{64,32},{96,64},{1,97},{33,1},{65,33},{97,65},{2,98}... | collective-permute-start | bytes 393224 | tf_op jit(solution)/shard_map/ppermute | solution.py:123
  160.8 11.9 %collective-permute-start.3 = (f32[2,4,16,128]{3,2,1,0:T(8,128)S(1)}, f32[2,4,16,128]{3,2,1,0:T(8,128)S(1)}, u32[]{:S(2)}, u32[]{:S(2)}) collective-permute-start(f32[2,4,16,128]{3,2,1,0:T(8,128)S(1)} %get-tuple-element.7), channel_id=1, source_target_pairs={{0,1},{1,2},{2,3},{3,4},{4,5},{5,6},{6,7},{7,8},{8,9},{9,10},{10,1... | collective-permute-start | bytes 196616 | tf_op jit(solution)/shard_map/ppermute | solution.py:26
  170.8 5.6 %collective-permute-start.4 = (f32[2,4,16,128]{3,2,1,0:T(8,128)S(1)}, f32[2,4,16,128]{3,2,1,0:T(8,128)S(1)}, u32[]{:S(2)}, u32[]{:S(2)}) collective-permute-start(f32[2,4,16,128]{3,2,1,0:T(8,128)S(1)} %get-tuple-element.8), channel_id=1, source_target_pairs={{1,0},{2,1},{3,2},{4,3},{5,4},{6,5},{7,6},{8,7},{9,8},{10,9},{11,1... | collective-permute-start | bytes 196616 | tf_op jit(solution)/shard_map/ppermute | solution.py:28

commit v15 on v14

--- a/solution.py
+++ b/solution.py
@@ -161,7 +161,7 @@
     ).astype(jnp.int32)
 
     chunk = 2 * rows + META
-    pack_steps = 4
+    pack_steps = 2
     correlate_steps = 2
     dests_per_step = devices // pack_steps
     payload = pl.pallas_call(

time: 179 us -> 179 us (level)
  no operation moved by 1% of the time
where the time goes in v15:
time: 179 us; the launch traced here: 178 us
  waiting for transfers between devices  108 us (60%)
  starting transfers between devices  30.4 us (17%)
  local copies, waits for them, and re-layouts  19.7 us (11%)
  Pallas kernels  13.9 us (8%)
  other arithmetic  4.83 us (3%)
    all_to_all x1, waiting for transfers between devices, local(): lax.all_to_all(payload, ('src', 'vol'), split_axis=0, concat_axis=0, tile...  101 us
    reshape x2, local copies, waits for them, and re-layouts, local(): jnp.transpose(adjoint, (0, 2, 1, 3))  13.8 us
    all_to_all x1, starting transfers between devices, local(): lax.all_to_all(payload, ('src', 'vol'), split_axis=0, concat_axis=0, tile...  10.8 us
    ppermute x1, starting transfers between devices, with_halo(): lax.ppermute(tail, axis, [(i, (i + 1) % count) for i in range(ends)])  9.95 us
    ppermute x3, starting transfers between devices, src_sum(): lax.ppermute(part, 'src', [(i, (i + k) % count) for i in range(count)])  7.72 us
    pallas_call x1, Pallas kernels, local(): pl.pallas_call(correlate_kernel, out_shape=jax.ShapeDtypeStruct((slot_tot...  7.12 us
    pallas_call x1, Pallas kernels, local(): pl.pallas_call(pack_kernel, out_shape=jax.ShapeDtypeStruct((devices, chun...  6.74 us
    ppermute x1, waiting for transfers between devices, with_halo(): lax.ppermute(head, axis, [((i + 1) % count, i) for i in range(ends)])  3.65 us
  transfers between devices with their start and end apart: 6, of which 3 were waited for; matrix products, arithmetic and copies ran while one was open for 8% of the time, Pallas kernels for 0%

profile of v15, /device:TPU:57, one launch (start us, length us, event | category | flops | bytes accessed | tf_op | source)
XLA Modules:
  0.0 177.6 jit_solution(4210953183290762527)
XLA Ops:
  0.0 0.9 select_reduce_fusion
  0.9 0.8 select_reduce_fusion.3
  1.7 0.2 convert_reduce_fusion
  1.9 0.1 fusion.54
  2.0 0.2 select_reduce_fusion.1
  2.1 0.0 copy-start
  2.2 2.3 %copy-done = bf16[128,36,512]{2,0,1:T(8,128)(2,1)S(1)} copy-done((bf16[128,36,512]{2,0,1:T(8,128)(2,1)S(1)}, bf16[128,36,512]{2,0,1:T(8,128)(2,1)}, u32[]{:S(2)}) %copy-start) | copy-done | bytes 4718616
  4.5 6.7 %shard_map.64 = bf16[128,304,128]{2,1,0:T(8,128)(2,1)} custom-call(s32[256]{0:T(256)S(1)} %get-tuple-element.12.src_ref, s32[256]{0:T(256)S(1)} %get-tuple-element.11.pair_ref, bf16[36,128,512]{2,1,0:T(8,128)(2,1)S(1)} %bitcast.28), custom_call_target="tpu_custom_call" | custom-call | tf_op jit(solution)/shard_map/pallas_call | solution.py:167
  11.2 10.8 %all-to-all-start = ((bf16[128,304,128]{2,1,0:T(8,128)(2,1)}), bf16[128,304,128]{2,1,0:T(8,128)(2,1)}, u32[]{:S(2)}, u32[]{:S(2)}) async-start(bf16[128,304,128]{2,1,0:T(8,128)(2,1)} %shard_map.64), calls=%async_computation | async-start | bytes 19922944 | tf_op jit(solution)/shard_map/all_to_all | solution.py:180
  22.0 7.7 %reshape.171 = bf16[4,36,32,4,128]{4,3,2,1,0:T(4,128)(2,1)} reshape(bf16[4,36,32,512]{3,2,1,0:T(8,128)(2,1)} %bitcast.30) | data formatting | bytes 9437184 | tf_op jit(solution)/shard_map/reshape | solution.py:185
  29.7 6.1 %copy.13 = bf16[4,36,32,4,128]{4,3,1,2,0:T(4,128)(2,1)} copy(bf16[4,36,32,4,128]{4,3,2,1,0:T(4,128)(2,1)} %reshape.171) | data formatting | bytes 9437184 | tf_op jit(solution)/shard_map/reshape | solution.py:185
  35.8 101.2 %all-to-all-done.arrived_ref = bf16[128,304,128]{2,1,0:T(8,128)(2,1)} async-done(((bf16[128,304,128]{2,1,0:T(8,128)(2,1)}), bf16[128,304,128]{2,1,0:T(8,128)(2,1)}, u32[]{:S(2)}, u32[]{:S(2)}) %all-to-all-start) | async-done | bytes 9961504 | tf_op jit(solution)/shard_map/all_to_all | solution.py:180
  137.1 1.2 fusion.56
  138.2 0.1 convert_element_type.27.pair_ref
  138.4 7.1 %shard_map.65 = f32[256,2,8,128]{3,2,1,0:T(8,128)S(1)} custom-call(s32[256]{0:T(256)S(1)} %convert_element_type.27.pair_ref, bf16[128,304,128]{2,1,0:T(8,128)(2,1)} %all-to-all-done.arrived_ref, bf16[4,32,144,128]{3,2,1,0:T(8,128)(2,1)} %bitcast.29), custom_call_target="tpu_custom_call" | custom-call | tf_op jit(solution)/shard_map/pallas_call | solution.py:188
  145.5 0.2 slice_subtract_fusion
  145.7 0.4 reshape.173
  146.2 0.3 copy.14
  146.5 0.7 convolution_bitcast_fusion
  147.2 0.6 copy.15
  147.8 1.0 reshape.174
  148.9 0.3 collective-permute-start
  149.1 5.5 %collective-permute-start.1 = (f32[2,8,16,128]{3,2,1,0:T(8,128)S(1)}, f32[2,8,16,128]{3,2,1,0:T(8,128)S(1)}, u32[]{:S(2)}, u32[]{:S(2)}) collective-permute-start(f32[2,8,16,128]{3,2,1,0:T(8,128)S(1)} %reshape.174), channel_id=1, source_target_pairs={{0,64},{32,96},{64,0},{96,32},{1,65},{33,97},{65,1},{97,33},{2,66}... | collective-permute-start | bytes 393224 | tf_op jit(solution)/shard_map/ppermute | solution.py:123
  154.6 2.0 %collective-permute-start.2 = (f32[2,8,16,128]{3,2,1,0:T(8,128)S(1)}, f32[2,8,16,128]{3,2,1,0:T(8,128)S(1)}, u32[]{:S(2)}, u32[]{:S(2)}) collective-permute-start(f32[2,8,16,128]{3,2,1,0:T(8,128)S(1)} %reshape.174), channel_id=1, source_target_pairs={{0,96},{32,0},{64,32},{96,64},{1,97},{33,1},{65,33},{97,65},{2,98}... | collective-permute-start | bytes 393224 | tf_op jit(solution)/shard_map/ppermute | solution.py:123
  156.6 1.0 stack_reshape.3
  157.6 3.1 %collective-permute-done.2 = f32[2,8,16,128]{3,2,1,0:T(8,128)S(1)} collective-permute-done((f32[2,8,16,128]{3,2,1,0:T(8,128)S(1)}, f32[2,8,16,128]{3,2,1,0:T(8,128)S(1)}, u32[]{:S(2)}, u32[]{:S(2)}) %collective-permute-start.2) | collective-permute-done | bytes 131104 | tf_op jit(solution)/shard_map/ppermute | solution.py:123
  160.9 10.0 %collective-permute-start.3 = (f32[2,4,16,128]{3,2,1,0:T(8,128)S(1)}, f32[2,4,16,128]{3,2,1,0:T(8,128)S(1)}, u32[]{:S(2)}, u32[]{:S(2)}) collective-permute-start(f32[2,4,16,128]{3,2,1,0:T(8,128)S(1)} %get-tuple-element.7), channel_id=1, source_target_pairs={{0,1},{1,2},{2,3},{3,4},{4,5},{5,6},{6,7},{7,8},{8,9},{9,10},{10,1... | collective-permute-start | bytes 196616 | tf_op jit(solution)/shard_map/ppermute | solution.py:26
  170.8 1.9 %collective-permute-start.4 = (f32[2,4,16,128]{3,2,1,0:T(8,128)S(1)}, f32[2,4,16,128]{3,2,1,0:T(8,128)S(1)}, u32[]{:S(2)}, u32[]{:S(2)}) collective-permute-start(f32[2,4,16,128]{3,2,1,0:T(8,128)S(1)} %get-tuple-element.8), channel_id=1, source_target_pairs={{1,0},{2,1},{3,2},{4,3},{5,4},{6,5},{7,6},{8,7},{9,8},{10,9},{11,1... | collective-permute-start | bytes 196616 | tf_op jit(solution)/shard_map/ppermute | solution.py:28
  172.8 3.6 %collective-permute-done.4 = f32[2,4,16,128]{3,2,1,0:T(8,128)S(1)} collective-permute-done((f32[2,4,16,128]{3,2,1,0:T(8,128)S(1)}, f32[2,4,16,128]{3,2,1,0:T(8,128)S(1)}, u32[]{:S(2)}, u32[]{:S(2)}) %collective-permute-start.4) | collective-permute-done | bytes 65568 | tf_op jit(solution)/shard_map/ppermute | solution.py:28
  176.4 0.1 fusion.3
  176.5 0.1 fusion.28
  176.6 1.0 fusion.44
  (12 shorter events, 0.1 us)
Async XLA Ops:
  2.1 2.3 %copy-start = (bf16[128,36,512]{2,0,1:T(8,128)(2,1)S(1)}, bf16[128,36,512]{2,0,1:T(8,128)(2,1)}, u32[]{:S(2)}) copy-start(bf16[128,36,512]{2,0,1:T(8,128)(2,1)} %param.6) | copy-start | bytes 14155780
  11.2 125.8 %all-to-all-start = ((bf16[128,304,128]{2,1,0:T(8,128)(2,1)}), bf16[128,304,128]{2,1,0:T(8,128)(2,1)}, u32[]{:S(2)}, u32[]{:S(2)}) async-start(bf16[128,304,128]{2,1,0:T(8,128)(2,1)} %shard_map.64), calls=%async_computation | async-start | bytes 19922944 | tf_op jit(solution)/shard_map/all_to_all | solution.py:180
  148.9 8.8 %collective-permute-start = (f32[2,8,16,128]{3,2,1,0:T(8,128)S(1)}, f32[2,8,16,128]{3,2,1,0:T(8,128)S(1)}, u32[]{:S(2)}, u32[]{:S(2)}) collective-permute-start(f32[2,8,16,128]{3,2,1,0:T(8,128)S(1)} %reshape.174), channel_id=1, source_target_pairs={{0,32},{32,64},{64,96},{96,0},{1,33},{33,65},{65,97},{97,1},{2,34}... | collective-permute-start | bytes 393224 | tf_op jit(solution)/shard_map/ppermute | solution.py:123
  149.1 8.5 %collective-permute-start.1 = (f32[2,8,16,128]{3,2,1,0:T(8,128)S(1)}, f32[2,8,16,128]{3,2,1,0:T(8,128)S(1)}, u32[]{:S(2)}, u32[]{:S(2)}) collective-permute-start(f32[2,8,16,128]{3,2,1,0:T(8,128)S(1)} %reshape.174), channel_id=1, source_target_pairs={{0,64},{32,96},{64,0},{96,32},{1,65},{33,97},{65,1},{97,33},{2,66}... | collective-permute-start | bytes 393224 | tf_op jit(solution)/shard_map/ppermute | solution.py:123
  154.6 6.1 %collective-permute-start.2 = (f32[2,8,16,128]{3,2,1,0:T(8,128)S(1)}, f32[2,8,16,128]{3,2,1,0:T(8,128)S(1)}, u32[]{:S(2)}, u32[]{:S(2)}) collective-permute-start(f32[2,8,16,128]{3,2,1,0:T(8,128)S(1)} %reshape.174), channel_id=1, source_target_pairs={{0,96},{32,0},{64,32},{96,64},{1,97},{33,1},{65,33},{97,65},{2,98}... | collective-permute-start | bytes 393224 | tf_op jit(solution)/shard_map/ppermute | solution.py:123
  160.9 11.9 %collective-permute-start.3 = (f32[2,4,16,128]{3,2,1,0:T(8,128)S(1)}, f32[2,4,16,128]{3,2,1,0:T(8,128)S(1)}, u32[]{:S(2)}, u32[]{:S(2)}) collective-permute-start(f32[2,4,16,128]{3,2,1,0:T(8,128)S(1)} %get-tuple-element.7), channel_id=1, source_target_pairs={{0,1},{1,2},{2,3},{3,4},{4,5},{5,6},{6,7},{7,8},{8,9},{9,10},{10,1... | collective-permute-start | bytes 196616 | tf_op jit(solution)/shard_map/ppermute | solution.py:26
  170.8 5.6 %collective-permute-start.4 = (f32[2,4,16,128]{3,2,1,0:T(8,128)S(1)}, f32[2,4,16,128]{3,2,1,0:T(8,128)S(1)}, u32[]{:S(2)}, u32[]{:S(2)}) collective-permute-start(f32[2,4,16,128]{3,2,1,0:T(8,128)S(1)} %get-tuple-element.8), channel_id=1, source_target_pairs={{1,0},{2,1},{3,2},{4,3},{5,4},{6,5},{7,6},{8,7},{9,8},{10,9},{11,1... | collective-permute-start | bytes 196616 | tf_op jit(solution)/shard_map/ppermute | solution.py:28

commit v16 on v15

--- a/solution.py
+++ b/solution.py
@@ -53,11 +53,6 @@
     widths = [(0, 0)] * field.ndim
     widths[axis] = (4, 4)
     return jnp.pad(field, widths)
-
-
-def lookup(indices, table):
-    hits = indices[:, None] == jnp.arange(table.shape[0], dtype=jnp.int32)[None, :]
-    return jnp.sum(jnp.where(hits, table[None, :], 0), axis=1)
 
 
 def pack_kernel(src_ref, pair_ref, fwd_ref, out_ref, bricks_ref):
@@ -142,8 +137,8 @@
     local_bricks = adjoint.shape[1]
     capacity = 2
     slot_total = devices * capacity
-    tx_at = lookup(item_tx, tx_place)
-    brick_at = lookup(item_brick, brick_place)
+    tx_at = jnp.take(tx_place, item_tx, mode="clip")
+    brick_at = jnp.take(brick_place, item_brick, mode="clip")
     destination = tx_at // local_tx * vol_count + brick_at // local_bricks
     pair_index = tx_at % local_tx * local_bricks + brick_at % local_bricks
     positions = jnp.arange(stored, dtype=jnp.int32)

time: 179 us -> 191 us (1.067)
  other arithmetic: 4.83 us -> 14.4 us
  local copies, waits for them, and re-layouts: 19.7 us -> 22.7 us
    add x1, other arithmetic: 0.02 us -> 10.6 us  [local(): pair_index = tx_at % local_tx * local_bricks + brick_at % local_bricks]
    gather x0 -> x2, local copies, waits for them, and re-layouts: none -> 2.92 us  [the longest x1 1.95 us: local(): tx_at = jnp.take(tx_place, item_tx, mode='clip')]
where the time goes in v16:
time: 191 us; the launch traced here: 190 us
  waiting for transfers between devices  108 us (57%)
  starting transfers between devices  30.4 us (16%)
  local copies, waits for them, and re-layouts  22.7 us (12%)
  other arithmetic  14.4 us (8%)
  Pallas kernels  13.9 us (7%)
    all_to_all x1, waiting for transfers between devices, local(): lax.all_to_all(payload, ('src', 'vol'), split_axis=0, concat_axis=0, tile...  101 us
    reshape x2, local copies, waits for them, and re-layouts, local(): jnp.transpose(adjoint, (0, 2, 1, 3))  13.8 us
    all_to_all x1, starting transfers between devices, local(): lax.all_to_all(payload, ('src', 'vol'), split_axis=0, concat_axis=0, tile...  10.8 us
    add x1, other arithmetic, local(): pair_index = tx_at % local_tx * local_bricks + brick_at % local_bricks  10.6 us
    ppermute x1, starting transfers between devices, with_halo(): lax.ppermute(tail, axis, [(i, (i + 1) % count) for i in range(ends)])  9.94 us
    ppermute x3, starting transfers between devices, src_sum(): lax.ppermute(part, 'src', [(i, (i + k) % count) for i in range(count)])  7.72 us
    pallas_call x1, Pallas kernels, local(): pl.pallas_call(correlate_kernel, out_shape=jax.ShapeDtypeStruct((slot_tot...  7.16 us
    pallas_call x1, Pallas kernels, local(): pl.pallas_call(pack_kernel, out_shape=jax.ShapeDtypeStruct((devices, chun...  6.73 us
  transfers between devices with their start and end apart: 6, of which 3 were waited for; matrix products, arithmetic and copies ran while one was open for 8% of the time, Pallas kernels for 0%

profile of v16, /device:TPU:57, one launch (start us, length us, event | category | flops | bytes accessed | tf_op | source)
XLA Modules:
  0.0 190.2 jit_solution(9238704563120746870)
XLA Ops:
  0.0 2.0 %fusion.67 = (s32[1]{0:T(128)}, s32[1]{0:T(128)}, s32[1]{0:T(128)}, s32[1]{0:T(128)}, s32[1]{0:T(128)}, /*index=5*/s32[1]{0:T(128)}, s32[1]{0:T(128)}, s32[1]{0:...) fusion(s32[16]{0:T(128)} %param.9), kind=kLoop, calls=%fused_computation.141 | loop fusion | bytes 128 | tf_op jit(solution)/shard_map/jit(_take)/gather | solution.py:140
  2.0 0.7 pad_clamp_fusion
  2.6 1.0 gather_fusion
  3.6 10.6 %fusion.64 = (s32[128]{0:T(128)S(1)}, s32[128]{0:T(128)S(1)}) fusion(s32[128]{0:T(128)S(1)} %gather_fusion, s32[]{:T(128)} %bitcast.15, s32[]{:T(128)} %bitcast.14, s32[128]{0:T(128)} %param.7, s32[]{:T(128)} %bitcast.13, s32[]{:T(128)} %bitcast.12, s32[]{:T(128)} %bitcast.11, s32[]{:T(128)} %bitcast.10, s32[]{:T(128)} %bitcast.9, s32[]{:T(128)} %bitcast.8, ...), kind=kLoop, calls=%fused_computation.133 | loop fusion | flops 6912 | bytes 2112 | tf_op jit(solution)/shard_map/add | solution.py:143
  14.2 0.2 convert_reduce_fusion
  14.4 0.1 fusion.54
  14.5 0.2 select_reduce_fusion
  14.7 2.3 %copy-done.1 = bf16[128,36,512]{2,0,1:T(8,128)(2,1)S(1)} copy-done((bf16[128,36,512]{2,0,1:T(8,128)(2,1)S(1)}, bf16[128,36,512]{2,0,1:T(8,128)(2,1)}, u32[]{:S(2)}) %copy-start.1) | copy-done | bytes 4718616
  17.1 6.7 %shard_map.64 = bf16[128,304,128]{2,1,0:T(8,128)(2,1)} custom-call(s32[256]{0:T(256)S(1)} %get-tuple-element.12.src_ref, s32[256]{0:T(256)S(1)} %get-tuple-element.11.pair_ref, bf16[36,128,512]{2,1,0:T(8,128)(2,1)S(1)} %bitcast.44), custom_call_target="tpu_custom_call" | custom-call | tf_op jit(solution)/shard_map/pallas_call | solution.py:162
  23.8 10.8 %all-to-all-start = ((bf16[128,304,128]{2,1,0:T(8,128)(2,1)}), bf16[128,304,128]{2,1,0:T(8,128)(2,1)}, u32[]{:S(2)}, u32[]{:S(2)}) async-start(bf16[128,304,128]{2,1,0:T(8,128)(2,1)} %shard_map.64), calls=%async_computation | async-start | bytes 19922944 | tf_op jit(solution)/shard_map/all_to_all | solution.py:175
  34.6 7.7 %reshape.167 = bf16[4,36,32,4,128]{4,3,2,1,0:T(4,128)(2,1)} reshape(bf16[4,36,32,512]{3,2,1,0:T(8,128)(2,1)} %bitcast.46) | data formatting | bytes 9437184 | tf_op jit(solution)/shard_map/reshape | solution.py:180
  42.3 6.1 %copy.13 = bf16[4,36,32,4,128]{4,3,1,2,0:T(4,128)(2,1)} copy(bf16[4,36,32,4,128]{4,3,2,1,0:T(4,128)(2,1)} %reshape.167) | data formatting | bytes 9437184 | tf_op jit(solution)/shard_map/reshape | solution.py:180
  48.4 101.2 %all-to-all-done.arrived_ref = bf16[128,304,128]{2,1,0:T(8,128)(2,1)} async-done(((bf16[128,304,128]{2,1,0:T(8,128)(2,1)}), bf16[128,304,128]{2,1,0:T(8,128)(2,1)}, u32[]{:S(2)}, u32[]{:S(2)}) %all-to-all-start) | async-done | bytes 9961504 | tf_op jit(solution)/shard_map/all_to_all | solution.py:175
  149.6 1.2 fusion.56
  150.8 0.1 convert_element_type.27.pair_ref
  150.9 7.2 %shard_map.65 = f32[256,2,8,128]{3,2,1,0:T(8,128)S(1)} custom-call(s32[256]{0:T(256)S(1)} %convert_element_type.27.pair_ref, bf16[128,304,128]{2,1,0:T(8,128)(2,1)} %all-to-all-done.arrived_ref, bf16[4,32,144,128]{3,2,1,0:T(8,128)(2,1)} %bitcast.45), custom_call_target="tpu_custom_call" | custom-call | tf_op jit(solution)/shard_map/pallas_call | solution.py:183
  158.1 0.2 slice_subtract_fusion
  158.3 0.4 reshape.169
  158.8 0.3 copy.14
  159.1 0.7 convolution_bitcast_fusion
  159.8 0.6 copy.15
  160.4 1.0 reshape.170
  161.5 0.3 collective-permute-start
  161.7 5.5 %collective-permute-start.1 = (f32[2,8,16,128]{3,2,1,0:T(8,128)S(1)}, f32[2,8,16,128]{3,2,1,0:T(8,128)S(1)}, u32[]{:S(2)}, u32[]{:S(2)}) collective-permute-start(f32[2,8,16,128]{3,2,1,0:T(8,128)S(1)} %reshape.170), channel_id=1, source_target_pairs={{0,64},{32,96},{64,0},{96,32},{1,65},{33,97},{65,1},{97,33},{2,66}... | collective-permute-start | bytes 393224 | tf_op jit(solution)/shard_map/ppermute | solution.py:118
  167.2 2.0 %collective-permute-start.2 = (f32[2,8,16,128]{3,2,1,0:T(8,128)S(1)}, f32[2,8,16,128]{3,2,1,0:T(8,128)S(1)}, u32[]{:S(2)}, u32[]{:S(2)}) collective-permute-start(f32[2,8,16,128]{3,2,1,0:T(8,128)S(1)} %reshape.170), channel_id=1, source_target_pairs={{0,96},{32,0},{64,32},{96,64},{1,97},{33,1},{65,33},{97,65},{2,98}... | collective-permute-start | bytes 393224 | tf_op jit(solution)/shard_map/ppermute | solution.py:118
  169.2 1.0 stack_reshape.3
  170.2 3.1 %collective-permute-done.2 = f32[2,8,16,128]{3,2,1,0:T(8,128)S(1)} collective-permute-done((f32[2,8,16,128]{3,2,1,0:T(8,128)S(1)}, f32[2,8,16,128]{3,2,1,0:T(8,128)S(1)}, u32[]{:S(2)}, u32[]{:S(2)}) %collective-permute-start.2) | collective-permute-done | bytes 131104 | tf_op jit(solution)/shard_map/ppermute | solution.py:118
  173.5 9.9 %collective-permute-start.3 = (f32[2,4,16,128]{3,2,1,0:T(8,128)S(1)}, f32[2,4,16,128]{3,2,1,0:T(8,128)S(1)}, u32[]{:S(2)}, u32[]{:S(2)}) collective-permute-start(f32[2,4,16,128]{3,2,1,0:T(8,128)S(1)} %get-tuple-element.9), channel_id=1, source_target_pairs={{0,1},{1,2},{2,3},{3,4},{4,5},{5,6},{6,7},{7,8},{8,9},{9,10},{10,1... | collective-permute-start | bytes 196616 | tf_op jit(solution)/shard_map/ppermute | solution.py:26
  183.4 1.9 %collective-permute-start.4 = (f32[2,4,16,128]{3,2,1,0:T(8,128)S(1)}, f32[2,4,16,128]{3,2,1,0:T(8,128)S(1)}, u32[]{:S(2)}, u32[]{:S(2)}) collective-permute-start(f32[2,4,16,128]{3,2,1,0:T(8,128)S(1)} %get-tuple-element.10), channel_id=1, source_target_pairs={{1,0},{2,1},{3,2},{4,3},{5,4},{6,5},{7,6},{8,7},{9,8},{10,9},{11,1... | collective-permute-start | bytes 196616 | tf_op jit(solution)/shard_map/ppermute | solution.py:28
  185.4 3.6 %collective-permute-done.4 = f32[2,4,16,128]{3,2,1,0:T(8,128)S(1)} collective-permute-done((f32[2,4,16,128]{3,2,1,0:T(8,128)S(1)}, f32[2,4,16,128]{3,2,1,0:T(8,128)S(1)}, u32[]{:S(2)}, u32[]{:S(2)}) %collective-permute-start.4) | collective-permute-done | bytes 65568 | tf_op jit(solution)/shard_map/ppermute | solution.py:28
  189.1 0.1 fusion.28
  189.2 1.0 fusion.44
  (16 shorter events, 0.2 us)
Async XLA Ops:
  0.0 2.6 %copy-start = (s32[1024]{0:T(1024)S(1)}, s32[1024]{0:T(1024)}, u32[]{:S(2)}) copy-start(s32[1024]{0:T(1024)} %param.10) | copy-start | bytes 12292
  14.7 2.3 %copy-start.1 = (bf16[128,36,512]{2,0,1:T(8,128)(2,1)S(1)}, bf16[128,36,512]{2,0,1:T(8,128)(2,1)}, u32[]{:S(2)}) copy-start(bf16[128,36,512]{2,0,1:T(8,128)(2,1)} %param.6) | copy-start | bytes 14155780
  23.8 125.8 %all-to-all-start = ((bf16[128,304,128]{2,1,0:T(8,128)(2,1)}), bf16[128,304,128]{2,1,0:T(8,128)(2,1)}, u32[]{:S(2)}, u32[]{:S(2)}) async-start(bf16[128,304,128]{2,1,0:T(8,128)(2,1)} %shard_map.64), calls=%async_computation | async-start | bytes 19922944 | tf_op jit(solution)/shard_map/all_to_all | solution.py:175
  161.5 8.8 %collective-permute-start = (f32[2,8,16,128]{3,2,1,0:T(8,128)S(1)}, f32[2,8,16,128]{3,2,1,0:T(8,128)S(1)}, u32[]{:S(2)}, u32[]{:S(2)}) collective-permute-start(f32[2,8,16,128]{3,2,1,0:T(8,128)S(1)} %reshape.170), channel_id=1, source_target_pairs={{0,32},{32,64},{64,96},{96,0},{1,33},{33,65},{65,97},{97,1},{2,34}... | collective-permute-start | bytes 393224 | tf_op jit(solution)/shard_map/ppermute | solution.py:118
  161.7 8.5 %collective-permute-start.1 = (f32[2,8,16,128]{3,2,1,0:T(8,128)S(1)}, f32[2,8,16,128]{3,2,1,0:T(8,128)S(1)}, u32[]{:S(2)}, u32[]{:S(2)}) collective-permute-start(f32[2,8,16,128]{3,2,1,0:T(8,128)S(1)} %reshape.170), channel_id=1, source_target_pairs={{0,64},{32,96},{64,0},{96,32},{1,65},{33,97},{65,1},{97,33},{2,66}... | collective-permute-start | bytes 393224 | tf_op jit(solution)/shard_map/ppermute | solution.py:118
  167.2 6.2 %collective-permute-start.2 = (f32[2,8,16,128]{3,2,1,0:T(8,128)S(1)}, f32[2,8,16,128]{3,2,1,0:T(8,128)S(1)}, u32[]{:S(2)}, u32[]{:S(2)}) collective-permute-start(f32[2,8,16,128]{3,2,1,0:T(8,128)S(1)} %reshape.170), channel_id=1, source_target_pairs={{0,96},{32,0},{64,32},{96,64},{1,97},{33,1},{65,33},{97,65},{2,98}... | collective-permute-start | bytes 393224 | tf_op jit(solution)/shard_map/ppermute | solution.py:118
  173.5 11.9 %collective-permute-start.3 = (f32[2,4,16,128]{3,2,1,0:T(8,128)S(1)}, f32[2,4,16,128]{3,2,1,0:T(8,128)S(1)}, u32[]{:S(2)}, u32[]{:S(2)}) collective-permute-start(f32[2,4,16,128]{3,2,1,0:T(8,128)S(1)} %get-tuple-element.9), channel_id=1, source_target_pairs={{0,1},{1,2},{2,3},{3,4},{4,5},{5,6},{6,7},{7,8},{8,9},{9,10},{10,1... | collective-permute-start | bytes 196616 | tf_op jit(solution)/shard_map/ppermute | solution.py:26
  183.4 5.6 %collective-permute-start.4 = (f32[2,4,16,128]{3,2,1,0:T(8,128)S(1)}, f32[2,4,16,128]{3,2,1,0:T(8,128)S(1)}, u32[]{:S(2)}, u32[]{:S(2)}) collective-permute-start(f32[2,4,16,128]{3,2,1,0:T(8,128)S(1)} %get-tuple-element.10), channel_id=1, source_target_pairs={{1,0},{2,1},{3,2},{4,3},{5,4},{6,5},{7,6},{8,7},{9,8},{10,9},{11,1... | collective-permute-start | bytes 196616 | tf_op jit(solution)/shard_map/ppermute | solution.py:28

commit v17 on v15

--- a/solution.py
+++ b/solution.py
@@ -162,7 +162,7 @@
 
     chunk = 2 * rows + META
     pack_steps = 2
-    correlate_steps = 2
+    correlate_steps = 1
     dests_per_step = devices // pack_steps
     payload = pl.pallas_call(
         pack_kernel,

time: 179 us -> 180 us (level)
  no operation moved by 1% of the time
where the time goes in v17:
time: 180 us; the launch traced here: 179 us
  waiting for transfers between devices  108 us (60%)
  starting transfers between devices  30.4 us (17%)
  local copies, waits for them, and re-layouts  19.7 us (11%)
  Pallas kernels  15 us (8%)
  other arithmetic  4.83 us (3%)
    all_to_all x1, waiting for transfers between devices, local(): lax.all_to_all(payload, ('src', 'vol'), split_axis=0, concat_axis=0, tile...  101 us
    reshape x2, local copies, waits for them, and re-layouts, local(): jnp.transpose(adjoint, (0, 2, 1, 3))  13.8 us
    all_to_all x1, starting transfers between devices, local(): lax.all_to_all(payload, ('src', 'vol'), split_axis=0, concat_axis=0, tile...  10.8 us
    ppermute x1, starting transfers between devices, with_halo(): lax.ppermute(tail, axis, [(i, (i + 1) % count) for i in range(ends)])  9.95 us
    pallas_call x1, Pallas kernels, local(): pl.pallas_call(correlate_kernel, out_shape=jax.ShapeDtypeStruct((slot_tot...  8.27 us
    ppermute x3, starting transfers between devices, src_sum(): lax.ppermute(part, 'src', [(i, (i + k) % count) for i in range(count)])  7.72 us
    pallas_call x1, Pallas kernels, local(): pl.pallas_call(pack_kernel, out_shape=jax.ShapeDtypeStruct((devices, chun...  6.73 us
    ppermute x1, waiting for transfers between devices, with_halo(): lax.ppermute(head, axis, [((i + 1) % count, i) for i in range(ends)])  3.65 us
  transfers between devices with their start and end apart: 6, of which 3 were waited for; matrix products, arithmetic and copies ran while one was open for 8% of the time, Pallas kernels for 0%

profile of v17, /device:TPU:57, one launch (start us, length us, event | category | flops | bytes accessed | tf_op | source)
XLA Modules:
  0.0 178.8 jit_solution(7819232129233898094)
XLA Ops:
  0.0 0.9 select_reduce_fusion
  0.9 0.8 select_reduce_fusion.3
  1.7 0.2 convert_reduce_fusion
  1.9 0.1 fusion.54
  2.0 0.2 select_reduce_fusion.1
  2.1 0.0 copy-start
  2.2 2.3 %copy-done = bf16[128,36,512]{2,0,1:T(8,128)(2,1)S(1)} copy-done((bf16[128,36,512]{2,0,1:T(8,128)(2,1)S(1)}, bf16[128,36,512]{2,0,1:T(8,128)(2,1)}, u32[]{:S(2)}) %copy-start) | copy-done | bytes 4718616
  4.5 6.7 %shard_map.64 = bf16[128,304,128]{2,1,0:T(8,128)(2,1)} custom-call(s32[256]{0:T(256)S(1)} %get-tuple-element.12.src_ref, s32[256]{0:T(256)S(1)} %get-tuple-element.11.pair_ref, bf16[36,128,512]{2,1,0:T(8,128)(2,1)S(1)} %bitcast.28), custom_call_target="tpu_custom_call" | custom-call | tf_op jit(solution)/shard_map/pallas_call | solution.py:167
  11.2 10.8 %all-to-all-start = ((bf16[128,304,128]{2,1,0:T(8,128)(2,1)}), bf16[128,304,128]{2,1,0:T(8,128)(2,1)}, u32[]{:S(2)}, u32[]{:S(2)}) async-start(bf16[128,304,128]{2,1,0:T(8,128)(2,1)} %shard_map.64), calls=%async_computation | async-start | bytes 19922944 | tf_op jit(solution)/shard_map/all_to_all | solution.py:180
  22.0 7.7 %reshape.171 = bf16[4,36,32,4,128]{4,3,2,1,0:T(4,128)(2,1)} reshape(bf16[4,36,32,512]{3,2,1,0:T(8,128)(2,1)} %bitcast.30) | data formatting | bytes 9437184 | tf_op jit(solution)/shard_map/reshape | solution.py:185
  29.7 6.1 %copy.13 = bf16[4,36,32,4,128]{4,3,1,2,0:T(4,128)(2,1)} copy(bf16[4,36,32,4,128]{4,3,2,1,0:T(4,128)(2,1)} %reshape.171) | data formatting | bytes 9437184 | tf_op jit(solution)/shard_map/reshape | solution.py:185
  35.8 101.2 %all-to-all-done.arrived_ref = bf16[128,304,128]{2,1,0:T(8,128)(2,1)} async-done(((bf16[128,304,128]{2,1,0:T(8,128)(2,1)}), bf16[128,304,128]{2,1,0:T(8,128)(2,1)}, u32[]{:S(2)}, u32[]{:S(2)}) %all-to-all-start) | async-done | bytes 9961504 | tf_op jit(solution)/shard_map/all_to_all | solution.py:180
  137.0 1.2 fusion.56
  138.2 0.1 convert_element_type.27.pair_ref
  138.4 8.3 %shard_map.65 = f32[256,2,8,128]{3,2,1,0:T(8,128)S(1)} custom-call(s32[256]{0:T(256)S(1)} %convert_element_type.27.pair_ref, bf16[128,304,128]{2,1,0:T(8,128)(2,1)} %all-to-all-done.arrived_ref, bf16[4,32,144,128]{3,2,1,0:T(8,128)(2,1)} %bitcast.29), custom_call_target="tpu_custom_call" | custom-call | tf_op jit(solution)/shard_map/pallas_call | solution.py:188
  146.7 0.2 slice_subtract_fusion
  146.9 0.4 reshape.173
  147.3 0.3 copy.14
  147.7 0.7 convolution_bitcast_fusion
  148.3 0.6 copy.15
  149.0 1.0 reshape.174
  150.0 0.3 collective-permute-start
  150.3 5.5 %collective-permute-start.1 = (f32[2,8,16,128]{3,2,1,0:T(8,128)S(1)}, f32[2,8,16,128]{3,2,1,0:T(8,128)S(1)}, u32[]{:S(2)}, u32[]{:S(2)}) collective-permute-start(f32[2,8,16,128]{3,2,1,0:T(8,128)S(1)} %reshape.174), channel_id=1, source_target_pairs={{0,64},{32,96},{64,0},{96,32},{1,65},{33,97},{65,1},{97,33},{2,66}... | collective-permute-start | bytes 393224 | tf_op jit(solution)/shard_map/ppermute | solution.py:123
  155.8 2.0 %collective-permute-start.2 = (f32[2,8,16,128]{3,2,1,0:T(8,128)S(1)}, f32[2,8,16,128]{3,2,1,0:T(8,128)S(1)}, u32[]{:S(2)}, u32[]{:S(2)}) collective-permute-start(f32[2,8,16,128]{3,2,1,0:T(8,128)S(1)} %reshape.174), channel_id=1, source_target_pairs={{0,96},{32,0},{64,32},{96,64},{1,97},{33,1},{65,33},{97,65},{2,98}... | collective-permute-start | bytes 393224 | tf_op jit(solution)/shard_map/ppermute | solution.py:123
  157.7 1.0 stack_reshape.3
  158.8 3.1 %collective-permute-done.2 = f32[2,8,16,128]{3,2,1,0:T(8,128)S(1)} collective-permute-done((f32[2,8,16,128]{3,2,1,0:T(8,128)S(1)}, f32[2,8,16,128]{3,2,1,0:T(8,128)S(1)}, u32[]{:S(2)}, u32[]{:S(2)}) %collective-permute-start.2) | collective-permute-done | bytes 131104 | tf_op jit(solution)/shard_map/ppermute | solution.py:123
  162.0 10.0 %collective-permute-start.3 = (f32[2,4,16,128]{3,2,1,0:T(8,128)S(1)}, f32[2,4,16,128]{3,2,1,0:T(8,128)S(1)}, u32[]{:S(2)}, u32[]{:S(2)}) collective-permute-start(f32[2,4,16,128]{3,2,1,0:T(8,128)S(1)} %get-tuple-element.7), channel_id=1, source_target_pairs={{0,1},{1,2},{2,3},{3,4},{4,5},{5,6},{6,7},{7,8},{8,9},{9,10},{10,1... | collective-permute-start | bytes 196616 | tf_op jit(solution)/shard_map/ppermute | solution.py:26
  172.0 1.9 %collective-permute-start.4 = (f32[2,4,16,128]{3,2,1,0:T(8,128)S(1)}, f32[2,4,16,128]{3,2,1,0:T(8,128)S(1)}, u32[]{:S(2)}, u32[]{:S(2)}) collective-permute-start(f32[2,4,16,128]{3,2,1,0:T(8,128)S(1)} %get-tuple-element.8), channel_id=1, source_target_pairs={{1,0},{2,1},{3,2},{4,3},{5,4},{6,5},{7,6},{8,7},{9,8},{10,9},{11,1... | collective-permute-start | bytes 196616 | tf_op jit(solution)/shard_map/ppermute | solution.py:28
  173.9 3.6 %collective-permute-done.4 = f32[2,4,16,128]{3,2,1,0:T(8,128)S(1)} collective-permute-done((f32[2,4,16,128]{3,2,1,0:T(8,128)S(1)}, f32[2,4,16,128]{3,2,1,0:T(8,128)S(1)}, u32[]{:S(2)}, u32[]{:S(2)}) %collective-permute-start.4) | collective-permute-done | bytes 65568 | tf_op jit(solution)/shard_map/ppermute | solution.py:28
  177.6 0.1 fusion.3
  177.6 0.1 fusion.28
  177.8 1.0 fusion.44
  (12 shorter events, 0.1 us)
Async XLA Ops:
  2.1 2.3 %copy-start = (bf16[128,36,512]{2,0,1:T(8,128)(2,1)S(1)}, bf16[128,36,512]{2,0,1:T(8,128)(2,1)}, u32[]{:S(2)}) copy-start(bf16[128,36,512]{2,0,1:T(8,128)(2,1)} %param.6) | copy-start | bytes 14155780
  11.2 125.8 %all-to-all-start = ((bf16[128,304,128]{2,1,0:T(8,128)(2,1)}), bf16[128,304,128]{2,1,0:T(8,128)(2,1)}, u32[]{:S(2)}, u32[]{:S(2)}) async-start(bf16[128,304,128]{2,1,0:T(8,128)(2,1)} %shard_map.64), calls=%async_computation | async-start | bytes 19922944 | tf_op jit(solution)/shard_map/all_to_all | solution.py:180
  150.0 8.8 %collective-permute-start = (f32[2,8,16,128]{3,2,1,0:T(8,128)S(1)}, f32[2,8,16,128]{3,2,1,0:T(8,128)S(1)}, u32[]{:S(2)}, u32[]{:S(2)}) collective-permute-start(f32[2,8,16,128]{3,2,1,0:T(8,128)S(1)} %reshape.174), channel_id=1, source_target_pairs={{0,32},{32,64},{64,96},{96,0},{1,33},{33,65},{65,97},{97,1},{2,34}... | collective-permute-start | bytes 393224 | tf_op jit(solution)/shard_map/ppermute | solution.py:123
  150.3 8.5 %collective-permute-start.1 = (f32[2,8,16,128]{3,2,1,0:T(8,128)S(1)}, f32[2,8,16,128]{3,2,1,0:T(8,128)S(1)}, u32[]{:S(2)}, u32[]{:S(2)}) collective-permute-start(f32[2,8,16,128]{3,2,1,0:T(8,128)S(1)} %reshape.174), channel_id=1, source_target_pairs={{0,64},{32,96},{64,0},{96,32},{1,65},{33,97},{65,1},{97,33},{2,66}... | collective-permute-start | bytes 393224 | tf_op jit(solution)/shard_map/ppermute | solution.py:123
  155.8 6.1 %collective-permute-start.2 = (f32[2,8,16,128]{3,2,1,0:T(8,128)S(1)}, f32[2,8,16,128]{3,2,1,0:T(8,128)S(1)}, u32[]{:S(2)}, u32[]{:S(2)}) collective-permute-start(f32[2,8,16,128]{3,2,1,0:T(8,128)S(1)} %reshape.174), channel_id=1, source_target_pairs={{0,96},{32,0},{64,32},{96,64},{1,97},{33,1},{65,33},{97,65},{2,98}... | collective-permute-start | bytes 393224 | tf_op jit(solution)/shard_map/ppermute | solution.py:123
  162.0 11.9 %collective-permute-start.3 = (f32[2,4,16,128]{3,2,1,0:T(8,128)S(1)}, f32[2,4,16,128]{3,2,1,0:T(8,128)S(1)}, u32[]{:S(2)}, u32[]{:S(2)}) collective-permute-start(f32[2,4,16,128]{3,2,1,0:T(8,128)S(1)} %get-tuple-element.7), channel_id=1, source_target_pairs={{0,1},{1,2},{2,3},{3,4},{4,5},{5,6},{6,7},{7,8},{8,9},{9,10},{10,1... | collective-permute-start | bytes 196616 | tf_op jit(solution)/shard_map/ppermute | solution.py:26
  172.0 5.6 %collective-permute-start.4 = (f32[2,4,16,128]{3,2,1,0:T(8,128)S(1)}, f32[2,4,16,128]{3,2,1,0:T(8,128)S(1)}, u32[]{:S(2)}, u32[]{:S(2)}) collective-permute-start(f32[2,4,16,128]{3,2,1,0:T(8,128)S(1)} %get-tuple-element.8), channel_id=1, source_target_pairs={{1,0},{2,1},{3,2},{4,3},{5,4},{6,5},{7,6},{8,7},{9,8},{10,9},{11,1... | collective-permute-start | bytes 196616 | tf_op jit(solution)/shard_map/ppermute | solution.py:28

commit v18 on v15

--- a/solution.py
+++ b/solution.py
@@ -123,10 +123,17 @@
         lax.ppermute(part, "src", [(i, (i + k) % count) for i in range(count)])
         for k in range(1, count)
     ]
-    stacked = jnp.stack(parts)
-    total = lax.dynamic_index_in_dim(stacked, me % count, keepdims=False)
+
+    def from_src(j):
+        shift = (me - j) % count
+        picked = parts[0]
+        for k in range(1, count):
+            picked = jnp.where(shift == k, parts[k], picked)
+        return picked
+
+    total = from_src(0)
     for j in range(1, count):
-        total = total + lax.dynamic_index_in_dim(stacked, (me - j) % count, keepdims=False)
+        total = total + from_src(j)
     return total
 
 

time: 179 us -> 180 us (level)
  transfers between devices with their start and end apart: 6 -> 6, of which waited for: 3 -> 4; matrix products, arithmetic and copies ran while one was open for 8% -> 8% of each run, Pallas kernels for 0% -> 0%
where the time goes in v18:
time: 180 us; the launch traced here: 178 us
  waiting for transfers between devices  109 us (61%)
  starting transfers between devices  30.6 us (17%)
  local copies, waits for them, and re-layouts  18.7 us (10%)
  Pallas kernels  13.9 us (8%)
  other arithmetic  4.82 us (3%)
    all_to_all x1, waiting for transfers between devices, local(): lax.all_to_all(payload, ('src', 'vol'), split_axis=0, concat_axis=0, tile...  101 us
    reshape x2, local copies, waits for them, and re-layouts, local(): jnp.transpose(adjoint, (0, 2, 1, 3))  13.8 us
    all_to_all x1, starting transfers between devices, local(): lax.all_to_all(payload, ('src', 'vol'), split_axis=0, concat_axis=0, tile...  10.8 us
    ppermute x1, starting transfers between devices, with_halo(): lax.ppermute(tail, axis, [(i, (i + 1) % count) for i in range(ends)])  10.2 us
    ppermute x3, starting transfers between devices, src_sum(): lax.ppermute(part, 'src', [(i, (i + k) % count) for i in range(count)])  7.72 us
    pallas_call x1, Pallas kernels, local(): pl.pallas_call(correlate_kernel, out_shape=jax.ShapeDtypeStruct((slot_tot...  7.12 us
    pallas_call x1, Pallas kernels, local(): pl.pallas_call(pack_kernel, out_shape=jax.ShapeDtypeStruct((devices, chun...  6.73 us
    ppermute x3, waiting for transfers between devices, src_sum(): lax.ppermute(part, 'src', [(i, (i + k) % count) for i in range(count)])  4.3 us
  transfers between devices with their start and end apart: 6, of which 4 were waited for; matrix products, arithmetic and copies ran while one was open for 8% of the time, Pallas kernels for 0%

profile of v18, /device:TPU:57, one launch (start us, length us, event | category | flops | bytes accessed | tf_op | source)
XLA Modules:
  0.0 178.0 jit_solution(3226653362814052802)
XLA Ops:
  0.0 0.9 select_reduce_fusion
  0.9 0.8 select_reduce_fusion.3
  1.7 0.2 convert_reduce_fusion
  1.9 0.1 fusion.54
  2.0 0.2 select_reduce_fusion.1
  2.2 2.3 %copy-done = bf16[128,36,512]{2,0,1:T(8,128)(2,1)S(1)} copy-done((bf16[128,36,512]{2,0,1:T(8,128)(2,1)S(1)}, bf16[128,36,512]{2,0,1:T(8,128)(2,1)}, u32[]{:S(2)}) %copy-start) | copy-done | bytes 4718616
  4.5 6.7 %shard_map.64 = bf16[128,304,128]{2,1,0:T(8,128)(2,1)} custom-call(s32[256]{0:T(256)S(1)} %get-tuple-element.12.src_ref, s32[256]{0:T(256)S(1)} %get-tuple-element.11.pair_ref, bf16[36,128,512]{2,1,0:T(8,128)(2,1)S(1)} %bitcast.21), custom_call_target="tpu_custom_call" | custom-call | tf_op jit(solution)/shard_map/pallas_call | solution.py:174
  11.2 10.8 %all-to-all-start = ((bf16[128,304,128]{2,1,0:T(8,128)(2,1)}), bf16[128,304,128]{2,1,0:T(8,128)(2,1)}, u32[]{:S(2)}, u32[]{:S(2)}) async-start(bf16[128,304,128]{2,1,0:T(8,128)(2,1)} %shard_map.64), calls=%async_computation | async-start | bytes 19922944 | tf_op jit(solution)/shard_map/all_to_all | solution.py:187
  22.0 7.7 %reshape.168 = bf16[4,36,32,4,128]{4,3,2,1,0:T(4,128)(2,1)} reshape(bf16[4,36,32,512]{3,2,1,0:T(8,128)(2,1)} %bitcast.23) | data formatting | bytes 9437184 | tf_op jit(solution)/shard_map/reshape | solution.py:192
  29.7 6.1 %copy.12 = bf16[4,36,32,4,128]{4,3,1,2,0:T(4,128)(2,1)} copy(bf16[4,36,32,4,128]{4,3,2,1,0:T(4,128)(2,1)} %reshape.168) | data formatting | bytes 9437184 | tf_op jit(solution)/shard_map/reshape | solution.py:192
  35.8 101.2 %all-to-all-done.arrived_ref = bf16[128,304,128]{2,1,0:T(8,128)(2,1)} async-done(((bf16[128,304,128]{2,1,0:T(8,128)(2,1)}), bf16[128,304,128]{2,1,0:T(8,128)(2,1)}, u32[]{:S(2)}, u32[]{:S(2)}) %all-to-all-start) | async-done | bytes 9961504 | tf_op jit(solution)/shard_map/all_to_all | solution.py:187
  137.0 1.2 fusion.56
  138.2 0.1 convert_element_type.27.pair_ref
  138.4 7.1 %shard_map.65 = f32[256,2,8,128]{3,2,1,0:T(8,128)S(1)} custom-call(s32[256]{0:T(256)S(1)} %convert_element_type.27.pair_ref, bf16[128,304,128]{2,1,0:T(8,128)(2,1)} %all-to-all-done.arrived_ref, bf16[4,32,144,128]{3,2,1,0:T(8,128)(2,1)} %bitcast.22), custom_call_target="tpu_custom_call" | custom-call | tf_op jit(solution)/shard_map/pallas_call | solution.py:195
  145.5 0.2 slice_subtract_fusion
  145.7 0.4 reshape.170
  146.2 0.3 copy.13
  146.5 0.7 convolution_bitcast_fusion
  147.2 0.6 copy.14
  147.8 1.0 reshape.171
  148.9 1.4 collective-permute-start
  150.3 4.3 %collective-permute-start.1 = (f32[2,8,16,128]{3,2,1,0:T(8,128)S(1)}, f32[2,8,16,128]{3,2,1,0:T(8,128)S(1)}, u32[]{:S(2)}, u32[]{:S(2)}) collective-permute-start(f32[2,8,16,128]{3,2,1,0:T(8,128)S(1)} %reshape.171), channel_id=1, source_target_pairs={{0,64},{32,96},{64,0},{96,32},{1,65},{33,97},{65,1},{97,33},{2,66}... | collective-permute-start | bytes 393224 | tf_op jit(solution)/shard_map/ppermute | solution.py:123
  154.6 2.0 %collective-permute-start.2 = (f32[2,8,16,128]{3,2,1,0:T(8,128)S(1)}, f32[2,8,16,128]{3,2,1,0:T(8,128)S(1)}, u32[]{:S(2)}, u32[]{:S(2)}) collective-permute-start(f32[2,8,16,128]{3,2,1,0:T(8,128)S(1)} %reshape.171), channel_id=1, source_target_pairs={{0,32},{32,64},{64,96},{96,0},{1,33},{33,65},{65,97},{97,1},{2,34}... | collective-permute-start | bytes 393224 | tf_op jit(solution)/shard_map/ppermute | solution.py:123
  156.6 3.7 %collective-permute-done.1 = f32[2,8,16,128]{3,2,1,0:T(8,128)S(1)} collective-permute-done((f32[2,8,16,128]{3,2,1,0:T(8,128)S(1)}, f32[2,8,16,128]{3,2,1,0:T(8,128)S(1)}, u32[]{:S(2)}, u32[]{:S(2)}) %collective-permute-start.1) | collective-permute-done | bytes 131104 | tf_op jit(solution)/shard_map/ppermute | solution.py:123
  160.3 0.6 collective-permute-done.2
  160.9 0.1 select_add_fusion
  161.0 10.2 %collective-permute-start.3 = (f32[2,4,16,128]{3,2,1,0:T(8,128)S(1)}, f32[2,4,16,128]{3,2,1,0:T(8,128)S(1)}, u32[]{:S(2)}, u32[]{:S(2)}) collective-permute-start(f32[2,4,16,128]{3,2,1,0:T(8,128)S(1)} %get-tuple-element.7), channel_id=1, source_target_pairs={{0,1},{1,2},{2,3},{3,4},{4,5},{5,6},{6,7},{7,8},{8,9},{9,10},{10,1... | collective-permute-start | bytes 196616 | tf_op jit(solution)/shard_map/ppermute | solution.py:26
  171.2 1.9 %collective-permute-start.4 = (f32[2,4,16,128]{3,2,1,0:T(8,128)S(1)}, f32[2,4,16,128]{3,2,1,0:T(8,128)S(1)}, u32[]{:S(2)}, u32[]{:S(2)}) collective-permute-start(f32[2,4,16,128]{3,2,1,0:T(8,128)S(1)} %get-tuple-element.8), channel_id=1, source_target_pairs={{1,0},{2,1},{3,2},{4,3},{5,4},{6,5},{7,6},{8,7},{9,8},{10,9},{11,1... | collective-permute-start | bytes 196616 | tf_op jit(solution)/shard_map/ppermute | solution.py:28
  173.1 3.6 %collective-permute-done.4 = f32[2,4,16,128]{3,2,1,0:T(8,128)S(1)} collective-permute-done((f32[2,4,16,128]{3,2,1,0:T(8,128)S(1)}, f32[2,4,16,128]{3,2,1,0:T(8,128)S(1)}, u32[]{:S(2)}, u32[]{:S(2)}) %collective-permute-start.4) | collective-permute-done | bytes 65568 | tf_op jit(solution)/shard_map/ppermute | solution.py:28
  176.7 0.1 fusion.3
  176.8 0.1 fusion.28
  177.0 1.0 fusion.44
  (10 shorter events, 0.1 us)
Async XLA Ops:
  2.1 2.3 %copy-start = (bf16[128,36,512]{2,0,1:T(8,128)(2,1)S(1)}, bf16[128,36,512]{2,0,1:T(8,128)(2,1)}, u32[]{:S(2)}) copy-start(bf16[128,36,512]{2,0,1:T(8,128)(2,1)} %param.6) | copy-start | bytes 14155780
  11.2 125.8 %all-to-all-start = ((bf16[128,304,128]{2,1,0:T(8,128)(2,1)}), bf16[128,304,128]{2,1,0:T(8,128)(2,1)}, u32[]{:S(2)}, u32[]{:S(2)}) async-start(bf16[128,304,128]{2,1,0:T(8,128)(2,1)} %shard_map.64), calls=%async_computation | async-start | bytes 19922944 | tf_op jit(solution)/shard_map/all_to_all | solution.py:187
  148.9 7.7 %collective-permute-start = (f32[2,8,16,128]{3,2,1,0:T(8,128)S(1)}, f32[2,8,16,128]{3,2,1,0:T(8,128)S(1)}, u32[]{:S(2)}, u32[]{:S(2)}) collective-permute-start(f32[2,8,16,128]{3,2,1,0:T(8,128)S(1)} %reshape.171), channel_id=1, source_target_pairs={{0,96},{32,0},{64,32},{96,64},{1,97},{33,1},{65,33},{97,65},{2,98}... | collective-permute-start | bytes 393224 | tf_op jit(solution)/shard_map/ppermute | solution.py:123
  150.3 10.0 %collective-permute-start.1 = (f32[2,8,16,128]{3,2,1,0:T(8,128)S(1)}, f32[2,8,16,128]{3,2,1,0:T(8,128)S(1)}, u32[]{:S(2)}, u32[]{:S(2)}) collective-permute-start(f32[2,8,16,128]{3,2,1,0:T(8,128)S(1)} %reshape.171), channel_id=1, source_target_pairs={{0,64},{32,96},{64,0},{96,32},{1,65},{33,97},{65,1},{97,33},{2,66}... | collective-permute-start | bytes 393224 | tf_op jit(solution)/shard_map/ppermute | solution.py:123
  154.6 6.3 %collective-permute-start.2 = (f32[2,8,16,128]{3,2,1,0:T(8,128)S(1)}, f32[2,8,16,128]{3,2,1,0:T(8,128)S(1)}, u32[]{:S(2)}, u32[]{:S(2)}) collective-permute-start(f32[2,8,16,128]{3,2,1,0:T(8,128)S(1)} %reshape.171), channel_id=1, source_target_pairs={{0,32},{32,64},{64,96},{96,0},{1,33},{33,65},{65,97},{97,1},{2,34}... | collective-permute-start | bytes 393224 | tf_op jit(solution)/shard_map/ppermute | solution.py:123
  161.0 12.1 %collective-permute-start.3 = (f32[2,4,16,128]{3,2,1,0:T(8,128)S(1)}, f32[2,4,16,128]{3,2,1,0:T(8,128)S(1)}, u32[]{:S(2)}, u32[]{:S(2)}) collective-permute-start(f32[2,4,16,128]{3,2,1,0:T(8,128)S(1)} %get-tuple-element.7), channel_id=1, source_target_pairs={{0,1},{1,2},{2,3},{3,4},{4,5},{5,6},{6,7},{7,8},{8,9},{9,10},{10,1... | collective-permute-start | bytes 196616 | tf_op jit(solution)/shard_map/ppermute | solution.py:26
  171.2 5.6 %collective-permute-start.4 = (f32[2,4,16,128]{3,2,1,0:T(8,128)S(1)}, f32[2,4,16,128]{3,2,1,0:T(8,128)S(1)}, u32[]{:S(2)}, u32[]{:S(2)}) collective-permute-start(f32[2,4,16,128]{3,2,1,0:T(8,128)S(1)} %get-tuple-element.8), channel_id=1, source_target_pairs={{1,0},{2,1},{3,2},{4,3},{5,4},{6,5},{7,6},{8,7},{9,8},{10,9},{11,1... | collective-permute-start | bytes 196616 | tf_op jit(solution)/shard_map/ppermute | solution.py:28
